TPU v7x, 512 devices: a whole 4x4x16 slice. The times are simulated.
512 devices in a mesh: space: 16 (over x_hi, y, core), seq: 32 (over x_lo, z).
Axes of the slice: x: 4 (x_hi: 2, x_lo: 2; x = x_hi * 2 + x_lo), y: 4, z: 16, core: 2. Of those that a mesh axis runs over, the one named last changes fastest.
Arguments:
- query_feats: bfloat16 [65536, 2048], P(('space', 'seq')), may hold values from -9 to 9
- key_feats: bfloat16 [65536, 2048], P(('space', 'seq')), may hold values from -6 to 6
- value_feats: bfloat16 [65536, 2048], P(('space', 'seq')), may hold values from -6 to 6
- grad_output: bfloat16 [65536, 2048], P(('space', 'seq')), may hold values from -6 to 6
- lengths: int32 [16, 96], replicated, may hold values from 1 to 64, as said below
- members: int32 [1536, 64], P('space'), may hold values from 0 to 4095, as said below
- neighbours: int32 [1536, 5], P('space'), may hold values from 0 to 127, as said below
Outputs:
- attended: bfloat16 [65536, 2048], P(('space', 'seq'))
- grad_queries: bfloat16 [65536, 2048], P(('space', 'seq'))
- grad_keys: bfloat16 [65536, 2048], P(('space', 'seq'))
- grad_values: bfloat16 [65536, 2048], P(('space', 'seq'))
Inputs may be any that keep to these rules, and one draw needn't show every extreme that they name: Row g holds the lengths of group g's 96 windows; they sum to 4096, and in every group some window has all 64 slots live. `members`: over a group's windows the live slots (t below the window's length) name each of the group's 4096 voxels exactly once; the other slots name some voxel of the group. `neighbours`: entries index the extended windows of the row's group: below 16 the last 16 windows of the group before, from 16 to 111 its own windows, above that the first 16 windows of the group after. An entry never names the window itself and lies within 16 extended windows of it; group 0 names no window before it and the last group none after it.
All inputs are finite; a program needn't handle non-finite values.
Results may differ from a plain program's by a relative error of at most 0.013.
The roundings to bfloat16 on the way count: a program that leaves them out, or rounds other values in their place, can miss the bound.
Values may be sent and summed in bfloat16 or wider, within the bound.
No kernel may reach another device: no remote copies, remote signals or barrier semaphores. Data moves between devices by JAX's collectives and lax.ppermute only.
A program may use at most 64 MiB of HBM per device.

v0:
```python
import jax
import jax.numpy as jnp
from jax import lax
from jax.sharding import PartitionSpec as P

HEAD = 64
WIN = 64


MASKED_SCORE = -1e30


def padded(value, sides, width):
    for axis, dim in sides:
        count, length = (lax.axis_size(axis), value.shape[dim])
        up = [(i, (i + 1) % count) for i in range(count - 1)]
        down = [(j, i) for i, j in up]
        last = lax.slice_in_dim(value, length - width, length, axis=dim)
        first = lax.slice_in_dim(value, 0, width, axis=dim)
        before = lax.ppermute(last, axis, up)
        after = lax.ppermute(first, axis, down)
        value = jnp.concatenate([before, value, after], axis=dim)
    return value


def gather_rows(source, indices):
    return jnp.take(source, indices, axis=0)


def to_windows(query_part, key_part, value_part, members):
    query_win = gather_rows(query_part, members)
    kv_win = gather_rows(jnp.concatenate([key_part, value_part], axis=1), members)
    return (query_win, kv_win)


def border_rows(source, border):
    return jnp.concatenate([source[:border], source[source.shape[0] - border :]], axis=0)


def extend_windows(kv_win, received, border):
    return jnp.concatenate([received[:border], kv_win, received[3 * border :]], axis=0)


def window_keys(block_id, per_block, border, neighbours):
    start_row = block_id * per_block
    own_rows = border + start_row + jnp.arange(per_block, dtype=jnp.int32)
    near_rows = lax.dynamic_slice_in_dim(neighbours, start_row, per_block, 0)
    return jnp.concatenate([own_rows[:, None], near_rows], axis=1)


def block_attention(query_blk, key_index, kv_ext, length_ext, head_count):
    block_n = query_blk.shape[0]
    col_width = query_blk.shape[-1]
    head_size = col_width // head_count
    key_rows = gather_rows(kv_ext, key_index).reshape(block_n, -1, 2 * col_width)
    key_length = gather_rows(length_ext, key_index)
    key_alive = (jnp.arange(WIN, dtype=jnp.int32)[None, None, :] < key_length[:, :, None]).reshape(
        block_n, -1
    )
    query_heads = query_blk.reshape(block_n, WIN, head_count, head_size)
    key_heads = key_rows[:, :, :col_width].reshape(block_n, -1, head_count, head_size)
    value_heads = key_rows[:, :, col_width:].reshape(block_n, -1, head_count, head_size)
    score_scale = head_size ** (-0.5)
    scores = (
        jnp.einsum("wqhd,wkhd->whqk", query_heads, key_heads, preferred_element_type=jnp.float32)
        * score_scale
    )
    scores = jnp.where(key_alive[:, None, None, :], scores, MASKED_SCORE)
    row_max = jnp.max(scores, axis=-1, keepdims=True)
    exp_scores = jnp.exp(scores - row_max)
    attn_probs = exp_scores / jnp.sum(exp_scores, axis=-1, keepdims=True)
    return (attn_probs, query_heads, key_heads, value_heads, score_scale)


def shards(query_feats, key_feats, value_feats, grad_output, lengths, members, neighbours):
    group_idx = lax.axis_index("space")
    groups = lax.axis_size("space")
    windows_n = members.shape[0]
    border = windows_n // 6
    per_block = 8
    block_count = windows_n // per_block
    col_width = query_feats.shape[1] // lax.axis_size("seq")
    head_count = col_width // HEAD
    own_length = lax.dynamic_index_in_dim(lengths, group_idx, 0, keepdims=False)
    before_length = lax.dynamic_index_in_dim(
        lengths, jnp.maximum(group_idx - 1, 0), 0, keepdims=False
    )
    after_length = lax.dynamic_index_in_dim(
        lengths, jnp.minimum(group_idx + 1, groups - 1), 0, keepdims=False
    )
    length_ext = jnp.concatenate(
        [
            jnp.where(group_idx > 0, before_length[windows_n - border :], 0),
            own_length,
            jnp.where(group_idx < groups - 1, after_length[:border], 0),
        ]
    )
    slot_alive = jnp.arange(WIN, dtype=jnp.int32)[None, :] < own_length[:, None]
    query_heads, key_heads, value_heads = (
        lax.all_to_all(query_feats, "seq", split_axis=1, concat_axis=0, tiled=True),
        lax.all_to_all(key_feats, "seq", split_axis=1, concat_axis=0, tiled=True),
        lax.all_to_all(value_feats, "seq", split_axis=1, concat_axis=0, tiled=True),
    )
    voxel_count = query_heads.shape[0]
    flat_slots = jnp.where(slot_alive, members, voxel_count).reshape(-1)
    slot_of = (
        jnp.zeros((voxel_count,), jnp.int32)
        .at[flat_slots]
        .set(jnp.arange(windows_n * WIN, dtype=jnp.int32), mode="drop")
    )

    def to_voxels(slot_vals):
        return gather_rows(slot_vals.reshape(windows_n * WIN, -1), slot_of)

    query_win, kv_win = to_windows(query_heads, key_heads, value_heads, members)
    received = padded(border_rows(kv_win, border), (("space", 0),), border)
    kv_ext = extend_windows(kv_win, received, border)

    def forward_block(block_id):
        key_index = window_keys(block_id, per_block, border, neighbours)
        query_blk = lax.dynamic_slice_in_dim(query_win, block_id * per_block, per_block, 0)
        attn_probs, query_h, key_h, value_h, score_scale = block_attention(
            query_blk, key_index, kv_ext, length_ext, head_count
        )
        slot_out = jnp.einsum(
            "whqk,wkhd->wqhd",
            attn_probs.astype(jnp.bfloat16),
            value_h,
            preferred_element_type=jnp.float32,
        )
        return slot_out.astype(jnp.bfloat16).reshape(per_block, WIN, col_width)

    out_slots = lax.map(forward_block, jnp.arange(block_count, dtype=jnp.int32)).reshape(
        windows_n, WIN, col_width
    )
    attended = lax.all_to_all(to_voxels(out_slots), "seq", split_axis=0, concat_axis=1, tiled=True)
    grad_heads = lax.all_to_all(grad_output, "seq", split_axis=1, concat_axis=0, tiled=True)
    grad_win = gather_rows(grad_heads, members) * slot_alive[:, :, None].astype(jnp.bfloat16)
    query_back, kv_back = (query_win, kv_ext)

    def backward_block(grad_ext, block_id):
        key_index = window_keys(block_id, per_block, border, neighbours)
        start_row = block_id * per_block
        query_blk = lax.dynamic_slice_in_dim(query_back, start_row, per_block, 0)
        attn_probs, query_h, key_h, value_h, score_scale = block_attention(
            query_blk, key_index, kv_back, length_ext, head_count
        )
        grad_h = lax.dynamic_slice_in_dim(grad_win, start_row, per_block, 0).reshape(
            per_block, WIN, head_count, -1
        )
        out_h = lax.dynamic_slice_in_dim(out_slots, start_row, per_block, 0).reshape(
            per_block, WIN, head_count, -1
        )
        row_delta = jnp.transpose(
            jnp.sum(grad_h.astype(jnp.float32) * out_h.astype(jnp.float32), axis=-1), (0, 2, 1)
        )
        grad_probs = jnp.einsum(
            "wqhd,wkhd->whqk", grad_h, value_h, preferred_element_type=jnp.float32
        )
        grad_scores = (attn_probs * (grad_probs - row_delta[..., None]) * score_scale).astype(
            jnp.bfloat16
        )
        grad_query = jnp.einsum(
            "whqk,wkhd->wqhd", grad_scores, key_h, preferred_element_type=jnp.float32
        )
        grad_key = jnp.einsum(
            "whqk,wqhd->wkhd", grad_scores, query_h, preferred_element_type=jnp.float32
        )
        grad_value = jnp.einsum(
            "whqk,wqhd->wkhd",
            attn_probs.astype(jnp.bfloat16),
            grad_h,
            preferred_element_type=jnp.float32,
        )
        key_count = key_index.shape[1]
        key_terms = jnp.concatenate(
            [
                grad_key.reshape(per_block, key_count, WIN, col_width),
                grad_value.reshape(per_block, key_count, WIN, col_width),
            ],
            axis=-1,
        )
        return (
            grad_ext.at[key_index].add(key_terms),
            grad_query.astype(jnp.bfloat16).reshape(per_block, WIN, col_width),
        )

    grad_start = jnp.zeros((windows_n + 2 * border, WIN, 2 * col_width), jnp.float32)
    grad_ext, grad_query_blocks = lax.scan(
        backward_block, grad_start, jnp.arange(block_count, dtype=jnp.int32)
    )
    received_grads = padded(
        border_rows(grad_ext, border).astype(jnp.bfloat16), (("space", 0),), border
    ).astype(jnp.float32)
    own_grads = grad_ext[border : border + windows_n]
    own_grads = own_grads.at[:border].add(received_grads[:border])
    own_grads = own_grads.at[windows_n - border :].add(received_grads[3 * border :])
    kv_grads = to_voxels(own_grads.astype(jnp.bfloat16))
    grad_q_vox = to_voxels(grad_query_blocks.reshape(windows_n, WIN, col_width))
    grad_queries, grad_keys, grad_values = (
        lax.all_to_all(grad_q_vox, "seq", split_axis=0, concat_axis=1, tiled=True),
        lax.all_to_all(kv_grads[:, :col_width], "seq", split_axis=0, concat_axis=1, tiled=True),
        lax.all_to_all(kv_grads[:, col_width:], "seq", split_axis=0, concat_axis=1, tiled=True),
    )
    return (attended, grad_queries, grad_keys, grad_values)


def solution(mesh):
    in_specs = (
        P(("space", "seq"), None),
        P(("space", "seq"), None),
        P(("space", "seq"), None),
        P(("space", "seq"), None),
        P(),
        P("space", None),
        P("space", None),
    )
    out_specs = (
        P(("space", "seq"), None),
        P(("space", "seq"), None),
        P(("space", "seq"), None),
        P(("space", "seq"), None),
    )
    return jax.shard_map(shards, mesh=mesh, in_specs=in_specs, out_specs=out_specs, check_vma=False)
```

profile of v0, /device:TPU:48, one launch (start us, length us, event | category | flops | bytes accessed | tf_op | source)
XLA Modules:
  0.0 857.8 jit_solution(11383126140608523299)
XLA Ops:
  2.7 16.4 %all-to-all-start.2 = ((bf16[128,32,64]{0,2,1:T(8,128)(2,1)}), bf16[128,32,64]{0,2,1:T(8,128)(2,1)S(1)}, u32[]{:S(2)}, u32[]{:S(2)}) async-start(bf16[128,32,64]{0,2,1:T(8,128)(2,1)} %bitcast.32), calls=%async_computation.2 | async-start | bytes 1048576 | tf_op jit(solution)/shard_map/all_to_all | solution.py:100
  20.2 31.2 %all-to-all-done.2 = bf16[128,32,64]{0,2,1:T(8,128)(2,1)S(1)} async-done(((bf16[128,32,64]{0,2,1:T(8,128)(2,1)}), bf16[128,32,64]{0,2,1:T(8,128)(2,1)S(1)}, u32[]{:S(2)}, u32[]{:S(2)}) %all-to-all-start.2) | async-done | bytes 524320 | tf_op jit(solution)/shard_map/all_to_all | solution.py:100
  56.7 31.3 %all-to-all-done = bf16[128,32,64]{0,2,1:T(8,128)(2,1)S(1)} async-done(((bf16[128,32,64]{0,2,1:T(8,128)(2,1)}), bf16[128,32,64]{0,2,1:T(8,128)(2,1)S(1)}, u32[]{:S(2)}, u32[]{:S(2)}) %all-to-all-start) | async-done | bytes 524320 | tf_op jit(solution)/shard_map/all_to_all | solution.py:101
  94.4 30.3 %all-to-all-done.1 = bf16[128,32,64]{0,2,1:T(8,128)(2,1)S(1)} async-done(((bf16[128,32,64]{0,2,1:T(8,128)(2,1)}), bf16[128,32,64]{0,2,1:T(8,128)(2,1)S(1)}, u32[]{:S(2)}, u32[]{:S(2)}) %all-to-all-start.1) | async-done | bytes 524320 | tf_op jit(solution)/shard_map/all_to_all | solution.py:102
  124.7 4.4 all-to-all-start.4
  129.7 23.0 %scatter_custom_fusion.1 = s32[4096]{0:T(1024)S(1)} fusion(s32[6144]{0:T(1024)S(1)} %bitcast.156, s32[6144]{0:T(1024)S(1)} %iota.34, s32[]{:T(128)} %constant.188.clone.1), kind=kCustom, calls=%fused_computation.100 | custom fusion | bytes 16388 | tf_op jit(solution)/shard_map/scatter | solution.py:109
  155.5 22.1 %gather_fusion.6 = bf16[6144,64]{1,0:T(8,128)(2,1)} fusion(bf16[4096,64]{1,0:T(8,128)(2,1)S(1)} %bitcast.126, s32[6144]{0:T(1024)S(1)} %broadcast_clamp_fusion), kind=kCustom, calls=%fused_computation.clone | custom fusion | bytes 1597440 | tf_op jit(solution)/shard_map/jit(_take)/gather | solution.py:27
  178.2 18.1 %gather_fusion.4 = bf16[6144,128]{1,0:T(8,128)(2,1)S(1)} fusion(bf16[4096,128]{1,0:T(8,128)(2,1)S(1)} %pad_maximum_fusion.2, s32[6144]{0:T(1024)S(1)} %broadcast_clamp_fusion), kind=kCustom, calls=%fused_computation.8 | custom fusion | bytes 3170304 | tf_op jit(solution)/shard_map/jit(_take)/gather | solution.py:27
  197.9 22.1 %gather_fusion.8 = bf16[6144,64]{1,0:T(8,128)(2,1)} fusion(bf16[4096,64]{1,0:T(8,128)(2,1)S(1)} %bitcast.127, s32[6144]{0:T(1024)S(1)} %broadcast_clamp_fusion), kind=kCustom, calls=%fused_computation.4.clone | custom fusion | bytes 1597440 | tf_op jit(solution)/shard_map/jit(_take)/gather | solution.py:27
  232.7 102.9 %while.24 = (s32[]{:T(128)}, bf16[12,8,64,64]{3,2,1,0:T(8,128)(2,1)S(1)}, s32[12]{0:T(128)S(1)}, s32[96,5]{1,0:T(8,128)S(1)}, bf16[128,64,128]{2,1,0:T(8,128)(2,...) while((s32[]{:T(128)}, ...), condition=%wide.region_3.7_spmd, body=%wide.region_0.6_spmd.sunk | while | flops 52139852 | bytes 8529363 | solution.py:133
  339.6 330.8 %while.25 = (s32[]{:T(128)}, f32[128,64,128]{2,1,0:T(8,128)}, bf16[12,8,64,64]{3,2,1,0:T(8,128)(2,1)}, s32[12]{0:T(128)S(1)}, s32[96,5]{1,0:T(8,128)S(1)}, /*ind...) while((s32[]{:T(128)}, f32[128,64,128]{2,1,0:T(8,128)}, ...), condition=%wide.region_10.15_spmd, body=%wide.region_5.0_spmd.sunk | while | flops 129537552 | bytes 31408988 | solution.py:189
  359.3 7.9 scatter_fusion
  386.9 7.9 scatter_fusion
  414.4 7.9 scatter_fusion
  442.0 7.9 scatter_fusion
  469.6 7.9 scatter_fusion
  497.1 7.9 scatter_fusion
  524.7 7.9 scatter_fusion
  552.3 7.9 scatter_fusion
  579.8 7.9 scatter_fusion
  607.4 7.9 scatter_fusion
  635.0 7.9 scatter_fusion
  662.6 7.9 scatter_fusion
  670.4 12.1 %gather_fusion.7 = bf16[4096,64]{1,0:T(8,128)(2,1)S(1)} fusion(bf16[6144,64]{1,0:T(8,128)(2,1)S(1)} %bitcast.139, s32[4096]{0:T(1024)S(1)} %fusion.37), kind=kCustom, calls=%fused_computation.3.clone | custom fusion | bytes 1064960 | tf_op jit(solution)/shard_map/jit(_take)/gather | solution.py:27
  682.6 12.6 %gather_fusion.9 = bf16[4096,64]{1,0:T(8,128)(2,1)S(1)} fusion(bf16[6144,64]{1,0:T(8,128)(2,1)} %bitcast.45, s32[4096]{0:T(1024)S(1)} %fusion.37), kind=kCustom, calls=%fused_computation.7.clone | custom fusion | bytes 1064960 | tf_op jit(solution)/shard_map/jit(_take)/gather | solution.py:27
  700.8 12.9 %all-to-all-start.3 = ((bf16[32,128,64]{1,2,0:T(8,128)(2,1)}), bf16[32,128,64]{1,2,0:T(8,128)(2,1)S(1)}, u32[]{:S(2)}, u32[]{:S(2)}) async-start(bf16[32,128,64]{1,2,0:T(8,128)(2,1)} %copy.129), calls=%async_computation.3 | async-start | bytes 1048576 | tf_op jit(solution)/shard_map/all_to_all | solution.py:136
  728.1 18.9 %all-to-all-done.3 = bf16[32,128,64]{1,2,0:T(8,128)(2,1)S(1)} async-done(((bf16[32,128,64]{1,2,0:T(8,128)(2,1)}), bf16[32,128,64]{1,2,0:T(8,128)(2,1)S(1)}, u32[]{:S(2)}, u32[]{:S(2)}) %all-to-all-start.3) | async-done | bytes 524320 | tf_op jit(solution)/shard_map/all_to_all | solution.py:136
  747.0 4.6 all-to-all-start.5
  755.8 12.1 %gather_fusion.5 = bf16[4096,128]{1,0:T(8,128)(2,1)S(1)} fusion(bf16[6144,128]{1,0:T(8,128)(2,1)S(1)} %bitcast.140, s32[4096]{0:T(1024)S(1)} %fusion.37), kind=kCustom, calls=%fused_computation.9 | custom fusion | bytes 2113536 | tf_op jit(solution)/shard_map/jit(_take)/gather | solution.py:27
  771.6 12.6 %all-to-all-done.5 = bf16[32,128,64]{1,2,0:T(8,128)(2,1)} async-done(((bf16[32,128,64]{1,2,0:T(8,128)(2,1)}), bf16[32,128,64]{1,2,0:T(8,128)(2,1)}, u32[]{:S(2)}, u32[]{:S(2)}) %all-to-all-start.5) | async-done | bytes 524320 | tf_op jit(solution)/shard_map/all_to_all | solution.py:201
  789.4 31.0 %all-to-all-done.6 = bf16[32,128,64]{1,2,0:T(8,128)(2,1)S(1)} async-done(((bf16[32,128,64]{1,2,0:T(8,128)(2,1)}), bf16[32,128,64]{1,2,0:T(8,128)(2,1)S(1)}, u32[]{:S(2)}, u32[]{:S(2)}) %all-to-all-start.6) | async-done | bytes 524320 | tf_op jit(solution)/shard_map/all_to_all | solution.py:202
  828.5 28.3 %all-to-all-done.7 = bf16[32,128,64]{1,2,0:T(8,128)(2,1)S(1)} async-done(((bf16[32,128,64]{1,2,0:T(8,128)(2,1)}), bf16[32,128,64]{1,2,0:T(8,128)(2,1)S(1)}, u32[]{:S(2)}, u32[]{:S(2)}) %all-to-all-start.7) | async-done | bytes 524320 | tf_op jit(solution)/shard_map/all_to_all | solution.py:203
  (770 shorter events, 399.8 us)
Async XLA Ops:
  0.6 18.5 %copy-start.7 = (bf16[128,2048]{1,0:T(8,128)(2,1)S(1)}, bf16[128,2048]{1,0:T(8,128)(2,1)}, u32[]{:S(2)}) copy-start(bf16[128,2048]{1,0:T(8,128)(2,1)} %param.24) | copy-start | bytes 1572868
  2.7 53.0 %copy-start.8 = (bf16[128,2048]{1,0:T(8,128)(2,1)S(1)}, bf16[128,2048]{1,0:T(8,128)(2,1)}, u32[]{:S(2)}) copy-start(bf16[128,2048]{1,0:T(8,128)(2,1)} %param.25) | copy-start | bytes 1572868
  2.7 48.7 %all-to-all-start.2 = ((bf16[128,32,64]{0,2,1:T(8,128)(2,1)}), bf16[128,32,64]{0,2,1:T(8,128)(2,1)S(1)}, u32[]{:S(2)}, u32[]{:S(2)}) async-start(bf16[128,32,64]{0,2,1:T(8,128)(2,1)} %bitcast.32), calls=%async_computation.2 | async-start | bytes 1048576 | tf_op jit(solution)/shard_map/all_to_all | solution.py:100
  51.4 41.8 %copy-start.10 = (s32[96,64]{0,1:T(8,128)S(1)}, s32[96,64]{0,1:T(8,128)}, u32[]{:S(2)}) copy-start(s32[96,64]{0,1:T(8,128)} %param.28) | copy-start | bytes 73732
  51.4 42.0 %copy-start.9 = (bf16[128,2048]{1,0:T(8,128)(2,1)S(1)}, bf16[128,2048]{1,0:T(8,128)(2,1)}, u32[]{:S(2)}) copy-start(bf16[128,2048]{1,0:T(8,128)(2,1)} %param.26) | copy-start | bytes 1572868
  51.4 36.7 %all-to-all-start = ((bf16[128,32,64]{0,2,1:T(8,128)(2,1)}), bf16[128,32,64]{0,2,1:T(8,128)(2,1)S(1)}, u32[]{:S(2)}, u32[]{:S(2)}) async-start(bf16[128,32,64]{0,2,1:T(8,128)(2,1)} %bitcast.23), calls=%async_computation | async-start | bytes 1048576 | tf_op jit(solution)/shard_map/all_to_all | solution.py:101
  88.1 41.4 %copy-start.11 = (s32[96,5]{0,1:T(8,128)S(1)}, s32[96,5]{0,1:T(8,128)}, u32[]{:S(2)}) copy-start(s32[96,5]{0,1:T(8,128)} %param.29) | copy-start | bytes 5764
  88.1 36.6 %all-to-all-start.1 = ((bf16[128,32,64]{0,2,1:T(8,128)(2,1)}), bf16[128,32,64]{0,2,1:T(8,128)(2,1)S(1)}, u32[]{:S(2)}, u32[]{:S(2)}) async-start(bf16[128,32,64]{0,2,1:T(8,128)(2,1)} %bitcast.26), calls=%async_computation.1 | async-start | bytes 1048576 | tf_op jit(solution)/shard_map/all_to_all | solution.py:102
  124.7 28.7 %copy-start.6 = (bf16[128,32,64]{0,2,1:T(8,128)(2,1)}, bf16[128,32,64]{0,2,1:T(8,128)(2,1)S(1)}, u32[]{:S(2)}) copy-start(bf16[128,32,64]{0,2,1:T(8,128)(2,1)S(1)} %all-to-all-done.1) | copy-start | bytes 1572868
  124.7 71.6 %all-to-all-start.4 = ((bf16[128,32,64]{0,2,1:T(8,128)(2,1)}), bf16[128,32,64]{0,2,1:T(8,128)(2,1)}, u32[]{:S(2)}, u32[]{:S(2)}) async-start(bf16[128,32,64]{0,2,1:T(8,128)(2,1)} %bitcast.40), calls=%async_computation.4 | async-start | bytes 1048576 | tf_op jit(solution)/shard_map/all_to_all | solution.py:137
  219.9 6.9 copy-start.4
  221.1 9.6 %collective-permute-start = (bf16[16,64,128]{2,1,0:T(8,128)(2,1)S(1)}, bf16[16,64,128]{2,1,0:T(8,128)(2,1)S(1)}, u32[]{:S(2)}, u32[]{:S(2)}) collective-permute-start(bf16[16,64,128]{2,1,0:T(8,128)(2,1)S(1)} %get-tuple-element.247), channel_id=1, source_target_pairs={{0,32},{32,64},{64,96},{96,128},{128,160},{160,192},{192,224},{224... | collective-permute-start | bytes 786440 | tf_op jit(solution)/shard_map/ppermute | solution.py:20
  223.0 7.6 collective-permute-start.1
  359.3 7.9 copy-start.2
  386.9 7.9 copy-start.2
  414.4 7.9 copy-start.2
  442.0 7.9 copy-start.2
  469.6 7.9 copy-start.2
  497.1 7.9 copy-start.2
  524.7 7.9 copy-start.2
  552.3 7.9 copy-start.2
  579.8 7.9 copy-start.2
  607.4 7.9 copy-start.2
  635.0 7.9 copy-start.2
  662.6 7.9 copy-start.2
  700.8 46.2 %all-to-all-start.3 = ((bf16[32,128,64]{1,2,0:T(8,128)(2,1)}), bf16[32,128,64]{1,2,0:T(8,128)(2,1)S(1)}, u32[]{:S(2)}, u32[]{:S(2)}) async-start(bf16[32,128,64]{1,2,0:T(8,128)(2,1)} %copy.129), calls=%async_computation.3 | async-start | bytes 1048576 | tf_op jit(solution)/shard_map/all_to_all | solution.py:136
  713.7 8.6 %copy-start = (f32[128,64,128]{2,1,0:T(8,128)S(1)}, f32[128,64,128]{2,1,0:T(8,128)}, u32[]{:S(2)}) copy-start(f32[128,64,128]{2,1,0:T(8,128)} %get-tuple-element.124) | copy-start | bytes 12582916
  716.6 8.8 %collective-permute-start.2 = (bf16[16,64,128]{2,1,0:T(8,128)(2,1)S(1)}, bf16[16,64,128]{2,1,0:T(8,128)(2,1)S(1)}, u32[]{:S(2)}, u32[]{:S(2)}) collective-permute-start(bf16[16,64,128]{2,1,0:T(8,128)(2,1)S(1)} %get-tuple-element.245), channel_id=1, source_target_pairs={{0,32},{32,64},{64,96},{96,128},{128,160},{160,192},{192,224},{224... | collective-permute-start | bytes 786440 | tf_op jit(solution)/shard_map/ppermute | solution.py:20
  719.5 6.8 collective-permute-start.3
  747.0 37.1 %all-to-all-start.5 = ((bf16[32,128,64]{1,2,0:T(8,128)(2,1)}), bf16[32,128,64]{1,2,0:T(8,128)(2,1)}, u32[]{:S(2)}, u32[]{:S(2)}) async-start(bf16[32,128,64]{1,2,0:T(8,128)(2,1)} %copy.138), calls=%async_computation.5 | async-start | bytes 1048576 | tf_op jit(solution)/shard_map/all_to_all | solution.py:201
  784.2 36.2 %all-to-all-start.6 = ((bf16[32,128,64]{1,2,0:T(8,128)(2,1)}), bf16[32,128,64]{1,2,0:T(8,128)(2,1)S(1)}, u32[]{:S(2)}, u32[]{:S(2)}) async-start(bf16[32,128,64]{1,2,0:T(8,128)(2,1)} %copy.139), calls=%async_computation.6 | async-start | bytes 1048576 | tf_op jit(solution)/shard_map/all_to_all | solution.py:202
  820.4 36.4 %all-to-all-start.7 = ((bf16[32,128,64]{1,2,0:T(8,128)(2,1)}), bf16[32,128,64]{1,2,0:T(8,128)(2,1)S(1)}, u32[]{:S(2)}, u32[]{:S(2)}) async-start(bf16[32,128,64]{1,2,0:T(8,128)(2,1)} %copy.140), calls=%async_computation.7 | async-start | bytes 1048576 | tf_op jit(solution)/shard_map/all_to_all | solution.py:203
  (14 other events, 41.6 us)
where the time goes:
time: 863 us; the launch traced here: 858 us
  local copies, waits for them, and re-layouts  286 us (33%)
  waiting for transfers between devices  185 us (21%)
  other arithmetic  178 us (21%)
  matrix products  124 us (14%)
  starting transfers between devices  66.5 us (8%)
  loops' own time  18.2 us (2%)
    gather x78, local copies, waits for them, and re-layouts, gather_rows(): return jnp.take(source, indices, axis=0)  175 us
    scatter-add x12, other arithmetic, backward_block(): grad_ext.at[key_index].add(key_terms)  94.7 us
    dot_general x12, matrix products, backward_block(): jnp.einsum('whqk,wqhd->wkhd', attn_probs.astype(jnp.bfloat16), grad_h, pr...  34.3 us
    dot_general x24, matrix products, block_attention(): jnp.einsum('wqhd,wkhd->whqk', query_heads, key_heads, preferred_element_t...  33 us
    all_to_all x1, waiting for transfers between devices, shards(): lax.all_to_all(key_feats, 'seq', split_axis=1, concat_axis=0, tiled=True)  31.3 us
    all_to_all x1, waiting for transfers between devices, shards(): lax.all_to_all(query_feats, 'seq', split_axis=1, concat_axis=0, tiled=True)  31.2 us
    all_to_all x1, waiting for transfers between devices, shards(): lax.all_to_all(kv_grads[:, :col_width], 'seq', split_axis=0, concat_axis=...  31 us
    all_to_all x1, waiting for transfers between devices, shards(): lax.all_to_all(value_feats, 'seq', split_axis=1, concat_axis=0, tiled=True)  30.3 us
  transfers between devices with their start and end apart: 12, of which 8 were waited for; matrix products, arithmetic and copies ran while one was open for 13% of the time, Pallas kernels for 0%

commit v1 on v0

--- a/solution.py
+++ b/solution.py
@@ -1,6 +1,8 @@
 import jax
 import jax.numpy as jnp
 from jax import lax
+from jax.experimental import pallas as pl
+from jax.experimental.pallas import tpu as pltpu
 from jax.sharding import PartitionSpec as P
 
 HEAD = 64
@@ -70,6 +72,75 @@
     exp_scores = jnp.exp(scores - row_max)
     attn_probs = exp_scores / jnp.sum(exp_scores, axis=-1, keepdims=True)
     return (attn_probs, query_heads, key_heads, value_heads, score_scale)
+
+
+def attention_kernel(idx_ref, len_ref, q_ref, k_ref, v_ref, g_ref, out_ref, dq_ref, dk_ref, dv_ref):
+    windows_n = q_ref.shape[0]
+    nb = idx_ref.shape[0] // windows_n
+    keys = nb * WIN
+    scale = HEAD ** (-0.5)
+    dk_ref[...] = jnp.zeros(dk_ref.shape, dk_ref.dtype)
+    dv_ref[...] = jnp.zeros(dv_ref.shape, dv_ref.dtype)
+    col = lax.broadcasted_iota(jnp.int32, (1, keys), 1)
+    col_block = col // WIN
+    col_slot = col % WIN
+
+    def body(w, carry):
+        ids = [idx_ref[w * nb + j] for j in range(nb)]
+        q = q_ref[w]
+        g = g_ref[w]
+        k_all = jnp.concatenate([k_ref[i] for i in ids], axis=0)
+        v_all = jnp.concatenate([v_ref[i] for i in ids], axis=0)
+        limit = jnp.zeros((1, keys), jnp.int32)
+        for j in range(nb):
+            limit = jnp.where(col_block == j, len_ref[ids[j]], limit)
+        alive = col_slot < limit
+        nt = (((1,), (1,)), ((), ()))
+        tn = (((0,), (0,)), ((), ()))
+        scores = lax.dot_general(q, k_all, nt, preferred_element_type=jnp.float32) * scale
+        scores = jnp.where(alive, scores, MASKED_SCORE)
+        row_max = jnp.max(scores, axis=-1, keepdims=True)
+        exp_scores = jnp.exp(scores - row_max)
+        probs = exp_scores / jnp.sum(exp_scores, axis=-1, keepdims=True)
+        weights = probs.astype(jnp.bfloat16)
+        slot_out = jnp.dot(weights, v_all, preferred_element_type=jnp.float32).astype(jnp.bfloat16)
+        out_ref[w] = slot_out
+        delta = jnp.sum(g.astype(jnp.float32) * slot_out.astype(jnp.float32), axis=-1, keepdims=True)
+        grad_probs = lax.dot_general(g, v_all, nt, preferred_element_type=jnp.float32)
+        grad_scores = (probs * (grad_probs - delta) * scale).astype(jnp.bfloat16)
+        dq_ref[w] = jnp.dot(grad_scores, k_all, preferred_element_type=jnp.float32).astype(jnp.bfloat16)
+        grad_k = lax.dot_general(grad_scores, q, tn, preferred_element_type=jnp.float32)
+        grad_v = lax.dot_general(weights, g, tn, preferred_element_type=jnp.float32)
+        for j in range(nb):
+            dk_ref[ids[j]] += grad_k[j * WIN : (j + 1) * WIN]
+            dv_ref[ids[j]] += grad_v[j * WIN : (j + 1) * WIN]
+        return carry
+
+    lax.fori_loop(0, windows_n, body, 0)
+
+
+def window_attention(key_index, length_ext, query_win, k_ext, v_ext, grad_win):
+    windows_n, _, width = query_win.shape
+    ext_n = k_ext.shape[0]
+    keys = (key_index.shape[0] // windows_n) * WIN
+    flops = 2 * windows_n * WIN * keys * width * 7
+    vmem = pl.BlockSpec(memory_space=pltpu.VMEM)
+    smem = pl.BlockSpec(memory_space=pltpu.SMEM)
+    return pl.pallas_call(
+        attention_kernel,
+        out_shape=(
+            jax.ShapeDtypeStruct(query_win.shape, jnp.bfloat16),
+            jax.ShapeDtypeStruct(query_win.shape, jnp.bfloat16),
+            jax.ShapeDtypeStruct((ext_n, WIN, width), jnp.float32),
+            jax.ShapeDtypeStruct((ext_n, WIN, width), jnp.float32),
+        ),
+        in_specs=[smem, smem, vmem, vmem, vmem, vmem],
+        out_specs=(vmem, vmem, vmem, vmem),
+        compiler_params=pltpu.CompilerParams(vmem_limit_bytes=48 * 1024 * 1024),
+        cost_estimate=pl.CostEstimate(
+            flops=flops, transcendentals=windows_n * WIN * keys, bytes_accessed=8 * 1024 * 1024
+        ),
+    )(key_index, length_ext, query_win, k_ext, v_ext, grad_win)
 
 
 def shards(query_feats, key_feats, value_feats, grad_output, lengths, members, neighbours):
@@ -112,83 +183,22 @@
     def to_voxels(slot_vals):
         return gather_rows(slot_vals.reshape(windows_n * WIN, -1), slot_of)
 
+    grad_heads_early = lax.all_to_all(grad_output, "seq", split_axis=1, concat_axis=0, tiled=True)
     query_win, kv_win = to_windows(query_heads, key_heads, value_heads, members)
     received = padded(border_rows(kv_win, border), (("space", 0),), border)
     kv_ext = extend_windows(kv_win, received, border)
 
-    def forward_block(block_id):
-        key_index = window_keys(block_id, per_block, border, neighbours)
-        query_blk = lax.dynamic_slice_in_dim(query_win, block_id * per_block, per_block, 0)
-        attn_probs, query_h, key_h, value_h, score_scale = block_attention(
-            query_blk, key_index, kv_ext, length_ext, head_count
-        )
-        slot_out = jnp.einsum(
-            "whqk,wkhd->wqhd",
-            attn_probs.astype(jnp.bfloat16),
-            value_h,
-            preferred_element_type=jnp.float32,
-        )
-        return slot_out.astype(jnp.bfloat16).reshape(per_block, WIN, col_width)
-
-    out_slots = lax.map(forward_block, jnp.arange(block_count, dtype=jnp.int32)).reshape(
-        windows_n, WIN, col_width
+    key_index = jnp.concatenate(
+        [border + jnp.arange(windows_n, dtype=jnp.int32)[:, None], neighbours], axis=1
+    ).reshape(-1)
+    k_ext = kv_ext[..., :col_width]
+    v_ext = kv_ext[..., col_width:]
+    grad_win = gather_rows(grad_heads_early, members) * slot_alive[:, :, None].astype(jnp.bfloat16)
+    out_slots, grad_query_blocks, dk_ext, dv_ext = window_attention(
+        key_index, length_ext, query_win, k_ext, v_ext, grad_win
     )
     attended = lax.all_to_all(to_voxels(out_slots), "seq", split_axis=0, concat_axis=1, tiled=True)
-    grad_heads = lax.all_to_all(grad_output, "seq", split_axis=1, concat_axis=0, tiled=True)
-    grad_win = gather_rows(grad_heads, members) * slot_alive[:, :, None].astype(jnp.bfloat16)
-    query_back, kv_back = (query_win, kv_ext)
-
-    def backward_block(grad_ext, block_id):
-        key_index = window_keys(block_id, per_block, border, neighbours)
-        start_row = block_id * per_block
-        query_blk = lax.dynamic_slice_in_dim(query_back, start_row, per_block, 0)
-        attn_probs, query_h, key_h, value_h, score_scale = block_attention(
-            query_blk, key_index, kv_back, length_ext, head_count
-        )
-        grad_h = lax.dynamic_slice_in_dim(grad_win, start_row, per_block, 0).reshape(
-            per_block, WIN, head_count, -1
-        )
-        out_h = lax.dynamic_slice_in_dim(out_slots, start_row, per_block, 0).reshape(
-            per_block, WIN, head_count, -1
-        )
-        row_delta = jnp.transpose(
-            jnp.sum(grad_h.astype(jnp.float32) * out_h.astype(jnp.float32), axis=-1), (0, 2, 1)
-        )
-        grad_probs = jnp.einsum(
-            "wqhd,wkhd->whqk", grad_h, value_h, preferred_element_type=jnp.float32
-        )
-        grad_scores = (attn_probs * (grad_probs - row_delta[..., None]) * score_scale).astype(
-            jnp.bfloat16
-        )
-        grad_query = jnp.einsum(
-            "whqk,wkhd->wqhd", grad_scores, key_h, preferred_element_type=jnp.float32
-        )
-        grad_key = jnp.einsum(
-            "whqk,wqhd->wkhd", grad_scores, query_h, preferred_element_type=jnp.float32
-        )
-        grad_value = jnp.einsum(
-            "whqk,wqhd->wkhd",
-            attn_probs.astype(jnp.bfloat16),
-            grad_h,
-            preferred_element_type=jnp.float32,
-        )
-        key_count = key_index.shape[1]
-        key_terms = jnp.concatenate(
-            [
-                grad_key.reshape(per_block, key_count, WIN, col_width),
-                grad_value.reshape(per_block, key_count, WIN, col_width),
-            ],
-            axis=-1,
-        )
-        return (
-            grad_ext.at[key_index].add(key_terms),
-            grad_query.astype(jnp.bfloat16).reshape(per_block, WIN, col_width),
-        )
-
-    grad_start = jnp.zeros((windows_n + 2 * border, WIN, 2 * col_width), jnp.float32)
-    grad_ext, grad_query_blocks = lax.scan(
-        backward_block, grad_start, jnp.arange(block_count, dtype=jnp.int32)
-    )
+    grad_ext = jnp.concatenate([dk_ext, dv_ext], axis=-1)
     received_grads = padded(
         border_rows(grad_ext, border).astype(jnp.bfloat16), (("space", 0),), border
     ).astype(jnp.float32)

time: 863 us -> 511 us (0.59)
  the two profiles are of different devices: /device:TPU:48 before, /device:TPU:40 now
where the time goes in v1:
time: 511 us; the launch traced here: 510 us
  waiting for transfers between devices  180 us (35%)
  local copies, waits for them, and re-layouts  153 us (30%)
  Pallas kernels  81.7 us (16%)
  starting transfers between devices  66 us (13%)
  other arithmetic  28.8 us (6%)
    gather x6, local copies, waits for them, and re-layouts, gather_rows(): return jnp.take(source, indices, axis=0)  105 us
    pallas_call x1, Pallas kernels, window_attention(): pl.pallas_call(attention_kernel, out_shape=(jax.ShapeDtypeStruct(query_wi...  81.7 us
    all_to_all x1, waiting for transfers between devices, shards(): lax.all_to_all(key_feats, 'seq', split_axis=1, concat_axis=0, tiled=True)  31.3 us
    all_to_all x1, waiting for transfers between devices, shards(): lax.all_to_all(query_feats, 'seq', split_axis=1, concat_axis=0, tiled=True)  31.2 us
    all_to_all x1, waiting for transfers between devices, shards(): lax.all_to_all(kv_grads[:, :col_width], 'seq', split_axis=0, concat_axis=...  31.1 us
    all_to_all x1, waiting for transfers between devices, shards(): lax.all_to_all(value_feats, 'seq', split_axis=1, concat_axis=0, tiled=True)  30.3 us
    all_to_all x1, waiting for transfers between devices, shards(): lax.all_to_all(kv_grads[:, col_width:], 'seq', split_axis=0, concat_axis=...  28.3 us
    scatter x1, local copies, waits for them, and re-layouts, shards(): slot_of = jnp.zeros((voxel_count,), jnp.int32).at[flat_slots].set(jnp.ara...  23 us
  transfers between devices with their start and end apart: 12, of which 8 were waited for; matrix products, arithmetic and copies ran while one was open for 22% of the time, Pallas kernels for 0%

profile of v1, /device:TPU:40, one launch (start us, length us, event | category | flops | bytes accessed | tf_op | source)
XLA Modules:
  0.0 510.2 jit_solution(16211252236119784083)
XLA Ops:
  2.8 16.3 %all-to-all-start = ((bf16[128,32,64]{0,2,1:T(8,128)(2,1)}), bf16[128,32,64]{0,2,1:T(8,128)(2,1)S(1)}, u32[]{:S(2)}, u32[]{:S(2)}) async-start(bf16[128,32,64]{0,2,1:T(8,128)(2,1)} %bitcast.4), calls=%async_computation | async-start | bytes 1048576 | tf_op jit(solution)/shard_map/all_to_all | solution.py:171
  20.1 31.2 %all-to-all-done = bf16[128,32,64]{0,2,1:T(8,128)(2,1)S(1)} async-done(((bf16[128,32,64]{0,2,1:T(8,128)(2,1)}), bf16[128,32,64]{0,2,1:T(8,128)(2,1)S(1)}, u32[]{:S(2)}, u32[]{:S(2)}) %all-to-all-start) | async-done | bytes 524320 | tf_op jit(solution)/shard_map/all_to_all | solution.py:171
  51.3 4.2 all-to-all-start.1
  56.5 31.3 %all-to-all-done.1 = bf16[128,32,64]{0,2,1:T(8,128)(2,1)S(1)} async-done(((bf16[128,32,64]{0,2,1:T(8,128)(2,1)}), bf16[128,32,64]{0,2,1:T(8,128)(2,1)S(1)}, u32[]{:S(2)}, u32[]{:S(2)}) %all-to-all-start.1) | async-done | bytes 524320 | tf_op jit(solution)/shard_map/all_to_all | solution.py:172
  87.8 4.1 all-to-all-start.2
  94.1 30.3 %all-to-all-done.2 = bf16[128,32,64]{0,2,1:T(8,128)(2,1)S(1)} async-done(((bf16[128,32,64]{0,2,1:T(8,128)(2,1)}), bf16[128,32,64]{0,2,1:T(8,128)(2,1)S(1)}, u32[]{:S(2)}, u32[]{:S(2)}) %all-to-all-start.2) | async-done | bytes 524320 | tf_op jit(solution)/shard_map/all_to_all | solution.py:173
  124.3 4.1 all-to-all-start.3
  129.2 23.0 %scatter_custom_fusion = s32[4096]{0:T(1024)S(1)} fusion(s32[6144]{0:T(1024)S(1)} %bitcast.63, s32[6144]{0:T(1024)S(1)} %iota.16, s32[]{:T(128)} %constant.122.clone.1), kind=kCustom, calls=%fused_computation.39 | custom fusion | bytes 16388 | tf_op jit(solution)/shard_map/scatter | solution.py:180
  155.6 22.2 %gather_fusion.2 = bf16[6144,64]{1,0:T(8,128)(2,1)} fusion(bf16[4096,64]{1,0:T(8,128)(2,1)S(1)} %bitcast.44, s32[6144]{0:T(1024)S(1)} %broadcast_clamp_fusion), kind=kCustom, calls=%fused_computation.clone | custom fusion | bytes 1597440 | tf_op jit(solution)/shard_map/jit(_take)/gather | solution.py:29
  179.9 18.1 %gather_fusion = bf16[6144,128]{1,0:T(8,128)(2,1)S(1)} fusion(bf16[4096,128]{1,0:T(8,128)(2,1)S(1)} %pad_maximum_fusion.1, s32[6144]{0:T(1024)S(1)} %broadcast_clamp_fusion), kind=kCustom, calls=%fused_computation.4 | custom fusion | bytes 3170304 | tf_op jit(solution)/shard_map/jit(_take)/gather | solution.py:29
  198.5 22.2 %gather_fusion.3 = bf16[6144,64]{1,0:T(8,128)(2,1)} fusion(bf16[4096,64]{1,0:T(8,128)(2,1)S(1)} %bitcast.45, s32[6144]{0:T(1024)S(1)} %broadcast_clamp_fusion), kind=kCustom, calls=%fused_computation.2.clone | custom fusion | bytes 1597440 | tf_op jit(solution)/shard_map/jit(_take)/gather | solution.py:29
  223.8 3.6 collective-permute-start.1
  227.5 3.5 select_multiply_fusion
  231.6 2.9 fusion.14
  234.5 81.7 %shard_map.102 = (bf16[96,64,64]{2,1,0:T(8,128)(2,1)S(1)}, bf16[96,64,64]{2,1,0:T(8,128)(2,1)S(1)}, f32[128,64,64]{2,1,0:T(8,128)}, f32[128,64,64]{2,1,0:T(8,128)}) custom-call(s32[576]{0:T(1024)S(1)} %reshape.198.idx_ref, s32[128]{0:T(128)S(1)} %pad_add_fusion.1.len_ref, bf16[96,64,64]{2,1,0:T(8,128)(2,1)S(1)} %get-tuple-element.53.q_ref, ...), custom_call_target="tpu_custom_call" | custom-call | flops 2113929216 | bytes 8388608 | tf_op jit(solution)/shard_map/pallas_call | solution.py:129
  316.1 15.0 %gather_fusion.4 = bf16[4096,64]{1,0:T(8,128)(2,1)} fusion(bf16[6144,64]{1,0:T(8,128)(2,1)S(1)} %bitcast.43, s32[4096]{0:T(1024)S(1)} %fusion.7), kind=kCustom, calls=%fused_computation.1.clone | custom fusion | bytes 1064960 | tf_op jit(solution)/shard_map/jit(_take)/gather | solution.py:29
  331.2 15.0 %gather_fusion.5 = bf16[4096,64]{1,0:T(8,128)(2,1)} fusion(bf16[6144,64]{1,0:T(8,128)(2,1)S(1)} %bitcast.42, s32[4096]{0:T(1024)S(1)} %fusion.7), kind=kCustom, calls=%fused_computation.3.clone | custom fusion | bytes 1064960 | tf_op jit(solution)/shard_map/jit(_take)/gather | solution.py:29
  346.2 4.2 broadcast_select_fusion.2
  350.4 2.3 copy.40
  352.7 13.1 %all-to-all-start.4 = ((bf16[32,128,64]{1,2,0:T(8,128)(2,1)}), bf16[32,128,64]{1,2,0:T(8,128)(2,1)S(1)}, u32[]{:S(2)}, u32[]{:S(2)}) async-start(bf16[32,128,64]{1,2,0:T(8,128)(2,1)} %copy.40), calls=%async_computation.4 | async-start | bytes 1048576 | tf_op jit(solution)/shard_map/all_to_all | solution.py:200
  365.9 4.4 maximum_convert_fusion
  370.4 3.2 collective-permute-start.2
  373.6 2.4 collective-permute-start.3
  377.1 5.5 %fusion = f32[96,64,128]{2,1,0:T(8,128)} fusion(f32[128,64,64]{2,1,0:T(8,128)} %get-tuple-element.36, f32[128,64,64]{2,1,0:T(8,128)} %get-tuple-element.37), kind=kLoop, calls=%fused_computation.12 | loop fusion | flops 786432 | bytes 7340032 | tf_op jit(solution)/shard_map/concatenate | solution.py:201
  384.4 14.3 %all-to-all-done.4 = bf16[32,128,64]{1,2,0:T(8,128)(2,1)S(1)} async-done(((bf16[32,128,64]{1,2,0:T(8,128)(2,1)}), bf16[32,128,64]{1,2,0:T(8,128)(2,1)S(1)}, u32[]{:S(2)}, u32[]{:S(2)}) %all-to-all-start.4) | async-done | bytes 524320 | tf_op jit(solution)/shard_map/all_to_all | solution.py:200
  398.8 4.8 all-to-all-start.5
  407.7 12.1 %gather_fusion.1 = bf16[4096,128]{1,0:T(8,128)(2,1)S(1)} fusion(bf16[6144,128]{1,0:T(8,128)(2,1)S(1)} %bitcast.46, s32[4096]{0:T(1024)S(1)} %fusion.7), kind=kCustom, calls=%fused_computation.5 | custom fusion | bytes 2113536 | tf_op jit(solution)/shard_map/jit(_take)/gather | solution.py:29
  423.5 12.7 %all-to-all-done.5 = bf16[32,128,64]{1,2,0:T(8,128)(2,1)} async-done(((bf16[32,128,64]{1,2,0:T(8,128)(2,1)}), bf16[32,128,64]{1,2,0:T(8,128)(2,1)}, u32[]{:S(2)}, u32[]{:S(2)}) %all-to-all-start.5) | async-done | bytes 524320 | tf_op jit(solution)/shard_map/all_to_all | solution.py:211
  436.3 4.1 all-to-all-start.6
  441.5 31.1 %all-to-all-done.6 = bf16[32,128,64]{1,2,0:T(8,128)(2,1)S(1)} async-done(((bf16[32,128,64]{1,2,0:T(8,128)(2,1)}), bf16[32,128,64]{1,2,0:T(8,128)(2,1)S(1)}, u32[]{:S(2)}, u32[]{:S(2)}) %all-to-all-start.6) | async-done | bytes 524320 | tf_op jit(solution)/shard_map/all_to_all | solution.py:212
  472.6 4.1 all-to-all-start.7
  480.8 28.3 %all-to-all-done.7 = bf16[32,128,64]{1,2,0:T(8,128)(2,1)S(1)} async-done(((bf16[32,128,64]{1,2,0:T(8,128)(2,1)}), bf16[32,128,64]{1,2,0:T(8,128)(2,1)S(1)}, u32[]{:S(2)}, u32[]{:S(2)}) %all-to-all-start.7) | async-done | bytes 524320 | tf_op jit(solution)/shard_map/all_to_all | solution.py:213
  (72 shorter events, 33.5 us)
Async XLA Ops:
  0.6 18.4 %copy-start.5 = (bf16[128,2048]{1,0:T(8,128)(2,1)S(1)}, bf16[128,2048]{1,0:T(8,128)(2,1)}, u32[]{:S(2)}) copy-start(bf16[128,2048]{1,0:T(8,128)(2,1)} %param.16) | copy-start | bytes 1572868
  0.6 54.8 %copy-start.6 = (bf16[128,2048]{1,0:T(8,128)(2,1)S(1)}, bf16[128,2048]{1,0:T(8,128)(2,1)}, u32[]{:S(2)}) copy-start(bf16[128,2048]{1,0:T(8,128)(2,1)} %param.17) | copy-start | bytes 1572868
  2.8 48.5 %all-to-all-start = ((bf16[128,32,64]{0,2,1:T(8,128)(2,1)}), bf16[128,32,64]{0,2,1:T(8,128)(2,1)S(1)}, u32[]{:S(2)}, u32[]{:S(2)}) async-start(bf16[128,32,64]{0,2,1:T(8,128)(2,1)} %bitcast.4), calls=%async_computation | async-start | bytes 1048576 | tf_op jit(solution)/shard_map/all_to_all | solution.py:171
  19.1 73.7 %copy-start.8 = (s32[96,64]{0,1:T(8,128)S(1)}, s32[96,64]{0,1:T(8,128)}, u32[]{:S(2)}) copy-start(s32[96,64]{0,1:T(8,128)} %param.20) | copy-start | bytes 73732
  19.1 73.9 %copy-start.7 = (bf16[128,2048]{1,0:T(8,128)(2,1)S(1)}, bf16[128,2048]{1,0:T(8,128)(2,1)}, u32[]{:S(2)}) copy-start(bf16[128,2048]{1,0:T(8,128)(2,1)} %param.18) | copy-start | bytes 1572868
  51.3 36.5 %all-to-all-start.1 = ((bf16[128,32,64]{0,2,1:T(8,128)(2,1)}), bf16[128,32,64]{0,2,1:T(8,128)(2,1)S(1)}, u32[]{:S(2)}, u32[]{:S(2)}) async-start(bf16[128,32,64]{0,2,1:T(8,128)(2,1)} %bitcast.8), calls=%async_computation.1 | async-start | bytes 1048576 | tf_op jit(solution)/shard_map/all_to_all | solution.py:172
  55.5 73.3 %copy-start.9 = (s32[96,5]{0,1:T(8,128)S(1)}, s32[96,5]{0,1:T(8,128)}, u32[]{:S(2)}) copy-start(s32[96,5]{0,1:T(8,128)} %param.21) | copy-start | bytes 5764
  87.8 36.5 %all-to-all-start.2 = ((bf16[128,32,64]{0,2,1:T(8,128)(2,1)}), bf16[128,32,64]{0,2,1:T(8,128)(2,1)S(1)}, u32[]{:S(2)}, u32[]{:S(2)}) async-start(bf16[128,32,64]{0,2,1:T(8,128)(2,1)} %bitcast.11), calls=%async_computation.2 | async-start | bytes 1048576 | tf_op jit(solution)/shard_map/all_to_all | solution.py:173
  124.3 73.7 %all-to-all-start.3 = ((bf16[128,32,64]{0,2,1:T(8,128)(2,1)}), bf16[128,32,64]{0,2,1:T(8,128)(2,1)S(1)}, u32[]{:S(2)}, u32[]{:S(2)}) async-start(bf16[128,32,64]{0,2,1:T(8,128)(2,1)} %bitcast.15), calls=%async_computation.3 | async-start | bytes 1048576 | tf_op jit(solution)/shard_map/all_to_all | solution.py:186
  220.7 6.8 %copy-start.2 = (bf16[6144,64]{1,0:T(8,128)(2,1)S(1)}, bf16[6144,64]{1,0:T(8,128)(2,1)}, u32[]{:S(2)}) copy-start(bf16[6144,64]{1,0:T(8,128)(2,1)} %gather_fusion.2) | copy-start | bytes 2359300
  220.7 6.8 %copy-start.3 = (bf16[6144,64]{1,0:T(8,128)(2,1)S(1)}, bf16[6144,64]{1,0:T(8,128)(2,1)}, u32[]{:S(2)}) copy-start(bf16[6144,64]{1,0:T(8,128)(2,1)} %gather_fusion.3) | copy-start | bytes 2359300
  221.9 9.1 %collective-permute-start = (bf16[16,64,128]{2,1,0:T(8,128)(2,1)S(1)}, bf16[16,64,128]{2,1,0:T(8,128)(2,1)S(1)}, u32[]{:S(2)}, u32[]{:S(2)}) collective-permute-start(bf16[16,64,128]{2,1,0:T(8,128)(2,1)S(1)} %get-tuple-element.46), channel_id=1, source_target_pairs={{0,32},{32,64},{64,96},{96,128},{128,160},{160,192},{192,224},{224... | collective-permute-start | bytes 786440 | tf_op jit(solution)/shard_map/ppermute | solution.py:22
  223.8 7.5 %collective-permute-start.1 = (bf16[16,64,128]{2,1,0:T(8,128)(2,1)S(1)}, bf16[16,64,128]{2,1,0:T(8,128)(2,1)S(1)}, u32[]{:S(2)}, u32[]{:S(2)}) collective-permute-start(bf16[16,64,128]{2,1,0:T(8,128)(2,1)S(1)} %get-tuple-element.47), channel_id=1, source_target_pairs={{32,0},{64,32},{96,64},{128,96},{160,128},{192,160},{224,192},{256... | collective-permute-start | bytes 786440 | tf_op jit(solution)/shard_map/ppermute | solution.py:23
  331.2 15.0 %copy-start.4 = (bf16[4096,64]{1,0:T(8,128)(2,1)S(1)}, bf16[4096,64]{1,0:T(8,128)(2,1)}, u32[]{:S(2)}) copy-start(bf16[4096,64]{1,0:T(8,128)(2,1)} %gather_fusion.4) | copy-start | bytes 1572868
  352.7 46.0 %all-to-all-start.4 = ((bf16[32,128,64]{1,2,0:T(8,128)(2,1)}), bf16[32,128,64]{1,2,0:T(8,128)(2,1)S(1)}, u32[]{:S(2)}, u32[]{:S(2)}) async-start(bf16[32,128,64]{1,2,0:T(8,128)(2,1)} %copy.40), calls=%async_computation.4 | async-start | bytes 1048576 | tf_op jit(solution)/shard_map/all_to_all | solution.py:200
  370.4 12.2 %collective-permute-start.2 = (bf16[16,64,128]{2,1,0:T(8,128)(2,1)S(1)}, bf16[16,64,128]{2,1,0:T(8,128)(2,1)S(1)}, u32[]{:S(2)}, u32[]{:S(2)}) collective-permute-start(bf16[16,64,128]{2,1,0:T(8,128)(2,1)S(1)} %get-tuple-element.42), channel_id=1, source_target_pairs={{0,32},{32,64},{64,96},{96,128},{128,160},{160,192},{192,224},{224... | collective-permute-start | bytes 786440 | tf_op jit(solution)/shard_map/ppermute | solution.py:22
  373.6 9.0 %collective-permute-start.3 = (bf16[16,64,128]{2,1,0:T(8,128)(2,1)S(1)}, bf16[16,64,128]{2,1,0:T(8,128)(2,1)S(1)}, u32[]{:S(2)}, u32[]{:S(2)}) collective-permute-start(bf16[16,64,128]{2,1,0:T(8,128)(2,1)S(1)} %get-tuple-element.43), channel_id=1, source_target_pairs={{32,0},{64,32},{96,64},{128,96},{160,128},{192,160},{224,192},{256... | collective-permute-start | bytes 786440 | tf_op jit(solution)/shard_map/ppermute | solution.py:23
  377.1 5.5 %copy-start = (f32[128,64,64]{2,1,0:T(8,128)S(1)}, f32[128,64,64]{2,1,0:T(8,128)}, u32[]{:S(2)}) copy-start(f32[128,64,64]{2,1,0:T(8,128)} %get-tuple-element.36) | copy-start | bytes 6291460
  377.1 6.3 %copy-start.1 = (f32[128,64,64]{2,1,0:T(8,128)S(1)}, f32[128,64,64]{2,1,0:T(8,128)}, u32[]{:S(2)}) copy-start(f32[128,64,64]{2,1,0:T(8,128)} %get-tuple-element.37) | copy-start | bytes 6291460
  398.8 37.5 %all-to-all-start.5 = ((bf16[32,128,64]{1,2,0:T(8,128)(2,1)}), bf16[32,128,64]{1,2,0:T(8,128)(2,1)}, u32[]{:S(2)}, u32[]{:S(2)}) async-start(bf16[32,128,64]{1,2,0:T(8,128)(2,1)} %copy.41), calls=%async_computation.5 | async-start | bytes 1048576 | tf_op jit(solution)/shard_map/all_to_all | solution.py:211
  436.3 36.4 %all-to-all-start.6 = ((bf16[32,128,64]{1,2,0:T(8,128)(2,1)}), bf16[32,128,64]{1,2,0:T(8,128)(2,1)S(1)}, u32[]{:S(2)}, u32[]{:S(2)}) async-start(bf16[32,128,64]{1,2,0:T(8,128)(2,1)} %copy.42), calls=%async_computation.6 | async-start | bytes 1048576 | tf_op jit(solution)/shard_map/all_to_all | solution.py:212
  472.6 36.5 %all-to-all-start.7 = ((bf16[32,128,64]{1,2,0:T(8,128)(2,1)}), bf16[32,128,64]{1,2,0:T(8,128)(2,1)S(1)}, u32[]{:S(2)}, u32[]{:S(2)}) async-start(bf16[32,128,64]{1,2,0:T(8,128)(2,1)} %copy.43), calls=%async_computation.7 | async-start | bytes 1048576 | tf_op jit(solution)/shard_map/all_to_all | solution.py:213

commit v2 on v1

--- a/solution.py
+++ b/solution.py
@@ -167,12 +167,13 @@
         ]
     )
     slot_alive = jnp.arange(WIN, dtype=jnp.int32)[None, :] < own_length[:, None]
-    query_heads, key_heads, value_heads = (
-        lax.all_to_all(query_feats, "seq", split_axis=1, concat_axis=0, tiled=True),
-        lax.all_to_all(key_feats, "seq", split_axis=1, concat_axis=0, tiled=True),
-        lax.all_to_all(value_feats, "seq", split_axis=1, concat_axis=0, tiled=True),
-    )
-    voxel_count = query_heads.shape[0]
+    rows = query_feats.shape[0]
+    seq_n = lax.axis_size("seq")
+    stacked = jnp.stack([query_feats, key_feats, value_feats, grad_output], axis=1)
+    stacked = stacked.reshape(rows, 4, seq_n, col_width)
+    heads_all = lax.all_to_all(stacked, "seq", split_axis=2, concat_axis=0, tiled=True)
+    voxel_count = heads_all.shape[0]
+    table = heads_all.reshape(voxel_count, 4 * col_width)
     flat_slots = jnp.where(slot_alive, members, voxel_count).reshape(-1)
     slot_of = (
         jnp.zeros((voxel_count,), jnp.int32)
@@ -183,8 +184,10 @@
     def to_voxels(slot_vals):
         return gather_rows(slot_vals.reshape(windows_n * WIN, -1), slot_of)
 
-    grad_heads_early = lax.all_to_all(grad_output, "seq", split_axis=1, concat_axis=0, tiled=True)
-    query_win, kv_win = to_windows(query_heads, key_heads, value_heads, members)
+    win_all = gather_rows(table, members)
+    query_win = win_all[..., :col_width]
+    kv_win = win_all[..., col_width : 3 * col_width]
+    grad_win = win_all[..., 3 * col_width :] * slot_alive[:, :, None].astype(jnp.bfloat16)
     received = padded(border_rows(kv_win, border), (("space", 0),), border)
     kv_ext = extend_windows(kv_win, received, border)
 
@@ -193,11 +196,9 @@
     ).reshape(-1)
     k_ext = kv_ext[..., :col_width]
     v_ext = kv_ext[..., col_width:]
-    grad_win = gather_rows(grad_heads_early, members) * slot_alive[:, :, None].astype(jnp.bfloat16)
     out_slots, grad_query_blocks, dk_ext, dv_ext = window_attention(
         key_index, length_ext, query_win, k_ext, v_ext, grad_win
     )
-    attended = lax.all_to_all(to_voxels(out_slots), "seq", split_axis=0, concat_axis=1, tiled=True)
     grad_ext = jnp.concatenate([dk_ext, dv_ext], axis=-1)
     received_grads = padded(
         border_rows(grad_ext, border).astype(jnp.bfloat16), (("space", 0),), border
@@ -205,14 +206,13 @@
     own_grads = grad_ext[border : border + windows_n]
     own_grads = own_grads.at[:border].add(received_grads[:border])
     own_grads = own_grads.at[windows_n - border :].add(received_grads[3 * border :])
-    kv_grads = to_voxels(own_grads.astype(jnp.bfloat16))
-    grad_q_vox = to_voxels(grad_query_blocks.reshape(windows_n, WIN, col_width))
-    grad_queries, grad_keys, grad_values = (
-        lax.all_to_all(grad_q_vox, "seq", split_axis=0, concat_axis=1, tiled=True),
-        lax.all_to_all(kv_grads[:, :col_width], "seq", split_axis=0, concat_axis=1, tiled=True),
-        lax.all_to_all(kv_grads[:, col_width:], "seq", split_axis=0, concat_axis=1, tiled=True),
-    )
-    return (attended, grad_queries, grad_keys, grad_values)
+    slot_vals = jnp.concatenate(
+        [out_slots, grad_query_blocks, own_grads.astype(jnp.bfloat16)], axis=-1
+    )
+    vox = to_voxels(slot_vals).reshape(voxel_count, 4, 1, col_width)
+    back = lax.all_to_all(vox, "seq", split_axis=0, concat_axis=2, tiled=True)
+    back = back.reshape(rows, 4, seq_n * col_width)
+    return (back[:, 0], back[:, 1], back[:, 2], back[:, 3])
 
 
 def solution(mesh):

time: 511 us -> 440 us (0.86)
  the two profiles are of different devices: /device:TPU:40 before, /device:TPU:57 now
where the time goes in v2:
time: 440 us; the launch traced here: 438 us
  local copies, waits for them, and re-layouts  124 us (28%)
  blocking collectives  98.9 us (22%)
  waiting for transfers between devices  90.5 us (21%)
  Pallas kernels  81.6 us (19%)
  starting transfers between devices  27 us (6%)
  other arithmetic  15.6 us (4%)
    all_to_all x1, blocking collectives, shards(): back = lax.all_to_all(vox, 'seq', split_axis=0, concat_axis=2, tiled=True)  98.9 us
    pallas_call x1, Pallas kernels, window_attention(): pl.pallas_call(attention_kernel, out_shape=(jax.ShapeDtypeStruct(query_wi...  81.6 us
    all_to_all x1, waiting for transfers between devices, shards(): lax.all_to_all(stacked, 'seq', split_axis=2, concat_axis=0, tiled=True)  75.6 us
    gather x3, local copies, waits for them, and re-layouts, gather_rows(): return jnp.take(source, indices, axis=0)  46 us
    unnamed x22, local copies, waits for them, and re-layouts  25.9 us
    scatter x1, local copies, waits for them, and re-layouts, shards(): slot_of = jnp.zeros((voxel_count,), jnp.int32).at[flat_slots].set(jnp.ara...  23 us
    all_to_all x1, starting transfers between devices, shards(): lax.all_to_all(stacked, 'seq', split_axis=2, concat_axis=0, tiled=True)  15.9 us
    ppermute x2, waiting for transfers between devices, padded(): after = lax.ppermute(first, axis, down)  14.9 us
  transfers between devices with their start and end apart: 5, of which 3 were waited for; matrix products, arithmetic and copies ran while one was open for 6% of the time, Pallas kernels for 0%

profile of v2, /device:TPU:57, one launch (start us, length us, event | category | flops | bytes accessed | tf_op | source)
XLA Modules:
  0.0 438.4 jit_solution(4354156557292577578)
XLA Ops:
  0.7 1.4 copy.56
  2.1 1.3 copy.57
  4.2 1.5 copy.60
  5.7 15.9 %all-to-all-start = ((bf16[128,4,32,64]{0,3,1,2:T(8,128)(2,1)}), bf16[128,4,32,64]{0,3,1,2:T(8,128)(2,1)S(1)}, u32[]{:S(2)}, u32[]{:S(2)}) async-start(bf16[128,4,32,64]{0,3,1,2:T(8,128)(2,1)} %copy.60), calls=%async_computation | async-start | bytes 4194304 | tf_op jit(solution)/shard_map/all_to_all | solution.py:174
  23.3 23.0 %scatter_custom_fusion = s32[4096]{0:T(1024)S(1)} fusion(s32[6144]{0:T(1024)S(1)} %bitcast.46, s32[6144]{0:T(1024)S(1)} %iota.15, s32[]{:T(128)} %constant.99.clone.1), kind=kCustom, calls=%fused_computation.37 | custom fusion | bytes 16388 | tf_op jit(solution)/shard_map/scatter | solution.py:181
  46.5 75.6 %all-to-all-done = bf16[128,4,32,64]{0,3,1,2:T(8,128)(2,1)S(1)} async-done(((bf16[128,4,32,64]{0,3,1,2:T(8,128)(2,1)}), bf16[128,4,32,64]{0,3,1,2:T(8,128)(2,1)S(1)}, u32[]{:S(2)}, u32[]{:S(2)}) %all-to-all-start) | async-done | bytes 2097184 | tf_op jit(solution)/shard_map/all_to_all | solution.py:174
  122.1 4.7 %copy.73 = bf16[32,128,4,1,64]{4,2,1,0,3:T(4,128)(2,1)} copy(bf16[32,128,4,1,64]{1,4,2,0,3:T(8,128)(2,1)S(1)} %bitcast.39) | data formatting | bytes 4194304 | tf_op jit(solution)/shard_map/reshape | solution.py:176
  126.8 6.0 %reshape.223 = bf16[4096,256]{1,0:T(8,128)(2,1)S(1)} reshape(bf16[32,128,4,1,64]{4,2,1,0,3:T(4,128)(2,1)} %copy.73) | data formatting | bytes 4194304 | tf_op jit(solution)/shard_map/reshape | solution.py:176
  132.8 24.9 %gather_fusion = bf16[6144,256]{1,0:T(8,128)(2,1)} fusion(bf16[4096,256]{1,0:T(8,128)(2,1)S(1)} %reshape.223, s32[6144]{0:T(1024)S(1)} %broadcast_clamp_fusion), kind=kCustom, calls=%fused_computation | custom fusion | bytes 6316032 | tf_op jit(solution)/shard_map/jit(_take)/gather | solution.py:29
  157.7 3.2 broadcast_select_fusion
  161.8 4.6 %collective-permute-start = (bf16[16,64,128]{2,1,0:T(8,128)(2,1)S(1)}, bf16[16,64,128]{2,1,0:T(8,128)(2,1)S(1)}, u32[]{:S(2)}, u32[]{:S(2)}) collective-permute-start(bf16[16,64,128]{2,1,0:T(8,128)(2,1)S(1)} %get-tuple-element.50), channel_id=1, source_target_pairs={{0,32},{32,64},{64,96},{96,128},{128,160},{160,192},{192,224},{224... | collective-permute-start | bytes 786440 | tf_op jit(solution)/shard_map/ppermute | solution.py:22
  166.3 1.9 collective-permute-start.1
  168.2 2.3 slice_multiply_fusion
  170.5 7.1 %collective-permute-done.1 = bf16[16,64,128]{2,1,0:T(8,128)(2,1)S(1)} collective-permute-done((bf16[16,64,128]{2,1,0:T(8,128)(2,1)S(1)}, bf16[16,64,128]{2,1,0:T(8,128)(2,1)S(1)}, u32[]{:S(2)}, u32[]{:S(2)}) %collective-permute-start.1) | collective-permute-done | bytes 262176 | tf_op jit(solution)/shard_map/ppermute | solution.py:23
  177.9 2.9 fusion.15
  180.7 81.6 %shard_map.102 = (bf16[96,64,64]{2,1,0:T(8,128)(2,1)S(1)}, bf16[96,64,64]{2,1,0:T(8,128)(2,1)S(1)}, f32[128,64,64]{2,1,0:T(8,128)}, f32[128,64,64]{2,1,0:T(8,128)}) custom-call(s32[576]{0:T(1024)S(1)} %reshape.192.idx_ref, s32[128]{0:T(128)S(1)} %pad_add_fusion.1.len_ref, bf16[96,64,64]{2,1,0:T(8,128)(2,1)S(1)} %get-tuple-element.49.q_ref, ...), custom_call_target="tpu_custom_call" | custom-call | flops 2113929216 | bytes 8388608 | tf_op jit(solution)/shard_map/pallas_call | solution.py:129
  262.4 4.6 %maximum_convert_fusion = bf16[128,64,128]{2,1,0:T(8,128)(2,1)S(1)} fusion(f32[128,64,64]{2,1,0:T(8,128)} %get-tuple-element.35, f32[128,64,64]{2,1,0:T(8,128)} %get-tuple-element.34), kind=kLoop, calls=%fused_computation.3 | loop fusion | flops 4194304 | bytes 6291456 | tf_op jit(solution)/shard_map/convert.2
  267.0 2.1 collective-permute-start.2
  269.1 2.6 collective-permute-start.3
  272.6 7.8 %collective-permute-done.3 = bf16[16,64,128]{2,1,0:T(8,128)(2,1)S(1)} collective-permute-done((bf16[16,64,128]{2,1,0:T(8,128)(2,1)S(1)}, bf16[16,64,128]{2,1,0:T(8,128)(2,1)S(1)}, u32[]{:S(2)}, u32[]{:S(2)}) %collective-permute-start.3) | collective-permute-done | bytes 262176 | tf_op jit(solution)/shard_map/ppermute | solution.py:23
  281.1 1.4 pad_maximum_fusion
  282.5 16.9 %gather_fusion.1 = bf16[4096,256]{1,0:T(8,128)(2,1)} fusion(bf16[6144,256]{1,0:T(8,128)(2,1)S(1)} %bitcast.35, s32[4096]{0:T(1024)S(1)} %fusion.7), kind=kCustom, calls=%fused_computation.1 | custom fusion | bytes 4210688 | tf_op jit(solution)/shard_map/jit(_take)/gather | solution.py:29
  299.4 4.1 copy.65
  303.5 1.8 broadcast_select_fusion.1
  305.3 4.7 %copy.66 = bf16[4096,4,1,64]{3,1,2,0:T(4,128)(2,1)} copy(bf16[4096,4,1,64]{0,3,1,2:T(8,128)(2,1)S(1)} %broadcast_select_fusion.1) | data formatting | bytes 4194304 | tf_op jit(solution)/shard_map/jit(_take)/select_n | solution.py:29
  310.0 7.6 %reshape.226 = bf16[32,2,16384]{2,1,0:T(2,128)(2,1)S(1)} reshape(bf16[4096,1,4,64]{3,2,1,0:T(4,128)(2,1)} %bitcast.36) | data formatting | bytes 4194304
  317.7 98.9 %all_to_all.30 = bf16[32,2,16384]{2,1,0:T(2,128)(2,1)} all-to-all(bf16[32,2,16384]{2,1,0:T(2,128)(2,1)S(1)} %reshape.226), channel_id=1, replica_groups=mesh['space'=16,'seq'=32] {'seq'}, dimensions={0} | all-to-all | bytes 4194304 | tf_op jit(solution)/shard_map/all_to_all | solution.py:213
  416.5 8.9 %reshape.227 = bf16[4096,1,4,64]{3,2,1,0:T(4,128)(2,1)} reshape(bf16[32,2,16384]{2,1,0:T(2,128)(2,1)} %all_to_all.30) | data formatting | bytes 4194304
  425.5 5.7 %copy.75 = bf16[32,128,4,1,64]{1,4,0,2,3:T(8,128)(2,1)S(1)} copy(bf16[32,128,4,1,64]{4,2,1,0,3:T(4,128)(2,1)} %bitcast.37) | data formatting | bytes 4194304 | tf_op jit(solution)/shard_map/all_to_all | solution.py:213
  431.2 1.1 slice_bitcast_fusion
  432.3 2.0 copy.72
  434.4 2.0 copy.71
  (48 shorter events, 7.4 us)
Async XLA Ops:
  0.6 2.7 copy-start.2
  0.6 3.0 copy-start.3
  5.7 15.9 %copy-start.4 = (s32[96,64]{0,1:T(8,128)S(1)}, s32[96,64]{0,1:T(8,128)}, u32[]{:S(2)}) copy-start(s32[96,64]{0,1:T(8,128)} %param.16) | copy-start | bytes 73732
  5.7 16.9 %copy-start.5 = (s32[96,5]{0,1:T(8,128)S(1)}, s32[96,5]{0,1:T(8,128)}, u32[]{:S(2)}) copy-start(s32[96,5]{0,1:T(8,128)} %param.17) | copy-start | bytes 5764
  5.7 116.4 %all-to-all-start = ((bf16[128,4,32,64]{0,3,1,2:T(8,128)(2,1)}), bf16[128,4,32,64]{0,3,1,2:T(8,128)(2,1)S(1)}, u32[]{:S(2)}, u32[]{:S(2)}) async-start(bf16[128,4,32,64]{0,3,1,2:T(8,128)(2,1)} %copy.60), calls=%async_computation | async-start | bytes 4194304 | tf_op jit(solution)/shard_map/all_to_all | solution.py:174
  161.8 8.8 %collective-permute-start = (bf16[16,64,128]{2,1,0:T(8,128)(2,1)S(1)}, bf16[16,64,128]{2,1,0:T(8,128)(2,1)S(1)}, u32[]{:S(2)}, u32[]{:S(2)}) collective-permute-start(bf16[16,64,128]{2,1,0:T(8,128)(2,1)S(1)} %get-tuple-element.50), channel_id=1, source_target_pairs={{0,32},{32,64},{64,96},{96,128},{128,160},{160,192},{192,224},{224... | collective-permute-start | bytes 786440 | tf_op jit(solution)/shard_map/ppermute | solution.py:22
  166.3 11.3 %collective-permute-start.1 = (bf16[16,64,128]{2,1,0:T(8,128)(2,1)S(1)}, bf16[16,64,128]{2,1,0:T(8,128)(2,1)S(1)}, u32[]{:S(2)}, u32[]{:S(2)}) collective-permute-start(bf16[16,64,128]{2,1,0:T(8,128)(2,1)S(1)} %get-tuple-element.51), channel_id=1, source_target_pairs={{32,0},{64,32},{96,64},{128,96},{160,128},{192,160},{224,192},{256... | collective-permute-start | bytes 786440 | tf_op jit(solution)/shard_map/ppermute | solution.py:23
  262.4 9.3 %copy-start = (f32[128,64,64]{2,1,0:T(8,128)S(1)}, f32[128,64,64]{2,1,0:T(8,128)}, u32[]{:S(2)}) copy-start(f32[128,64,64]{2,1,0:T(8,128)} %get-tuple-element.34) | copy-start | bytes 6291460
  262.4 9.3 %copy-start.1 = (f32[128,64,64]{2,1,0:T(8,128)S(1)}, f32[128,64,64]{2,1,0:T(8,128)}, u32[]{:S(2)}) copy-start(f32[128,64,64]{2,1,0:T(8,128)} %get-tuple-element.35) | copy-start | bytes 6291460
  267.0 5.6 %collective-permute-start.2 = (bf16[16,64,128]{2,1,0:T(8,128)(2,1)S(1)}, bf16[16,64,128]{2,1,0:T(8,128)(2,1)S(1)}, u32[]{:S(2)}, u32[]{:S(2)}) collective-permute-start(bf16[16,64,128]{2,1,0:T(8,128)(2,1)S(1)} %get-tuple-element.56), channel_id=1, source_target_pairs={{0,32},{32,64},{64,96},{96,128},{128,160},{160,192},{192,224},{224... | collective-permute-start | bytes 786440 | tf_op jit(solution)/shard_map/ppermute | solution.py:22
  269.1 11.3 %collective-permute-start.3 = (bf16[16,64,128]{2,1,0:T(8,128)(2,1)S(1)}, bf16[16,64,128]{2,1,0:T(8,128)(2,1)S(1)}, u32[]{:S(2)}, u32[]{:S(2)}) collective-permute-start(bf16[16,64,128]{2,1,0:T(8,128)(2,1)S(1)} %get-tuple-element.57), channel_id=1, source_target_pairs={{32,0},{64,32},{96,64},{128,96},{160,128},{192,160},{224,192},{256... | collective-permute-start | bytes 786440 | tf_op jit(solution)/shard_map/ppermute | solution.py:23

commit v3 on v2

--- a/solution.py
+++ b/solution.py
@@ -169,10 +169,15 @@
     slot_alive = jnp.arange(WIN, dtype=jnp.int32)[None, :] < own_length[:, None]
     rows = query_feats.shape[0]
     seq_n = lax.axis_size("seq")
-    stacked = jnp.stack([query_feats, key_feats, value_feats, grad_output], axis=1)
-    stacked = stacked.reshape(rows, 4, seq_n, col_width)
-    heads_all = lax.all_to_all(stacked, "seq", split_axis=2, concat_axis=0, tiled=True)
-    voxel_count = heads_all.shape[0]
+    stacked = jnp.stack(
+        [
+            jnp.transpose(part.reshape(rows, seq_n, col_width), (1, 0, 2))
+            for part in (query_feats, key_feats, value_feats, grad_output)
+        ],
+        axis=2,
+    ).reshape(seq_n, rows, 4 * col_width)
+    heads_all = lax.all_to_all(stacked, "seq", split_axis=0, concat_axis=0, tiled=True)
+    voxel_count = seq_n * rows
     table = heads_all.reshape(voxel_count, 4 * col_width)
     flat_slots = jnp.where(slot_alive, members, voxel_count).reshape(-1)
     slot_of = (
@@ -209,10 +214,12 @@
     slot_vals = jnp.concatenate(
         [out_slots, grad_query_blocks, own_grads.astype(jnp.bfloat16)], axis=-1
     )
-    vox = to_voxels(slot_vals).reshape(voxel_count, 4, 1, col_width)
-    back = lax.all_to_all(vox, "seq", split_axis=0, concat_axis=2, tiled=True)
-    back = back.reshape(rows, 4, seq_n * col_width)
-    return (back[:, 0], back[:, 1], back[:, 2], back[:, 3])
+    vox = to_voxels(slot_vals).reshape(seq_n, rows, 4 * col_width)
+    back = lax.all_to_all(vox, "seq", split_axis=0, concat_axis=0, tiled=True)
+    back = back.reshape(seq_n, rows, 4, col_width)
+    return tuple(
+        jnp.transpose(back[:, :, i], (1, 0, 2)).reshape(rows, seq_n * col_width) for i in range(4)
+    )
 
 
 def solution(mesh):

time: 440 us -> 399 us (0.907)
  local copies, waits for them, and re-layouts: 124 us -> 85.6 us
    unnamed x22 -> x20, local copies, waits for them, and re-layouts: 25.9 us -> 7.3 us
    reshape x2 -> x0, local copies, waits for them, and re-layouts: 10.6 us -> none  [shards(): table = heads_all.reshape(voxel_count, 4 * col_width)]
    select_n x2 -> x1, local copies, waits for them, and re-layouts: 4.78 us -> 0.08 us  [gather_rows(): return jnp.take(source, indices, axis=0)]
  transfers between devices with their start and end apart: 5 -> 5, of which waited for: 3 -> 3; matrix products, arithmetic and copies ran while one was open for 6% -> 7% of each run, Pallas kernels for 0% -> 0%
where the time goes in v3:
time: 399 us
  blocking collectives  98.8 us (25%)
  waiting for transfers between devices  90.5 us (23%)
  local copies, waits for them, and re-layouts  85.6 us (21%)
  Pallas kernels  81.6 us (20%)
  starting transfers between devices  27 us (7%)
  other arithmetic  14 us (4%)
    all_to_all x1, blocking collectives, shards(): back = lax.all_to_all(vox, 'seq', split_axis=0, concat_axis=0, tiled=True)  98.8 us
    pallas_call x1, Pallas kernels, window_attention(): pl.pallas_call(attention_kernel, out_shape=(jax.ShapeDtypeStruct(query_wi...  81.6 us
    all_to_all x1, waiting for transfers between devices, shards(): lax.all_to_all(stacked, 'seq', split_axis=0, concat_axis=0, tiled=True)  75.7 us
    gather x3, local copies, waits for them, and re-layouts, gather_rows(): return jnp.take(source, indices, axis=0)  45.1 us
    scatter x1, local copies, waits for them, and re-layouts, shards(): slot_of = jnp.zeros((voxel_count,), jnp.int32).at[flat_slots].set(jnp.ara...  23 us
    all_to_all x1, starting transfers between devices, shards(): lax.all_to_all(stacked, 'seq', split_axis=0, concat_axis=0, tiled=True)  15.9 us
    ppermute x2, waiting for transfers between devices, padded(): after = lax.ppermute(first, axis, down)  14.9 us
  transfers between devices with their start and end apart: 5, of which 3 were waited for; matrix products, arithmetic and copies ran while one was open for 7% of the time, Pallas kernels for 0%

profile of v3, /device:TPU:57, one launch (start us, length us, event | category | flops | bytes accessed | tf_op | source)
XLA Modules:
  0.0 398.6 jit_solution(2693106299395906874)
XLA Ops:
  0.7 1.4 copy.21
  2.1 1.3 copy.22
  3.4 0.3 copy.23
  4.2 1.5 copy.25
  5.7 15.9 %all-to-all-start = ((bf16[32,128,256]{1,2,0:T(8,128)(2,1)}), bf16[32,128,256]{1,2,0:T(8,128)(2,1)}, u32[]{:S(2)}, u32[]{:S(2)}) async-start(bf16[32,128,256]{1,2,0:T(8,128)(2,1)} %bitcast.17), calls=%async_computation | async-start | bytes 4194304 | tf_op jit(solution)/shard_map/all_to_all | solution.py:179
  21.8 0.8 constant_dynamic-slice_fusion.1
  23.4 23.0 %scatter_custom_fusion = s32[4096]{0:T(1024)S(1)} fusion(s32[6144]{0:T(1024)S(1)} %bitcast.69, s32[6144]{0:T(1024)S(1)} %iota.15, s32[]{:T(128)} %constant.99.clone.1), kind=kCustom, calls=%fused_computation.33 | custom fusion | bytes 16388 | tf_op jit(solution)/shard_map/scatter | solution.py:186
  46.5 75.7 %all-to-all-done = bf16[32,128,256]{1,2,0:T(8,128)(2,1)} async-done(((bf16[32,128,256]{1,2,0:T(8,128)(2,1)}), bf16[32,128,256]{1,2,0:T(8,128)(2,1)}, u32[]{:S(2)}, u32[]{:S(2)}) %all-to-all-start) | async-done | bytes 2097184 | tf_op jit(solution)/shard_map/all_to_all | solution.py:179
  122.2 3.3 copy.26
  125.5 24.9 %gather_fusion = bf16[6144,256]{1,0:T(8,128)(2,1)} fusion(bf16[4096,256]{1,0:T(8,128)(2,1)S(1)} %bitcast.56, s32[6144]{0:T(1024)S(1)} %broadcast_clamp_fusion), kind=kCustom, calls=%fused_computation | custom fusion | bytes 6316032 | tf_op jit(solution)/shard_map/jit(_take)/gather | solution.py:29
  150.4 3.2 broadcast_select_fusion
  153.9 0.6 slice.137
  154.5 4.6 %collective-permute-start = (bf16[16,64,128]{2,1,0:T(8,128)(2,1)S(1)}, bf16[16,64,128]{2,1,0:T(8,128)(2,1)S(1)}, u32[]{:S(2)}, u32[]{:S(2)}) collective-permute-start(bf16[16,64,128]{2,1,0:T(8,128)(2,1)S(1)} %get-tuple-element.42), channel_id=1, source_target_pairs={{0,32},{32,64},{64,96},{96,128},{128,160},{160,192},{192,224},{224... | collective-permute-start | bytes 786440 | tf_op jit(solution)/shard_map/ppermute | solution.py:22
  159.0 1.9 collective-permute-start.1
  161.0 2.3 slice_multiply_fusion
  163.3 7.1 %collective-permute-done.1 = bf16[16,64,128]{2,1,0:T(8,128)(2,1)S(1)} collective-permute-done((bf16[16,64,128]{2,1,0:T(8,128)(2,1)S(1)}, bf16[16,64,128]{2,1,0:T(8,128)(2,1)S(1)}, u32[]{:S(2)}, u32[]{:S(2)}) %collective-permute-start.1) | collective-permute-done | bytes 262176 | tf_op jit(solution)/shard_map/ppermute | solution.py:23
  170.6 2.9 fusion.16
  173.5 81.6 %shard_map.102 = (bf16[96,64,64]{2,1,0:T(8,128)(2,1)S(1)}, bf16[96,64,64]{2,1,0:T(8,128)(2,1)S(1)}, f32[128,64,64]{2,1,0:T(8,128)}, f32[128,64,64]{2,1,0:T(8,128)}) custom-call(s32[576]{0:T(1024)S(1)} %reshape.199.idx_ref, s32[128]{0:T(128)S(1)} %pad_add_fusion.1.len_ref, bf16[96,64,64]{2,1,0:T(8,128)(2,1)S(1)} %get-tuple-element.41.q_ref, ...), custom_call_target="tpu_custom_call" | custom-call | flops 2113929216 | bytes 8388608 | tf_op jit(solution)/shard_map/pallas_call | solution.py:129
  255.1 4.6 %maximum_convert_fusion = bf16[128,64,128]{2,1,0:T(8,128)(2,1)S(1)} fusion(f32[128,64,64]{2,1,0:T(8,128)} %get-tuple-element.35, f32[128,64,64]{2,1,0:T(8,128)} %get-tuple-element.34), kind=kLoop, calls=%fused_computation.3 | loop fusion | flops 4194304 | bytes 6291456 | tf_op jit(solution)/shard_map/convert.2
  259.7 2.1 collective-permute-start.2
  261.8 2.6 collective-permute-start.3
  264.4 0.9 fusion
  265.3 7.8 %collective-permute-done.3 = bf16[16,64,128]{2,1,0:T(8,128)(2,1)S(1)} collective-permute-done((bf16[16,64,128]{2,1,0:T(8,128)(2,1)S(1)}, bf16[16,64,128]{2,1,0:T(8,128)(2,1)S(1)}, u32[]{:S(2)}, u32[]{:S(2)}) %collective-permute-start.3) | collective-permute-done | bytes 262176 | tf_op jit(solution)/shard_map/ppermute | solution.py:23
  273.4 0.3 convert_element_type.17
  273.8 1.4 pad_maximum_fusion
  275.2 16.9 %gather_fusion.1 = bf16[4096,256]{1,0:T(8,128)(2,1)} fusion(bf16[6144,256]{1,0:T(8,128)(2,1)S(1)} %bitcast.57, s32[4096]{0:T(1024)S(1)} %fusion.7), kind=kCustom, calls=%fused_computation.1 | custom fusion | bytes 4210688 | tf_op jit(solution)/shard_map/jit(_take)/gather | solution.py:29
  292.2 3.2 copy.29
  295.6 98.8 %all_to_all.10 = bf16[32,128,256]{1,2,0:T(8,128)(2,1)S(1)} all-to-all(bf16[32,128,256]{1,2,0:T(8,128)(2,1)S(1)} %broadcast_select_fusion.1), channel_id=1, replica_groups=mesh['space'=16,'seq'=32] {'seq'}, dimensions={0} | all-to-all | bytes 4194304 | tf_op jit(solution)/shard_map/all_to_all | solution.py:218
  394.6 1.0 copy.33
  395.6 1.0 copy.32
  396.6 1.0 copy.31
  397.6 1.0 copy.30
  (43 shorter events, 2.8 us)
Async XLA Ops:
  0.6 2.7 copy-start.2
  0.6 3.0 copy-start.3
  5.7 15.9 %copy-start.4 = (s32[96,64]{0,1:T(8,128)S(1)}, s32[96,64]{0,1:T(8,128)}, u32[]{:S(2)}) copy-start(s32[96,64]{0,1:T(8,128)} %param.16) | copy-start | bytes 73732
  5.7 17.0 %copy-start.5 = (s32[96,5]{0,1:T(8,128)S(1)}, s32[96,5]{0,1:T(8,128)}, u32[]{:S(2)}) copy-start(s32[96,5]{0,1:T(8,128)} %param.17) | copy-start | bytes 5764
  5.7 116.5 %all-to-all-start = ((bf16[32,128,256]{1,2,0:T(8,128)(2,1)}), bf16[32,128,256]{1,2,0:T(8,128)(2,1)}, u32[]{:S(2)}, u32[]{:S(2)}) async-start(bf16[32,128,256]{1,2,0:T(8,128)(2,1)} %bitcast.17), calls=%async_computation | async-start | bytes 4194304 | tf_op jit(solution)/shard_map/all_to_all | solution.py:179
  154.5 8.8 %collective-permute-start = (bf16[16,64,128]{2,1,0:T(8,128)(2,1)S(1)}, bf16[16,64,128]{2,1,0:T(8,128)(2,1)S(1)}, u32[]{:S(2)}, u32[]{:S(2)}) collective-permute-start(bf16[16,64,128]{2,1,0:T(8,128)(2,1)S(1)} %get-tuple-element.42), channel_id=1, source_target_pairs={{0,32},{32,64},{64,96},{96,128},{128,160},{160,192},{192,224},{224... | collective-permute-start | bytes 786440 | tf_op jit(solution)/shard_map/ppermute | solution.py:22
  159.0 11.3 %collective-permute-start.1 = (bf16[16,64,128]{2,1,0:T(8,128)(2,1)S(1)}, bf16[16,64,128]{2,1,0:T(8,128)(2,1)S(1)}, u32[]{:S(2)}, u32[]{:S(2)}) collective-permute-start(bf16[16,64,128]{2,1,0:T(8,128)(2,1)S(1)} %get-tuple-element.43), channel_id=1, source_target_pairs={{32,0},{64,32},{96,64},{128,96},{160,128},{192,160},{224,192},{256... | collective-permute-start | bytes 786440 | tf_op jit(solution)/shard_map/ppermute | solution.py:23
  255.1 9.3 %copy-start = (f32[128,64,64]{2,1,0:T(8,128)S(1)}, f32[128,64,64]{2,1,0:T(8,128)}, u32[]{:S(2)}) copy-start(f32[128,64,64]{2,1,0:T(8,128)} %get-tuple-element.34) | copy-start | bytes 6291460
  255.1 9.3 %copy-start.1 = (f32[128,64,64]{2,1,0:T(8,128)S(1)}, f32[128,64,64]{2,1,0:T(8,128)}, u32[]{:S(2)}) copy-start(f32[128,64,64]{2,1,0:T(8,128)} %get-tuple-element.35) | copy-start | bytes 6291460
  259.7 5.6 %collective-permute-start.2 = (bf16[16,64,128]{2,1,0:T(8,128)(2,1)S(1)}, bf16[16,64,128]{2,1,0:T(8,128)(2,1)S(1)}, u32[]{:S(2)}, u32[]{:S(2)}) collective-permute-start(bf16[16,64,128]{2,1,0:T(8,128)(2,1)S(1)} %get-tuple-element.48), channel_id=1, source_target_pairs={{0,32},{32,64},{64,96},{96,128},{128,160},{160,192},{192,224},{224... | collective-permute-start | bytes 786440 | tf_op jit(solution)/shard_map/ppermute | solution.py:22
  261.8 11.3 %collective-permute-start.3 = (bf16[16,64,128]{2,1,0:T(8,128)(2,1)S(1)}, bf16[16,64,128]{2,1,0:T(8,128)(2,1)S(1)}, u32[]{:S(2)}, u32[]{:S(2)}) collective-permute-start(bf16[16,64,128]{2,1,0:T(8,128)(2,1)S(1)} %get-tuple-element.49), channel_id=1, source_target_pairs={{32,0},{64,32},{96,64},{128,96},{160,128},{192,160},{224,192},{256... | collective-permute-start | bytes 786440 | tf_op jit(solution)/shard_map/ppermute | solution.py:23

commit v4 on v3

--- a/solution.py
+++ b/solution.py
@@ -74,73 +74,77 @@
     return (attn_probs, query_heads, key_heads, value_heads, score_scale)
 
 
-def attention_kernel(idx_ref, len_ref, q_ref, k_ref, v_ref, g_ref, out_ref, dq_ref, dk_ref, dv_ref):
-    windows_n = q_ref.shape[0]
+def attention_kernel(idx_ref, len_ref, qg_ref, kv_ref, out_ref, dkv_ref):
+    windows_n, _, lanes = qg_ref.shape
+    width = lanes // 2
     nb = idx_ref.shape[0] // windows_n
     keys = nb * WIN
     scale = HEAD ** (-0.5)
-    dk_ref[...] = jnp.zeros(dk_ref.shape, dk_ref.dtype)
-    dv_ref[...] = jnp.zeros(dv_ref.shape, dv_ref.dtype)
+    dkv_ref[...] = jnp.zeros(dkv_ref.shape, dkv_ref.dtype)
     col = lax.broadcasted_iota(jnp.int32, (1, keys), 1)
     col_block = col // WIN
     col_slot = col % WIN
+    lane = lax.broadcasted_iota(jnp.int32, (1, lanes), 1)
+    first_half = lane < width
+    nt = (((1,), (1,)), ((), ()))
+    tn = (((0,), (0,)), ((), ()))
 
     def body(w, carry):
         ids = [idx_ref[w * nb + j] for j in range(nb)]
-        q = q_ref[w]
-        g = g_ref[w]
-        k_all = jnp.concatenate([k_ref[i] for i in ids], axis=0)
-        v_all = jnp.concatenate([v_ref[i] for i in ids], axis=0)
+        qg = qg_ref[w]
+        zero = jnp.zeros_like(qg)
+        q_pad = jnp.where(first_half, qg, zero)
+        g_pad = jnp.where(first_half, zero, qg)
+        qg_blocks = jnp.concatenate([q_pad, g_pad], axis=0)
+        kv_all = jnp.concatenate([kv_ref[i] for i in ids], axis=0)
         limit = jnp.zeros((1, keys), jnp.int32)
         for j in range(nb):
             limit = jnp.where(col_block == j, len_ref[ids[j]], limit)
         alive = col_slot < limit
-        nt = (((1,), (1,)), ((), ()))
-        tn = (((0,), (0,)), ((), ()))
-        scores = lax.dot_general(q, k_all, nt, preferred_element_type=jnp.float32) * scale
+        both = lax.dot_general(qg_blocks, kv_all, nt, preferred_element_type=jnp.float32)
+        scores = both[:WIN] * scale
+        grad_probs = both[WIN:]
         scores = jnp.where(alive, scores, MASKED_SCORE)
         row_max = jnp.max(scores, axis=-1, keepdims=True)
         exp_scores = jnp.exp(scores - row_max)
         probs = exp_scores / jnp.sum(exp_scores, axis=-1, keepdims=True)
         weights = probs.astype(jnp.bfloat16)
-        slot_out = jnp.dot(weights, v_all, preferred_element_type=jnp.float32).astype(jnp.bfloat16)
-        out_ref[w] = slot_out
-        delta = jnp.sum(g.astype(jnp.float32) * slot_out.astype(jnp.float32), axis=-1, keepdims=True)
-        grad_probs = lax.dot_general(g, v_all, nt, preferred_element_type=jnp.float32)
+        out_full = jnp.dot(weights, kv_all, preferred_element_type=jnp.float32).astype(jnp.bfloat16)
+        delta = jnp.sum(
+            g_pad.astype(jnp.float32) * out_full.astype(jnp.float32), axis=-1, keepdims=True
+        )
         grad_scores = (probs * (grad_probs - delta) * scale).astype(jnp.bfloat16)
-        dq_ref[w] = jnp.dot(grad_scores, k_all, preferred_element_type=jnp.float32).astype(jnp.bfloat16)
-        grad_k = lax.dot_general(grad_scores, q, tn, preferred_element_type=jnp.float32)
-        grad_v = lax.dot_general(weights, g, tn, preferred_element_type=jnp.float32)
+        dq_full = jnp.dot(grad_scores, kv_all, preferred_element_type=jnp.float32).astype(jnp.bfloat16)
+        out_ref[w] = jnp.where(first_half, dq_full, out_full)
+        score_blocks = jnp.concatenate([grad_scores, weights], axis=0)
+        grad_kv = lax.dot_general(score_blocks, qg_blocks, tn, preferred_element_type=jnp.float32)
         for j in range(nb):
-            dk_ref[ids[j]] += grad_k[j * WIN : (j + 1) * WIN]
-            dv_ref[ids[j]] += grad_v[j * WIN : (j + 1) * WIN]
+            dkv_ref[ids[j]] += grad_kv[j * WIN : (j + 1) * WIN]
         return carry
 
-    lax.fori_loop(0, windows_n, body, 0)
-
-
-def window_attention(key_index, length_ext, query_win, k_ext, v_ext, grad_win):
-    windows_n, _, width = query_win.shape
-    ext_n = k_ext.shape[0]
+    lax.fori_loop(0, windows_n, body, 0, unroll=2)
+
+
+def window_attention(key_index, length_ext, qg_win, kv_ext):
+    windows_n, _, lanes = qg_win.shape
+    ext_n = kv_ext.shape[0]
     keys = (key_index.shape[0] // windows_n) * WIN
-    flops = 2 * windows_n * WIN * keys * width * 7
+    flops = 2 * windows_n * WIN * keys * lanes * 6
     vmem = pl.BlockSpec(memory_space=pltpu.VMEM)
     smem = pl.BlockSpec(memory_space=pltpu.SMEM)
     return pl.pallas_call(
         attention_kernel,
         out_shape=(
-            jax.ShapeDtypeStruct(query_win.shape, jnp.bfloat16),
-            jax.ShapeDtypeStruct(query_win.shape, jnp.bfloat16),
-            jax.ShapeDtypeStruct((ext_n, WIN, width), jnp.float32),
-            jax.ShapeDtypeStruct((ext_n, WIN, width), jnp.float32),
+            jax.ShapeDtypeStruct(qg_win.shape, jnp.bfloat16),
+            jax.ShapeDtypeStruct((ext_n, WIN, lanes), jnp.float32),
         ),
-        in_specs=[smem, smem, vmem, vmem, vmem, vmem],
-        out_specs=(vmem, vmem, vmem, vmem),
+        in_specs=[smem, smem, vmem, vmem],
+        out_specs=(vmem, vmem),
         compiler_params=pltpu.CompilerParams(vmem_limit_bytes=48 * 1024 * 1024),
         cost_estimate=pl.CostEstimate(
             flops=flops, transcendentals=windows_n * WIN * keys, bytes_accessed=8 * 1024 * 1024
         ),
-    )(key_index, length_ext, query_win, k_ext, v_ext, grad_win)
+    )(key_index, length_ext, qg_win, kv_ext)
 
 
 def shards(query_feats, key_feats, value_feats, grad_output, lengths, members, neighbours):
@@ -172,7 +176,7 @@
     stacked = jnp.stack(
         [
             jnp.transpose(part.reshape(rows, seq_n, col_width), (1, 0, 2))
-            for part in (query_feats, key_feats, value_feats, grad_output)
+            for part in (query_feats, grad_output, key_feats, value_feats)
         ],
         axis=2,
     ).reshape(seq_n, rows, 4 * col_width)
@@ -190,21 +194,19 @@
         return gather_rows(slot_vals.reshape(windows_n * WIN, -1), slot_of)
 
     win_all = gather_rows(table, members)
-    query_win = win_all[..., :col_width]
-    kv_win = win_all[..., col_width : 3 * col_width]
-    grad_win = win_all[..., 3 * col_width :] * slot_alive[:, :, None].astype(jnp.bfloat16)
+    lane_live = jnp.logical_or(
+        jnp.arange(2 * col_width, dtype=jnp.int32)[None, None, :] < col_width,
+        slot_alive[:, :, None],
+    )
+    qg_win = win_all[..., : 2 * col_width] * lane_live.astype(jnp.bfloat16)
+    kv_win = win_all[..., 2 * col_width :]
     received = padded(border_rows(kv_win, border), (("space", 0),), border)
     kv_ext = extend_windows(kv_win, received, border)
 
     key_index = jnp.concatenate(
         [border + jnp.arange(windows_n, dtype=jnp.int32)[:, None], neighbours], axis=1
     ).reshape(-1)
-    k_ext = kv_ext[..., :col_width]
-    v_ext = kv_ext[..., col_width:]
-    out_slots, grad_query_blocks, dk_ext, dv_ext = window_attention(
-        key_index, length_ext, query_win, k_ext, v_ext, grad_win
-    )
-    grad_ext = jnp.concatenate([dk_ext, dv_ext], axis=-1)
+    dq_out, grad_ext = window_attention(key_index, length_ext, qg_win, kv_ext)
     received_grads = padded(
         border_rows(grad_ext, border).astype(jnp.bfloat16), (("space", 0),), border
     ).astype(jnp.float32)
@@ -212,14 +214,15 @@
     own_grads = own_grads.at[:border].add(received_grads[:border])
     own_grads = own_grads.at[windows_n - border :].add(received_grads[3 * border :])
     slot_vals = jnp.concatenate(
-        [out_slots, grad_query_blocks, own_grads.astype(jnp.bfloat16)], axis=-1
+        [dq_out, own_grads.astype(jnp.bfloat16)], axis=-1
     )
     vox = to_voxels(slot_vals).reshape(seq_n, rows, 4 * col_width)
     back = lax.all_to_all(vox, "seq", split_axis=0, concat_axis=0, tiled=True)
     back = back.reshape(seq_n, rows, 4, col_width)
-    return tuple(
+    results = [
         jnp.transpose(back[:, :, i], (1, 0, 2)).reshape(rows, seq_n * col_width) for i in range(4)
-    )
+    ]
+    return (results[1], results[0], results[2], results[3])
 
 
 def solution(mesh):

time: 399 us -> 383 us (0.960)
  Pallas kernels: 81.6 us -> 71.6 us
  other arithmetic: 14 us -> 9.46 us
    pallas_call x1, Pallas kernels: 81.6 us -> 71.6 us  [window_attention(): pl.pallas_call(attention_kernel, out_shape=(jax.ShapeDtypeStruct(qg_win.s...]
  transfers between devices with their start and end apart: 5 -> 5, of which waited for: 3 -> 4; matrix products, arithmetic and copies ran while one was open for 7% -> 7% of each run, Pallas kernels for 0% -> 0%
where the time goes in v4:
time: 383 us; the launch traced here: 382 us
  blocking collectives  98.8 us (26%)
  waiting for transfers between devices  92.3 us (24%)
  local copies, waits for them, and re-layouts  82.3 us (21%)
  Pallas kernels  71.6 us (19%)
  starting transfers between devices  26.7 us (7%)
  other arithmetic  9.46 us (2%)
    all_to_all x1, blocking collectives, shards(): back = lax.all_to_all(vox, 'seq', split_axis=0, concat_axis=0, tiled=True)  98.8 us
    all_to_all x1, waiting for transfers between devices, shards(): lax.all_to_all(stacked, 'seq', split_axis=0, concat_axis=0, tiled=True)  75.7 us
    pallas_call x1, Pallas kernels, window_attention(): pl.pallas_call(attention_kernel, out_shape=(jax.ShapeDtypeStruct(qg_win.s...  71.6 us
    gather x3, local copies, waits for them, and re-layouts, gather_rows(): return jnp.take(source, indices, axis=0)  45.2 us
    scatter x1, local copies, waits for them, and re-layouts, shards(): slot_of = jnp.zeros((voxel_count,), jnp.int32).at[flat_slots].set(jnp.ara...  23 us
    ppermute x2, waiting for transfers between devices, padded(): after = lax.ppermute(first, axis, down)  16 us
    all_to_all x1, starting transfers between devices, shards(): lax.all_to_all(stacked, 'seq', split_axis=0, concat_axis=0, tiled=True)  15.9 us
  transfers between devices with their start and end apart: 5, of which 4 were waited for; matrix products, arithmetic and copies ran while one was open for 7% of the time, Pallas kernels for 0%

profile of v4, /device:TPU:57, one launch (start us, length us, event | category | flops | bytes accessed | tf_op | source)
XLA Modules:
  0.0 382.2 jit_solution(1855696810478192421)
XLA Ops:
  0.7 1.4 copy.22
  2.1 1.3 copy.24
  3.4 0.3 copy.25
  3.7 0.3 copy.23
  3.9 0.3 pad_maximum_fusion.1
  4.2 1.5 copy.26
  5.7 15.9 %all-to-all-start = ((bf16[32,128,256]{1,2,0:T(8,128)(2,1)}), bf16[32,128,256]{1,2,0:T(8,128)(2,1)}, u32[]{:S(2)}, u32[]{:S(2)}) async-start(bf16[32,128,256]{1,2,0:T(8,128)(2,1)} %bitcast.17), calls=%async_computation | async-start | bytes 4194304 | tf_op jit(solution)/shard_map/all_to_all | solution.py:183
  21.6 0.8 constant_dynamic-slice_fusion.1
  23.4 23.0 %scatter_custom_fusion = s32[4096]{0:T(1024)S(1)} fusion(s32[6144]{0:T(1024)S(1)} %bitcast.69, s32[6144]{0:T(1024)S(1)} %iota.20, s32[]{:T(128)} %constant.101.clone.1), kind=kCustom, calls=%fused_computation.25 | custom fusion | bytes 16388 | tf_op jit(solution)/shard_map/scatter | solution.py:190
  46.6 75.7 %all-to-all-done = bf16[32,128,256]{1,2,0:T(8,128)(2,1)} async-done(((bf16[32,128,256]{1,2,0:T(8,128)(2,1)}), bf16[32,128,256]{1,2,0:T(8,128)(2,1)}, u32[]{:S(2)}, u32[]{:S(2)}) %all-to-all-start) | async-done | bytes 2097184 | tf_op jit(solution)/shard_map/all_to_all | solution.py:183
  122.2 3.3 copy.27
  125.5 25.0 %gather_fusion = bf16[6144,256]{1,0:T(8,128)(2,1)} fusion(bf16[4096,256]{1,0:T(8,128)(2,1)S(1)} %bitcast.56, s32[6144]{0:T(1024)S(1)} %broadcast_clamp_fusion), kind=kCustom, calls=%fused_computation | custom fusion | bytes 6316032 | tf_op jit(solution)/shard_map/jit(_take)/gather | solution.py:29
  150.5 3.2 broadcast_select_fusion
  153.8 4.6 %collective-permute-start = (bf16[16,64,128]{2,1,0:T(8,128)(2,1)S(1)}, bf16[16,64,128]{2,1,0:T(8,128)(2,1)S(1)}, u32[]{:S(2)}, u32[]{:S(2)}) collective-permute-start(bf16[16,64,128]{2,1,0:T(8,128)(2,1)S(1)} %get-tuple-element.36), channel_id=1, source_target_pairs={{0,32},{32,64},{64,96},{96,128},{128,160},{160,192},{192,224},{224... | collective-permute-start | bytes 786440 | tf_op jit(solution)/shard_map/ppermute | solution.py:22
  158.3 1.9 collective-permute-start.1
  160.3 1.3 fusion.9
  161.6 8.0 %collective-permute-done.1 = bf16[16,64,128]{2,1,0:T(8,128)(2,1)S(1)} collective-permute-done((bf16[16,64,128]{2,1,0:T(8,128)(2,1)S(1)}, bf16[16,64,128]{2,1,0:T(8,128)(2,1)S(1)}, u32[]{:S(2)}, u32[]{:S(2)}) %collective-permute-start.1) | collective-permute-done | bytes 262176 | tf_op jit(solution)/shard_map/ppermute | solution.py:23
  169.9 71.6 %shard_map.102 = (bf16[96,64,128]{2,1,0:T(8,128)(2,1)S(1)}, f32[128,64,128]{2,1,0:T(8,128)}) custom-call(s32[576]{0:T(1024)S(1)} %reshape.202.idx_ref, s32[128]{0:T(128)S(1)} %pad_add_fusion.1.len_ref, bf16[96,64,128]{2,1,0:T(8,128)(2,1)S(1)} %get-tuple-element.39.qg_ref, bf16[128,64,128]{2,1,0:T(8,128)(2,1)S(1)} %pad_maximum_fusion.2.kv_ref), custom_call_target="tpu_custom_call" | custom-call | flops 3623878656 | bytes 8388608 | tf_op jit(solution)/shard_map/pallas_call | solution.py:135
  241.5 2.8 convert.6
  244.4 1.9 collective-permute-start.2
  246.4 2.4 collective-permute-start.3
  249.0 0.6 collective-permute-done.2
  249.7 8.0 %collective-permute-done.3 = bf16[16,64,128]{2,1,0:T(8,128)(2,1)S(1)} collective-permute-done((bf16[16,64,128]{2,1,0:T(8,128)(2,1)S(1)}, bf16[16,64,128]{2,1,0:T(8,128)(2,1)S(1)}, u32[]{:S(2)}, u32[]{:S(2)}) %collective-permute-start.3) | collective-permute-done | bytes 262176 | tf_op jit(solution)/shard_map/ppermute | solution.py:23
  257.9 0.3 convert_element_type.9
  258.2 0.6 pad_maximum_fusion
  258.8 17.0 %gather_fusion.1 = bf16[4096,256]{1,0:T(8,128)(2,1)} fusion(bf16[6144,256]{1,0:T(8,128)(2,1)S(1)} %bitcast.57, s32[4096]{0:T(1024)S(1)} %fusion.2), kind=kCustom, calls=%fused_computation.1 | custom fusion | bytes 4210688 | tf_op jit(solution)/shard_map/jit(_take)/gather | solution.py:29
  275.8 3.2 copy.29
  279.2 98.8 %all_to_all.10 = bf16[32,128,256]{1,2,0:T(8,128)(2,1)S(1)} all-to-all(bf16[32,128,256]{1,2,0:T(8,128)(2,1)S(1)} %broadcast_select_fusion.1), channel_id=1, replica_groups=mesh['space'=16,'seq'=32] {'seq'}, dimensions={0} | all-to-all | bytes 4194304 | tf_op jit(solution)/shard_map/all_to_all | solution.py:220
  378.2 1.0 copy.33
  379.2 1.0 copy.32
  380.2 1.0 copy.31
  381.2 1.0 copy.30
  (40 shorter events, 2.3 us)
Async XLA Ops:
  0.6 2.7 copy-start.1
  0.6 3.0 copy-start.2
  5.7 16.8 %copy-start.3 = (s32[96,64]{0,1:T(8,128)S(1)}, s32[96,64]{0,1:T(8,128)}, u32[]{:S(2)}) copy-start(s32[96,64]{0,1:T(8,128)} %param.16) | copy-start | bytes 73732
  5.7 17.0 %copy-start.4 = (s32[96,5]{0,1:T(8,128)S(1)}, s32[96,5]{0,1:T(8,128)}, u32[]{:S(2)}) copy-start(s32[96,5]{0,1:T(8,128)} %param.17) | copy-start | bytes 5764
  5.7 116.5 %all-to-all-start = ((bf16[32,128,256]{1,2,0:T(8,128)(2,1)}), bf16[32,128,256]{1,2,0:T(8,128)(2,1)}, u32[]{:S(2)}, u32[]{:S(2)}) async-start(bf16[32,128,256]{1,2,0:T(8,128)(2,1)} %bitcast.17), calls=%async_computation | async-start | bytes 4194304 | tf_op jit(solution)/shard_map/all_to_all | solution.py:183
  153.8 7.9 %collective-permute-start = (bf16[16,64,128]{2,1,0:T(8,128)(2,1)S(1)}, bf16[16,64,128]{2,1,0:T(8,128)(2,1)S(1)}, u32[]{:S(2)}, u32[]{:S(2)}) collective-permute-start(bf16[16,64,128]{2,1,0:T(8,128)(2,1)S(1)} %get-tuple-element.36), channel_id=1, source_target_pairs={{0,32},{32,64},{64,96},{96,128},{128,160},{160,192},{192,224},{224... | collective-permute-start | bytes 786440 | tf_op jit(solution)/shard_map/ppermute | solution.py:22
  158.3 11.3 %collective-permute-start.1 = (bf16[16,64,128]{2,1,0:T(8,128)(2,1)S(1)}, bf16[16,64,128]{2,1,0:T(8,128)(2,1)S(1)}, u32[]{:S(2)}, u32[]{:S(2)}) collective-permute-start(bf16[16,64,128]{2,1,0:T(8,128)(2,1)S(1)} %get-tuple-element.37), channel_id=1, source_target_pairs={{32,0},{64,32},{96,64},{128,96},{160,128},{192,160},{224,192},{256... | collective-permute-start | bytes 786440 | tf_op jit(solution)/shard_map/ppermute | solution.py:23
  241.5 7.3 %copy-start = (f32[128,64,128]{2,1,0:T(8,128)S(1)}, f32[128,64,128]{2,1,0:T(8,128)}, u32[]{:S(2)}) copy-start(f32[128,64,128]{2,1,0:T(8,128)} %get-tuple-element.31) | copy-start | bytes 12582916
  244.4 5.2 %collective-permute-start.2 = (bf16[16,64,128]{2,1,0:T(8,128)(2,1)S(1)}, bf16[16,64,128]{2,1,0:T(8,128)(2,1)S(1)}, u32[]{:S(2)}, u32[]{:S(2)}) collective-permute-start(bf16[16,64,128]{2,1,0:T(8,128)(2,1)S(1)} %get-tuple-element.44), channel_id=1, source_target_pairs={{0,32},{32,64},{64,96},{96,128},{128,160},{160,192},{192,224},{224... | collective-permute-start | bytes 786440 | tf_op jit(solution)/shard_map/ppermute | solution.py:22
  246.4 11.3 %collective-permute-start.3 = (bf16[16,64,128]{2,1,0:T(8,128)(2,1)S(1)}, bf16[16,64,128]{2,1,0:T(8,128)(2,1)S(1)}, u32[]{:S(2)}, u32[]{:S(2)}) collective-permute-start(bf16[16,64,128]{2,1,0:T(8,128)(2,1)S(1)} %get-tuple-element.45), channel_id=1, source_target_pairs={{32,0},{64,32},{96,64},{128,96},{160,128},{192,160},{224,192},{256... | collective-permute-start | bytes 786440 | tf_op jit(solution)/shard_map/ppermute | solution.py:23

commit v5 on v4

--- a/solution.py
+++ b/solution.py
@@ -74,8 +74,9 @@
     return (attn_probs, query_heads, key_heads, value_heads, score_scale)
 
 
-def attention_kernel(idx_ref, len_ref, qg_ref, kv_ref, out_ref, dkv_ref):
-    windows_n, _, lanes = qg_ref.shape
+def attention_kernel(idx_ref, len_ref, win_ref, kv_ref, out_ref, dkv_ref):
+    windows_n = win_ref.shape[0]
+    lanes = kv_ref.shape[-1]
     width = lanes // 2
     nb = idx_ref.shape[0] // windows_n
     keys = nb * WIN
@@ -86,15 +87,17 @@
     col_slot = col % WIN
     lane = lax.broadcasted_iota(jnp.int32, (1, lanes), 1)
     first_half = lane < width
+    slot_row = lax.broadcasted_iota(jnp.int32, (WIN, 1), 0)
     nt = (((1,), (1,)), ((), ()))
     tn = (((0,), (0,)), ((), ()))
 
     def body(w, carry):
         ids = [idx_ref[w * nb + j] for j in range(nb)]
-        qg = qg_ref[w]
+        qg = win_ref[w, :, :lanes]
         zero = jnp.zeros_like(qg)
         q_pad = jnp.where(first_half, qg, zero)
-        g_pad = jnp.where(first_half, zero, qg)
+        g_live = jnp.logical_and(jnp.logical_not(first_half), slot_row < len_ref[ids[0]])
+        g_pad = jnp.where(g_live, qg, zero)
         qg_blocks = jnp.concatenate([q_pad, g_pad], axis=0)
         kv_all = jnp.concatenate([kv_ref[i] for i in ids], axis=0)
         limit = jnp.zeros((1, keys), jnp.int32)
@@ -122,11 +125,12 @@
             dkv_ref[ids[j]] += grad_kv[j * WIN : (j + 1) * WIN]
         return carry
 
-    lax.fori_loop(0, windows_n, body, 0, unroll=2)
-
-
-def window_attention(key_index, length_ext, qg_win, kv_ext):
-    windows_n, _, lanes = qg_win.shape
+    lax.fori_loop(0, windows_n, body, 0, unroll=8)
+
+
+def window_attention(key_index, length_ext, win_all, kv_ext):
+    windows_n = win_all.shape[0]
+    lanes = kv_ext.shape[-1]
     ext_n = kv_ext.shape[0]
     keys = (key_index.shape[0] // windows_n) * WIN
     flops = 2 * windows_n * WIN * keys * lanes * 6
@@ -135,7 +139,7 @@
     return pl.pallas_call(
         attention_kernel,
         out_shape=(
-            jax.ShapeDtypeStruct(qg_win.shape, jnp.bfloat16),
+            jax.ShapeDtypeStruct((windows_n, WIN, lanes), jnp.bfloat16),
             jax.ShapeDtypeStruct((ext_n, WIN, lanes), jnp.float32),
         ),
         in_specs=[smem, smem, vmem, vmem],
@@ -144,7 +148,7 @@
         cost_estimate=pl.CostEstimate(
             flops=flops, transcendentals=windows_n * WIN * keys, bytes_accessed=8 * 1024 * 1024
         ),
-    )(key_index, length_ext, qg_win, kv_ext)
+    )(key_index, length_ext, win_all, kv_ext)
 
 
 def shards(query_feats, key_feats, value_feats, grad_output, lengths, members, neighbours):
@@ -194,11 +198,6 @@
         return gather_rows(slot_vals.reshape(windows_n * WIN, -1), slot_of)
 
     win_all = gather_rows(table, members)
-    lane_live = jnp.logical_or(
-        jnp.arange(2 * col_width, dtype=jnp.int32)[None, None, :] < col_width,
-        slot_alive[:, :, None],
-    )
-    qg_win = win_all[..., : 2 * col_width] * lane_live.astype(jnp.bfloat16)
     kv_win = win_all[..., 2 * col_width :]
     received = padded(border_rows(kv_win, border), (("space", 0),), border)
     kv_ext = extend_windows(kv_win, received, border)
@@ -206,7 +205,7 @@
     key_index = jnp.concatenate(
         [border + jnp.arange(windows_n, dtype=jnp.int32)[:, None], neighbours], axis=1
     ).reshape(-1)
-    dq_out, grad_ext = window_attention(key_index, length_ext, qg_win, kv_ext)
+    dq_out, grad_ext = window_attention(key_index, length_ext, win_all, kv_ext)
     received_grads = padded(
         border_rows(grad_ext, border).astype(jnp.bfloat16), (("space", 0),), border
     ).astype(jnp.float32)

time: 383 us -> 377 us (0.984)
  Pallas kernels: 71.6 us -> 65.4 us
    pallas_call x1, Pallas kernels: 71.6 us -> 65.4 us  [window_attention(): pl.pallas_call(attention_kernel, out_shape=(jax.ShapeDtypeStruct((windows...]
  transfers between devices with their start and end apart: 5 -> 5, of which waited for: 4 -> 5; matrix products, arithmetic and copies ran while one was open for 7% -> 7% of each run, Pallas kernels for 0% -> 0%
where the time goes in v5:
time: 377 us; the launch traced here: 376 us
  blocking collectives  98.8 us (26%)
  waiting for transfers between devices  93.4 us (25%)
  local copies, waits for them, and re-layouts  82.6 us (22%)
  Pallas kernels  65.4 us (17%)
  starting transfers between devices  26.7 us (7%)
  other arithmetic  8.13 us (2%)
    all_to_all x1, blocking collectives, shards(): back = lax.all_to_all(vox, 'seq', split_axis=0, concat_axis=0, tiled=True)  98.8 us
    all_to_all x1, waiting for transfers between devices, shards(): lax.all_to_all(stacked, 'seq', split_axis=0, concat_axis=0, tiled=True)  75.9 us
    pallas_call x1, Pallas kernels, window_attention(): pl.pallas_call(attention_kernel, out_shape=(jax.ShapeDtypeStruct((windows...  65.4 us
    gather x3, local copies, waits for them, and re-layouts, gather_rows(): return jnp.take(source, indices, axis=0)  45.2 us
    scatter x1, local copies, waits for them, and re-layouts, shards(): slot_of = jnp.zeros((voxel_count,), jnp.int32).at[flat_slots].set(jnp.ara...  23 us
    ppermute x2, waiting for transfers between devices, padded(): after = lax.ppermute(first, axis, down)  16 us
    all_to_all x1, starting transfers between devices, shards(): lax.all_to_all(stacked, 'seq', split_axis=0, concat_axis=0, tiled=True)  15.9 us
  transfers between devices with their start and end apart: 5, of which 5 were waited for; matrix products, arithmetic and copies ran while one was open for 7% of the time, Pallas kernels for 0%

profile of v5, /device:TPU:57, one launch (start us, length us, event | category | flops | bytes accessed | tf_op | source)
XLA Modules:
  0.0 376.0 jit_solution(3282352952772360792)
XLA Ops:
  0.7 1.4 copy.20
  2.1 1.3 copy.22
  3.4 0.3 copy.23
  3.7 0.3 copy.21
  4.2 1.5 copy.24
  5.7 15.9 %all-to-all-start = ((bf16[32,128,256]{1,2,0:T(8,128)(2,1)}), bf16[32,128,256]{1,2,0:T(8,128)(2,1)}, u32[]{:S(2)}, u32[]{:S(2)}) async-start(bf16[32,128,256]{1,2,0:T(8,128)(2,1)} %bitcast.17), calls=%async_computation | async-start | bytes 4194304 | tf_op jit(solution)/shard_map/all_to_all | solution.py:187
  22.1 0.8 constant_dynamic-slice_fusion.1
  23.3 23.0 %scatter_custom_fusion = s32[4096]{0:T(1024)S(1)} fusion(s32[6144]{0:T(1024)S(1)} %bitcast.69, s32[6144]{0:T(1024)S(1)} %iota.11, s32[]{:T(128)} %constant.99.clone.1), kind=kCustom, calls=%fused_computation.24 | custom fusion | bytes 16388 | tf_op jit(solution)/shard_map/scatter | solution.py:194
  46.3 75.9 %all-to-all-done = bf16[32,128,256]{1,2,0:T(8,128)(2,1)} async-done(((bf16[32,128,256]{1,2,0:T(8,128)(2,1)}), bf16[32,128,256]{1,2,0:T(8,128)(2,1)}, u32[]{:S(2)}, u32[]{:S(2)}) %all-to-all-start) | async-done | bytes 2097184 | tf_op jit(solution)/shard_map/all_to_all | solution.py:187
  122.2 3.3 copy.25
  125.5 25.0 %gather_fusion = bf16[6144,256]{1,0:T(8,128)(2,1)} fusion(bf16[4096,256]{1,0:T(8,128)(2,1)S(1)} %bitcast.56, s32[6144]{0:T(1024)S(1)} %broadcast_clamp_fusion), kind=kCustom, calls=%fused_computation | custom fusion | bytes 6316032 | tf_op jit(solution)/shard_map/jit(_take)/gather | solution.py:29
  150.5 3.2 broadcast_select_fusion.win_ref
  153.8 4.6 %collective-permute-start = (bf16[16,64,128]{2,1,0:T(8,128)(2,1)S(1)}, bf16[16,64,128]{2,1,0:T(8,128)(2,1)S(1)}, u32[]{:S(2)}, u32[]{:S(2)}) collective-permute-start(bf16[16,64,128]{2,1,0:T(8,128)(2,1)S(1)} %get-tuple-element.36), channel_id=1, source_target_pairs={{0,32},{32,64},{64,96},{96,128},{128,160},{160,192},{192,224},{224... | collective-permute-start | bytes 786440 | tf_op jit(solution)/shard_map/ppermute | solution.py:22
  158.3 1.9 collective-permute-start.1
  160.4 0.3 slice.120
  160.8 0.9 collective-permute-done
  161.6 8.0 %collective-permute-done.1 = bf16[16,64,128]{2,1,0:T(8,128)(2,1)S(1)} collective-permute-done((bf16[16,64,128]{2,1,0:T(8,128)(2,1)S(1)}, bf16[16,64,128]{2,1,0:T(8,128)(2,1)S(1)}, u32[]{:S(2)}, u32[]{:S(2)}) %collective-permute-start.1) | collective-permute-done | bytes 262176 | tf_op jit(solution)/shard_map/ppermute | solution.py:23
  169.9 65.4 %shard_map.102 = (bf16[96,64,128]{2,1,0:T(8,128)(2,1)S(1)}, f32[128,64,128]{2,1,0:T(8,128)}) custom-call(s32[576]{0:T(1024)S(1)} %reshape.174.idx_ref, s32[128]{0:T(128)S(1)} %pad_add_fusion.1.len_ref, bf16[96,64,256]{2,1,0:T(8,128)(2,1)} %copy-done.1, bf16[128,64,128]{2,1,0:T(8,128)(2,1)S(1)} %pad_maximum_fusion.2.kv_ref), custom_call_target="tpu_custom_call" | custom-call | flops 3623878656 | bytes 8388608 | tf_op jit(solution)/shard_map/pallas_call | solution.py:139
  235.3 2.8 convert.6
  238.2 1.9 collective-permute-start.2
  240.1 2.4 collective-permute-start.3
  242.8 0.6 collective-permute-done.2
  243.4 8.0 %collective-permute-done.3 = bf16[16,64,128]{2,1,0:T(8,128)(2,1)S(1)} collective-permute-done((bf16[16,64,128]{2,1,0:T(8,128)(2,1)S(1)}, bf16[16,64,128]{2,1,0:T(8,128)(2,1)S(1)}, u32[]{:S(2)}, u32[]{:S(2)}) %collective-permute-start.3) | collective-permute-done | bytes 262176 | tf_op jit(solution)/shard_map/ppermute | solution.py:23
  251.6 0.3 convert_element_type.8
  252.0 0.6 pad_maximum_fusion
  252.6 17.0 %gather_fusion.1 = bf16[4096,256]{1,0:T(8,128)(2,1)} fusion(bf16[6144,256]{1,0:T(8,128)(2,1)S(1)} %bitcast.57, s32[4096]{0:T(1024)S(1)} %fusion.3), kind=kCustom, calls=%fused_computation.1 | custom fusion | bytes 4210688 | tf_op jit(solution)/shard_map/jit(_take)/gather | solution.py:29
  269.6 3.2 copy.27
  273.0 98.8 %all_to_all.10 = bf16[32,128,256]{1,2,0:T(8,128)(2,1)S(1)} all-to-all(bf16[32,128,256]{1,2,0:T(8,128)(2,1)S(1)} %broadcast_select_fusion.1), channel_id=1, replica_groups=mesh['space'=16,'seq'=32] {'seq'}, dimensions={0} | all-to-all | bytes 4194304 | tf_op jit(solution)/shard_map/all_to_all | solution.py:219
  372.0 1.0 copy.31
  373.0 1.0 copy.30
  374.0 1.0 copy.29
  375.0 1.0 copy.28
  (39 shorter events, 2.4 us)
Async XLA Ops:
  0.6 2.7 copy-start.2
  0.6 3.0 copy-start.3
  5.7 15.9 %copy-start.4 = (s32[96,64]{0,1:T(8,128)S(1)}, s32[96,64]{0,1:T(8,128)}, u32[]{:S(2)}) copy-start(s32[96,64]{0,1:T(8,128)} %param.16) | copy-start | bytes 73732
  5.7 16.1 %copy-start.5 = (s32[96,5]{0,1:T(8,128)S(1)}, s32[96,5]{0,1:T(8,128)}, u32[]{:S(2)}) copy-start(s32[96,5]{0,1:T(8,128)} %param.17) | copy-start | bytes 5764
  5.7 116.5 %all-to-all-start = ((bf16[32,128,256]{1,2,0:T(8,128)(2,1)}), bf16[32,128,256]{1,2,0:T(8,128)(2,1)}, u32[]{:S(2)}, u32[]{:S(2)}) async-start(bf16[32,128,256]{1,2,0:T(8,128)(2,1)} %bitcast.17), calls=%async_computation | async-start | bytes 4194304 | tf_op jit(solution)/shard_map/all_to_all | solution.py:187
  153.7 7.1 %copy-start.1 = (bf16[96,64,256]{2,1,0:T(8,128)(2,1)}, bf16[96,64,256]{2,1,0:T(8,128)(2,1)S(1)}, u32[]{:S(2)}) copy-start(bf16[96,64,256]{2,1,0:T(8,128)(2,1)S(1)} %broadcast_select_fusion.win_ref) | copy-start | bytes 9437188
  153.8 7.9 %collective-permute-start = (bf16[16,64,128]{2,1,0:T(8,128)(2,1)S(1)}, bf16[16,64,128]{2,1,0:T(8,128)(2,1)S(1)}, u32[]{:S(2)}, u32[]{:S(2)}) collective-permute-start(bf16[16,64,128]{2,1,0:T(8,128)(2,1)S(1)} %get-tuple-element.36), channel_id=1, source_target_pairs={{0,32},{32,64},{64,96},{96,128},{128,160},{160,192},{192,224},{224... | collective-permute-start | bytes 786440 | tf_op jit(solution)/shard_map/ppermute | solution.py:22
  158.3 11.3 %collective-permute-start.1 = (bf16[16,64,128]{2,1,0:T(8,128)(2,1)S(1)}, bf16[16,64,128]{2,1,0:T(8,128)(2,1)S(1)}, u32[]{:S(2)}, u32[]{:S(2)}) collective-permute-start(bf16[16,64,128]{2,1,0:T(8,128)(2,1)S(1)} %get-tuple-element.37), channel_id=1, source_target_pairs={{32,0},{64,32},{96,64},{128,96},{160,128},{192,160},{224,192},{256... | collective-permute-start | bytes 786440 | tf_op jit(solution)/shard_map/ppermute | solution.py:23
  235.3 7.3 %copy-start = (f32[128,64,128]{2,1,0:T(8,128)S(1)}, f32[128,64,128]{2,1,0:T(8,128)}, u32[]{:S(2)}) copy-start(f32[128,64,128]{2,1,0:T(8,128)} %get-tuple-element.31) | copy-start | bytes 12582916
  238.2 5.2 %collective-permute-start.2 = (bf16[16,64,128]{2,1,0:T(8,128)(2,1)S(1)}, bf16[16,64,128]{2,1,0:T(8,128)(2,1)S(1)}, u32[]{:S(2)}, u32[]{:S(2)}) collective-permute-start(bf16[16,64,128]{2,1,0:T(8,128)(2,1)S(1)} %get-tuple-element.42), channel_id=1, source_target_pairs={{0,32},{32,64},{64,96},{96,128},{128,160},{160,192},{192,224},{224... | collective-permute-start | bytes 786440 | tf_op jit(solution)/shard_map/ppermute | solution.py:22
  240.1 11.3 %collective-permute-start.3 = (bf16[16,64,128]{2,1,0:T(8,128)(2,1)S(1)}, bf16[16,64,128]{2,1,0:T(8,128)(2,1)S(1)}, u32[]{:S(2)}, u32[]{:S(2)}) collective-permute-start(bf16[16,64,128]{2,1,0:T(8,128)(2,1)S(1)} %get-tuple-element.43), channel_id=1, source_target_pairs={{32,0},{64,32},{96,64},{128,96},{160,128},{192,160},{224,192},{256... | collective-permute-start | bytes 786440 | tf_op jit(solution)/shard_map/ppermute | solution.py:23

commit v6 on v5

--- a/solution.py
+++ b/solution.py
@@ -1,3 +1,5 @@
+import functools
+
 import jax
 import jax.numpy as jnp
 from jax import lax
@@ -74,14 +76,19 @@
     return (attn_probs, query_heads, key_heads, value_heads, score_scale)
 
 
-def attention_kernel(idx_ref, len_ref, win_ref, kv_ref, out_ref, dkv_ref):
+def attention_kernel(ranges, kv_offset, fresh, idx_ref, len_ref, win_ref, kv_ref, *refs):
+    out_ref, dkv_ref = refs[-2:]
     windows_n = win_ref.shape[0]
     lanes = kv_ref.shape[-1]
     width = lanes // 2
     nb = idx_ref.shape[0] // windows_n
     keys = nb * WIN
     scale = HEAD ** (-0.5)
-    dkv_ref[...] = jnp.zeros(dkv_ref.shape, dkv_ref.dtype)
+    if fresh:
+        dkv_ref[...] = jnp.zeros(dkv_ref.shape, dkv_ref.dtype)
+    else:
+        out_ref[...] = refs[0][...]
+        dkv_ref[...] = refs[1][...]
     col = lax.broadcasted_iota(jnp.int32, (1, keys), 1)
     col_block = col // WIN
     col_slot = col % WIN
@@ -99,7 +106,7 @@
         g_live = jnp.logical_and(jnp.logical_not(first_half), slot_row < len_ref[ids[0]])
         g_pad = jnp.where(g_live, qg, zero)
         qg_blocks = jnp.concatenate([q_pad, g_pad], axis=0)
-        kv_all = jnp.concatenate([kv_ref[i] for i in ids], axis=0)
+        kv_all = jnp.concatenate([kv_ref[i - kv_offset] for i in ids], axis=0)
         limit = jnp.zeros((1, keys), jnp.int32)
         for j in range(nb):
             limit = jnp.where(col_block == j, len_ref[ids[j]], limit)
@@ -125,30 +132,39 @@
             dkv_ref[ids[j]] += grad_kv[j * WIN : (j + 1) * WIN]
         return carry
 
-    lax.fori_loop(0, windows_n, body, 0, unroll=8)
-
-
-def window_attention(key_index, length_ext, win_all, kv_ext):
+    for start, stop in ranges:
+        lax.fori_loop(start, stop, body, 0, unroll=8)
+
+
+def window_attention(ranges, kv_offset, key_index, length_ext, win_all, kv_part, carried=None):
     windows_n = win_all.shape[0]
-    lanes = kv_ext.shape[-1]
-    ext_n = kv_ext.shape[0]
+    lanes = kv_part.shape[-1]
+    ext_n = length_ext.shape[0]
     keys = (key_index.shape[0] // windows_n) * WIN
-    flops = 2 * windows_n * WIN * keys * lanes * 6
+    count = sum(stop - start for start, stop in ranges)
+    flops = 2 * count * WIN * keys * lanes * 6
     vmem = pl.BlockSpec(memory_space=pltpu.VMEM)
     smem = pl.BlockSpec(memory_space=pltpu.SMEM)
+    operands = [key_index, length_ext, win_all, kv_part]
+    aliases = {}
+    if carried is not None:
+        operands += list(carried)
+        aliases = {4: 0, 5: 1}
+    kernel = functools.partial(attention_kernel, tuple(ranges), kv_offset, carried is None)
     return pl.pallas_call(
-        attention_kernel,
+        kernel,
         out_shape=(
             jax.ShapeDtypeStruct((windows_n, WIN, lanes), jnp.bfloat16),
             jax.ShapeDtypeStruct((ext_n, WIN, lanes), jnp.float32),
         ),
-        in_specs=[smem, smem, vmem, vmem],
+        in_specs=[smem, smem] + [vmem] * (len(operands) - 2),
         out_specs=(vmem, vmem),
+        input_output_aliases=aliases,
         compiler_params=pltpu.CompilerParams(vmem_limit_bytes=48 * 1024 * 1024),
         cost_estimate=pl.CostEstimate(
-            flops=flops, transcendentals=windows_n * WIN * keys, bytes_accessed=8 * 1024 * 1024
+            flops=flops, transcendentals=count * WIN * keys, bytes_accessed=count * 96 * 1024
         ),
-    )(key_index, length_ext, win_all, kv_ext)
+    )(*operands)
 
 
 def shards(query_feats, key_feats, value_feats, grad_output, lengths, members, neighbours):
@@ -205,10 +221,18 @@
     key_index = jnp.concatenate(
         [border + jnp.arange(windows_n, dtype=jnp.int32)[:, None], neighbours], axis=1
     ).reshape(-1)
-    dq_out, grad_ext = window_attention(key_index, length_ext, win_all, kv_ext)
-    received_grads = padded(
-        border_rows(grad_ext, border).astype(jnp.bfloat16), (("space", 0),), border
-    ).astype(jnp.float32)
+    kv_own = win_all[..., 2 * col_width :]
+    middle = windows_n - 2 * border
+    first_part = [(border, border + middle // 2)]
+    rim_part = [(0, border), (windows_n - border, windows_n)]
+    last_part = [(border + middle // 2, windows_n - border)]
+    carried = window_attention(first_part, border, key_index, length_ext, win_all, kv_own)
+    carried = window_attention(rim_part, 0, key_index, length_ext, win_all, kv_ext, carried)
+    rim_grads = border_rows(carried[1], border).astype(jnp.bfloat16)
+    dq_out, grad_ext = window_attention(
+        last_part, border, key_index, length_ext, win_all, kv_own, carried
+    )
+    received_grads = padded(rim_grads, (("space", 0),), border).astype(jnp.float32)
     own_grads = grad_ext[border : border + windows_n]
     own_grads = own_grads.at[:border].add(received_grads[:border])
     own_grads = own_grads.at[windows_n - border :].add(received_grads[3 * border :])

time: 377 us -> 383 us (1.016)
  the two profiles are of different devices: /device:TPU:57 before, /device:TPU:36 now
where the time goes in v6:
time: 383 us
  blocking collectives  98.6 us (26%)
  local copies, waits for them, and re-layouts  85.5 us (22%)
  Pallas kernels  77 us (20%)
  waiting for transfers between devices  75.6 us (20%)
  starting transfers between devices  34.9 us (9%)
  other arithmetic  9.96 us (3%)
    all_to_all x1, blocking collectives, shards(): back = lax.all_to_all(vox, 'seq', split_axis=0, concat_axis=0, tiled=True)  98.6 us
    pallas_call x3, Pallas kernels, window_attention(): pl.pallas_call(kernel, out_shape=(jax.ShapeDtypeStruct((windows_n, WIN, l...  77 us
    all_to_all x1, waiting for transfers between devices, shards(): lax.all_to_all(stacked, 'seq', split_axis=0, concat_axis=0, tiled=True)  75.6 us
    gather x3, local copies, waits for them, and re-layouts, gather_rows(): return jnp.take(source, indices, axis=0)  45.3 us
    scatter x1, local copies, waits for them, and re-layouts, shards(): slot_of = jnp.zeros((voxel_count,), jnp.int32).at[flat_slots].set(jnp.ara...  23 us
    all_to_all x1, starting transfers between devices, shards(): lax.all_to_all(stacked, 'seq', split_axis=0, concat_axis=0, tiled=True)  16.2 us
    ppermute x2, starting transfers between devices, padded(): after = lax.ppermute(first, axis, down)  14.9 us
  transfers between devices with their start and end apart: 5, of which 1 were waited for; matrix products, arithmetic and copies ran while one was open for 7% of the time, Pallas kernels for 13%

profile of v6, /device:TPU:36, one launch (start us, length us, event | category | flops | bytes accessed | tf_op | source)
XLA Modules:
  0.0 382.5 jit_solution(2277964159791114782)
XLA Ops:
  0.7 1.4 copy.24
  2.1 1.3 copy.26
  4.2 1.5 copy.28
  5.7 16.2 %all-to-all-start = ((bf16[32,128,256]{1,2,0:T(8,128)(2,1)}), bf16[32,128,256]{1,2,0:T(8,128)(2,1)}, u32[]{:S(2)}, u32[]{:S(2)}) async-start(bf16[32,128,256]{1,2,0:T(8,128)(2,1)} %bitcast.17), calls=%async_computation | async-start | bytes 4194304 | tf_op jit(solution)/shard_map/all_to_all | solution.py:203
  22.0 0.8 constant_dynamic-slice_fusion.1
  23.2 23.0 %scatter_custom_fusion = s32[4096]{0:T(1024)S(1)} fusion(s32[6144]{0:T(1024)S(1)} %bitcast.69, s32[6144]{0:T(1024)S(1)} %iota.11, s32[]{:T(128)} %constant.99.clone.1), kind=kCustom, calls=%fused_computation.24 | custom fusion | bytes 16388 | tf_op jit(solution)/shard_map/scatter | solution.py:210
  46.3 75.6 %all-to-all-done = bf16[32,128,256]{1,2,0:T(8,128)(2,1)} async-done(((bf16[32,128,256]{1,2,0:T(8,128)(2,1)}), bf16[32,128,256]{1,2,0:T(8,128)(2,1)}, u32[]{:S(2)}, u32[]{:S(2)}) %all-to-all-start) | async-done | bytes 2097184 | tf_op jit(solution)/shard_map/all_to_all | solution.py:203
  121.9 3.3 copy.29
  125.2 25.1 %gather_fusion = bf16[6144,256]{1,0:T(8,128)(2,1)} fusion(bf16[4096,256]{1,0:T(8,128)(2,1)S(1)} %bitcast.56, s32[6144]{0:T(1024)S(1)} %broadcast_clamp_fusion), kind=kCustom, calls=%fused_computation | custom fusion | bytes 6316032 | tf_op jit(solution)/shard_map/jit(_take)/gather | solution.py:31
  150.2 3.2 broadcast_select_fusion.win_ref
  153.5 1.0 fusion.9
  154.5 1.9 collective-permute-start
  156.4 7.4 %collective-permute-start.1 = (bf16[16,64,128]{2,1,0:T(8,128)(2,1)}, bf16[16,64,128]{2,1,0:T(8,128)(2,1)}, u32[]{:S(2)}, u32[]{:S(2)}) collective-permute-start(bf16[16,64,128]{2,1,0:T(8,128)(2,1)} %get-tuple-element.45), channel_id=1, source_target_pairs={{32,0},{64,32},{96,64},{128,96},{160,128},{192,160},{224,192},{256... | collective-permute-start | bytes 786440 | tf_op jit(solution)/shard_map/ppermute | solution.py:25
  164.2 0.3 slice.120.kv_ref
  164.5 24.6 %shard_map.102 = (bf16[96,64,128]{2,1,0:T(8,128)(2,1)S(1)}, f32[128,64,128]{2,1,0:T(8,128)}) custom-call(s32[576]{0:T(1024)S(1)} %reshape.174.idx_ref, s32[128]{0:T(128)S(1)} %pad_add_fusion.1.len_ref, bf16[96,64,256]{2,1,0:T(8,128)(2,1)} %copy-done, bf16[96,64,128]{2,1,0:T(8,128)(2,1)S(1)} %slice.120.kv_ref), custom_call_target="tpu_custom_call" | custom-call | flops 1207959552 | bytes 3145728 | tf_op jit(solution)/shard_map/pallas_call | solution.py:154
  189.1 1.2 pad_maximum_fusion.2.kv_ref
  190.3 26.2 %shard_map.103 = (bf16[96,64,128]{2,1,0:T(8,128)(2,1)S(1)}, f32[128,64,128]{2,1,0:T(8,128)}) custom-call(s32[576]{0:T(1024)S(1)} %reshape.174.idx_ref, s32[128]{0:T(128)S(1)} %pad_add_fusion.1.len_ref, bf16[96,64,256]{2,1,0:T(8,128)(2,1)} %copy-done, ...), custom_call_target="tpu_custom_call", output_to_operand_aliasing={{0}: (4, {}), {1}: (5, {})} | custom-call | flops 1207959552 | bytes 3145728 | tf_op jit(solution)/shard_map/pallas_call | solution.py:154
  216.5 2.7 convert.6
  219.2 1.9 collective-permute-start.2
  221.1 7.5 %collective-permute-start.3 = (bf16[16,64,128]{2,1,0:T(8,128)(2,1)S(1)}, bf16[16,64,128]{2,1,0:T(8,128)(2,1)S(1)}, u32[]{:S(2)}, u32[]{:S(2)}) collective-permute-start(bf16[16,64,128]{2,1,0:T(8,128)(2,1)S(1)} %get-tuple-element.51), channel_id=1, source_target_pairs={{32,0},{64,32},{96,64},{128,96},{160,128},{192,160},{224,192},{256... | collective-permute-start | bytes 786440 | tf_op jit(solution)/shard_map/ppermute | solution.py:25
  228.6 26.2 %shard_map.104 = (bf16[96,64,128]{2,1,0:T(8,128)(2,1)S(1)}, f32[128,64,128]{2,1,0:T(8,128)}) custom-call(s32[576]{0:T(1024)S(1)} %reshape.174.idx_ref, s32[128]{0:T(128)S(1)} %pad_add_fusion.1.len_ref, bf16[96,64,256]{2,1,0:T(8,128)(2,1)} %copy-done, bf16[96,64,128]{2,1,0:T(8,128)(2,1)S(1)} %slice.120.kv_ref, ...), custom_call_target="tpu_custom_call", output_to_operand_aliasing={{0}: (4, {}), {1}: (5, {})} | custom-call | flops 1207959552 | bytes 3145728 | tf_op jit(solution)/shard_map/pallas_call | solution.py:154
  254.8 2.1 slice.105
  257.0 1.1 fusion.1
  258.2 0.3 convert_element_type.8
  258.6 0.6 pad_maximum_fusion
  259.2 17.0 %gather_fusion.1 = bf16[4096,256]{1,0:T(8,128)(2,1)} fusion(bf16[6144,256]{1,0:T(8,128)(2,1)S(1)} %bitcast.57, s32[4096]{0:T(1024)S(1)} %fusion.3), kind=kCustom, calls=%fused_computation.1 | custom fusion | bytes 4210688 | tf_op jit(solution)/shard_map/jit(_take)/gather | solution.py:31
  276.2 3.2 copy.31
  279.7 98.6 %all_to_all.10 = bf16[32,128,256]{1,2,0:T(8,128)(2,1)S(1)} all-to-all(bf16[32,128,256]{1,2,0:T(8,128)(2,1)S(1)} %broadcast_select_fusion.1), channel_id=1, replica_groups=mesh['space'=16,'seq'=32] {'seq'}, dimensions={0} | all-to-all | bytes 4194304 | tf_op jit(solution)/shard_map/all_to_all | solution.py:243
  378.5 1.0 copy.35
  379.5 1.0 copy.34
  380.5 1.0 copy.33
  381.5 1.0 copy.32
  (39 shorter events, 2.3 us)
Async XLA Ops:
  0.6 2.7 copy-start.1
  0.6 3.0 copy-start.2
  5.7 16.2 %copy-start.3 = (s32[96,64]{0,1:T(8,128)S(1)}, s32[96,64]{0,1:T(8,128)}, u32[]{:S(2)}) copy-start(s32[96,64]{0,1:T(8,128)} %param.16) | copy-start | bytes 73732
  5.7 116.2 %all-to-all-start = ((bf16[32,128,256]{1,2,0:T(8,128)(2,1)}), bf16[32,128,256]{1,2,0:T(8,128)(2,1)}, u32[]{:S(2)}, u32[]{:S(2)}) async-start(bf16[32,128,256]{1,2,0:T(8,128)(2,1)} %bitcast.17), calls=%async_computation | async-start | bytes 4194304 | tf_op jit(solution)/shard_map/all_to_all | solution.py:203
  150.2 13.6 %copy-start.4 = (s32[96,5]{0,1:T(8,128)S(1)}, s32[96,5]{0,1:T(8,128)}, u32[]{:S(2)}) copy-start(s32[96,5]{0,1:T(8,128)} %param.17) | copy-start | bytes 5764
  153.4 11.1 %copy-start = (bf16[96,64,256]{2,1,0:T(8,128)(2,1)}, bf16[96,64,256]{2,1,0:T(8,128)(2,1)S(1)}, u32[]{:S(2)}) copy-start(bf16[96,64,256]{2,1,0:T(8,128)(2,1)S(1)} %broadcast_select_fusion.win_ref) | copy-start | bytes 9437188
  154.5 34.6 %collective-permute-start = (bf16[16,64,128]{2,1,0:T(8,128)(2,1)}, bf16[16,64,128]{2,1,0:T(8,128)(2,1)S(1)}, u32[]{:S(2)}, u32[]{:S(2)}) collective-permute-start(bf16[16,64,128]{2,1,0:T(8,128)(2,1)} %get-tuple-element.44), channel_id=1, source_target_pairs={{0,32},{32,64},{64,96},{96,128},{128,160},{160,192},{192,224},{224... | collective-permute-start | bytes 786440 | tf_op jit(solution)/shard_map/ppermute | solution.py:24
  156.4 32.7 %collective-permute-start.1 = (bf16[16,64,128]{2,1,0:T(8,128)(2,1)}, bf16[16,64,128]{2,1,0:T(8,128)(2,1)}, u32[]{:S(2)}, u32[]{:S(2)}) collective-permute-start(bf16[16,64,128]{2,1,0:T(8,128)(2,1)} %get-tuple-element.45), channel_id=1, source_target_pairs={{32,0},{64,32},{96,64},{128,96},{160,128},{192,160},{224,192},{256... | collective-permute-start | bytes 786440 | tf_op jit(solution)/shard_map/ppermute | solution.py:25
  219.2 37.8 %collective-permute-start.2 = (bf16[16,64,128]{2,1,0:T(8,128)(2,1)S(1)}, bf16[16,64,128]{2,1,0:T(8,128)(2,1)S(1)}, u32[]{:S(2)}, u32[]{:S(2)}) collective-permute-start(bf16[16,64,128]{2,1,0:T(8,128)(2,1)S(1)} %get-tuple-element.50), channel_id=1, source_target_pairs={{0,32},{32,64},{64,96},{96,128},{128,160},{160,192},{192,224},{224... | collective-permute-start | bytes 786440 | tf_op jit(solution)/shard_map/ppermute | solution.py:24
  221.1 35.8 %collective-permute-start.3 = (bf16[16,64,128]{2,1,0:T(8,128)(2,1)S(1)}, bf16[16,64,128]{2,1,0:T(8,128)(2,1)S(1)}, u32[]{:S(2)}, u32[]{:S(2)}) collective-permute-start(bf16[16,64,128]{2,1,0:T(8,128)(2,1)S(1)} %get-tuple-element.51), channel_id=1, source_target_pairs={{32,0},{64,32},{96,64},{128,96},{160,128},{192,160},{224,192},{256... | collective-permute-start | bytes 786440 | tf_op jit(solution)/shard_map/ppermute | solution.py:25

commit v7 on v5

--- a/solution.py
+++ b/solution.py
@@ -26,7 +26,7 @@
 
 
 def gather_rows(source, indices):
-    return jnp.take(source, indices, axis=0)
+    return source.at[indices].get(mode="promise_in_bounds")
 
 
 def to_windows(query_part, key_part, value_part, members):

time: 377 us -> 399 us (1.058)
  waiting for transfers between devices: 93.4 us -> 107 us
  local copies, waits for them, and re-layouts: 82.6 us -> 87.6 us
    all_to_all x1, waiting for transfers between devices: 75.9 us -> 99.1 us  [shards(): lax.all_to_all(stacked, 'seq', split_axis=0, concat_axis=0, tiled=True)]
    ppermute x2, waiting for transfers between devices: 16 us -> 7.68 us  [padded(): after = lax.ppermute(first, axis, down)]
    gather x3 -> x2, local copies, waits for them, and re-layouts: 45.2 us -> 43 us  [gather_rows(): return source.at[indices].get(mode='promise_in_bounds')]
  transfers between devices with their start and end apart: 5 -> 5, of which waited for: 5 -> 2; matrix products, arithmetic and copies ran while one was open for 7% -> 7% of each run, Pallas kernels for 0% -> 0%
where the time goes in v7:
time: 399 us; the launch traced here: 397 us
  waiting for transfers between devices  107 us (27%)
  blocking collectives  102 us (26%)
  local copies, waits for them, and re-layouts  87.6 us (22%)
  Pallas kernels  65.4 us (16%)
  starting transfers between devices  26.7 us (7%)
  other arithmetic  7.24 us (2%)
    all_to_all x1, blocking collectives, shards(): back = lax.all_to_all(vox, 'seq', split_axis=0, concat_axis=0, tiled=True)  102 us
    all_to_all x1, waiting for transfers between devices, shards(): lax.all_to_all(stacked, 'seq', split_axis=0, concat_axis=0, tiled=True)  99.1 us
    pallas_call x1, Pallas kernels, window_attention(): pl.pallas_call(attention_kernel, out_shape=(jax.ShapeDtypeStruct((windows...  65.4 us
    gather x2, local copies, waits for them, and re-layouts, gather_rows(): return source.at[indices].get(mode='promise_in_bounds')  43 us
    scatter x1, local copies, waits for them, and re-layouts, shards(): slot_of = jnp.zeros((voxel_count,), jnp.int32).at[flat_slots].set(jnp.ara...  23 us
    all_to_all x1, starting transfers between devices, shards(): lax.all_to_all(stacked, 'seq', split_axis=0, concat_axis=0, tiled=True)  15.9 us
  transfers between devices with their start and end apart: 5, of which 2 were waited for; matrix products, arithmetic and copies ran while one was open for 7% of the time, Pallas kernels for 0%

profile of v7, /device:TPU:57, one launch (start us, length us, event | category | flops | bytes accessed | tf_op | source)
XLA Modules:
  0.0 396.9 jit_solution(10410216720461004497)
XLA Ops:
  0.7 1.4 copy.17
  2.1 1.3 copy.19
  3.4 0.3 copy.20
  3.7 0.3 copy.18
  3.9 0.3 pad_maximum_fusion.1
  4.2 1.5 copy.21
  5.7 15.9 %all-to-all-start = ((bf16[32,128,256]{1,2,0:T(8,128)(2,1)}), bf16[32,128,256]{1,2,0:T(8,128)(2,1)}, u32[]{:S(2)}, u32[]{:S(2)}) async-start(bf16[32,128,256]{1,2,0:T(8,128)(2,1)} %bitcast.15), calls=%async_computation | async-start | bytes 4194304 | tf_op jit(solution)/shard_map/all_to_all | solution.py:187
  21.9 0.8 constant_dynamic-slice_fusion.2
  23.1 99.1 %all-to-all-done = bf16[32,128,256]{1,2,0:T(8,128)(2,1)} async-done(((bf16[32,128,256]{1,2,0:T(8,128)(2,1)}), bf16[32,128,256]{1,2,0:T(8,128)(2,1)}, u32[]{:S(2)}, u32[]{:S(2)}) %all-to-all-start) | async-done | bytes 2097184 | tf_op jit(solution)/shard_map/all_to_all | solution.py:187
  122.2 3.3 copy.22
  125.5 24.9 %gather_fusion = bf16[6144,256]{1,0:T(8,128)(2,1)} fusion(bf16[4096,256]{1,0:T(8,128)(2,1)S(1)} %bitcast.54, s32[6144]{0:T(1024)S(1)} %broadcast_clamp_fusion), kind=kCustom, calls=%fused_computation | custom fusion | bytes 6316032 | tf_op jit(solution)/shard_map/gather | solution.py:29
  150.4 1.1 fusion.9
  151.5 4.6 %collective-permute-start = (bf16[16,64,128]{2,1,0:T(8,128)(2,1)S(1)}, bf16[16,64,128]{2,1,0:T(8,128)(2,1)S(1)}, u32[]{:S(2)}, u32[]{:S(2)}) collective-permute-start(bf16[16,64,128]{2,1,0:T(8,128)(2,1)S(1)} %get-tuple-element.36), channel_id=1, source_target_pairs={{0,32},{32,64},{64,96},{96,128},{128,160},{160,192},{192,224},{224... | collective-permute-start | bytes 786440 | tf_op jit(solution)/shard_map/ppermute | solution.py:22
  156.0 1.9 collective-permute-start.1
  158.1 1.5 slice.120
  159.6 7.7 %collective-permute-done.1 = bf16[16,64,128]{2,1,0:T(8,128)(2,1)S(1)} collective-permute-done((bf16[16,64,128]{2,1,0:T(8,128)(2,1)S(1)}, bf16[16,64,128]{2,1,0:T(8,128)(2,1)S(1)}, u32[]{:S(2)}, u32[]{:S(2)}) %collective-permute-start.1) | collective-permute-done | bytes 262176 | tf_op jit(solution)/shard_map/ppermute | solution.py:23
  167.6 65.4 %shard_map.102 = (bf16[96,64,128]{2,1,0:T(8,128)(2,1)S(1)}, f32[128,64,128]{2,1,0:T(8,128)}) custom-call(s32[576]{0:T(1024)S(1)} %reshape.159.idx_ref, s32[128]{0:T(128)S(1)} %pad_add_fusion.1.len_ref, bf16[96,64,256]{2,1,0:T(8,128)(2,1)} %bitcast.58, bf16[128,64,128]{2,1,0:T(8,128)(2,1)S(1)} %pad_maximum_fusion.2.kv_ref), custom_call_target="tpu_custom_call" | custom-call | flops 3623878656 | bytes 8388608 | tf_op jit(solution)/shard_map/pallas_call | solution.py:139
  233.0 2.7 convert.6
  235.7 1.9 collective-permute-start.2
  237.6 2.4 collective-permute-start.3
  240.1 23.0 %scatter_custom_fusion = s32[4096]{0:T(1024)S(1)} fusion(s32[6144]{0:T(1024)S(1)} %bitcast.69, s32[6144]{0:T(1024)S(1)} %iota.12, s32[]{:T(128)} %constant.81.clone.1), kind=kCustom, calls=%fused_computation.20 | custom fusion | bytes 16388 | tf_op jit(solution)/shard_map/scatter | solution.py:194
  263.1 2.1 slice.104
  265.2 1.1 fusion.1
  266.5 0.3 convert_element_type.8
  266.8 2.2 pad_maximum_fusion
  269.1 18.1 %gather_fusion.1 = bf16[4096,256]{1,0:T(8,128)(2,1)} fusion(bf16[6144,256]{1,0:T(8,128)(2,1)} %bitcast.55, s32[4096]{0:T(1024)S(1)} %fusion.3), kind=kCustom, calls=%fused_computation.1 | custom fusion | bytes 4210688 | tf_op jit(solution)/shard_map/gather | solution.py:29
  287.2 3.2 copy.25
  290.4 102.2 %all_to_all.10 = bf16[32,128,256]{1,2,0:T(8,128)(2,1)S(1)} all-to-all(bf16[32,128,256]{1,2,0:T(8,128)(2,1)S(1)} %copy.25), channel_id=1, replica_groups=mesh['space'=16,'seq'=32] {'seq'}, dimensions={0} | all-to-all | bytes 4194304 | tf_op jit(solution)/shard_map/all_to_all | solution.py:219
  392.8 1.0 copy.29
  393.8 1.0 copy.28
  394.9 1.0 copy.27
  395.9 1.0 copy.26
  (30 shorter events, 1.4 us)
Async XLA Ops:
  0.6 2.7 copy-start
  0.6 3.0 copy-start.1
  5.7 15.9 %copy-start.3 = (s32[96,5]{0,1:T(8,128)S(1)}, s32[96,5]{0,1:T(8,128)}, u32[]{:S(2)}) copy-start(s32[96,5]{0,1:T(8,128)} %param.17) | copy-start | bytes 5764
  5.7 17.0 %copy-start.2 = (s32[96,64]{0,1:T(8,128)S(1)}, s32[96,64]{0,1:T(8,128)}, u32[]{:S(2)}) copy-start(s32[96,64]{0,1:T(8,128)} %param.16) | copy-start | bytes 73732
  5.7 116.5 %all-to-all-start = ((bf16[32,128,256]{1,2,0:T(8,128)(2,1)}), bf16[32,128,256]{1,2,0:T(8,128)(2,1)}, u32[]{:S(2)}, u32[]{:S(2)}) async-start(bf16[32,128,256]{1,2,0:T(8,128)(2,1)} %bitcast.15), calls=%async_computation | async-start | bytes 4194304 | tf_op jit(solution)/shard_map/all_to_all | solution.py:187
  151.5 8.2 %collective-permute-start = (bf16[16,64,128]{2,1,0:T(8,128)(2,1)S(1)}, bf16[16,64,128]{2,1,0:T(8,128)(2,1)S(1)}, u32[]{:S(2)}, u32[]{:S(2)}) collective-permute-start(bf16[16,64,128]{2,1,0:T(8,128)(2,1)S(1)} %get-tuple-element.36), channel_id=1, source_target_pairs={{0,32},{32,64},{64,96},{96,128},{128,160},{160,192},{192,224},{224... | collective-permute-start | bytes 786440 | tf_op jit(solution)/shard_map/ppermute | solution.py:22
  156.0 11.3 %collective-permute-start.1 = (bf16[16,64,128]{2,1,0:T(8,128)(2,1)S(1)}, bf16[16,64,128]{2,1,0:T(8,128)(2,1)S(1)}, u32[]{:S(2)}, u32[]{:S(2)}) collective-permute-start(bf16[16,64,128]{2,1,0:T(8,128)(2,1)S(1)} %get-tuple-element.37), channel_id=1, source_target_pairs={{32,0},{64,32},{96,64},{128,96},{160,128},{192,160},{224,192},{256... | collective-permute-start | bytes 786440 | tf_op jit(solution)/shard_map/ppermute | solution.py:23
  235.7 29.5 %collective-permute-start.2 = (bf16[16,64,128]{2,1,0:T(8,128)(2,1)S(1)}, bf16[16,64,128]{2,1,0:T(8,128)(2,1)S(1)}, u32[]{:S(2)}, u32[]{:S(2)}) collective-permute-start(bf16[16,64,128]{2,1,0:T(8,128)(2,1)S(1)} %get-tuple-element.42), channel_id=1, source_target_pairs={{0,32},{32,64},{64,96},{96,128},{128,160},{160,192},{192,224},{224... | collective-permute-start | bytes 786440 | tf_op jit(solution)/shard_map/ppermute | solution.py:22
  237.6 27.6 %collective-permute-start.3 = (bf16[16,64,128]{2,1,0:T(8,128)(2,1)S(1)}, bf16[16,64,128]{2,1,0:T(8,128)(2,1)S(1)}, u32[]{:S(2)}, u32[]{:S(2)}) collective-permute-start(bf16[16,64,128]{2,1,0:T(8,128)(2,1)S(1)} %get-tuple-element.43), channel_id=1, source_target_pairs={{32,0},{64,32},{96,64},{128,96},{160,128},{192,160},{224,192},{256... | collective-permute-start | bytes 786440 | tf_op jit(solution)/shard_map/ppermute | solution.py:23

commit v8 on v7

--- a/solution.py
+++ b/solution.py
@@ -194,6 +194,8 @@
         .set(jnp.arange(windows_n * WIN, dtype=jnp.int32), mode="drop")
     )
 
+    table, slot_of = lax.optimization_barrier((table, slot_of))
+
     def to_voxels(slot_vals):
         return gather_rows(slot_vals.reshape(windows_n * WIN, -1), slot_of)
 

time: 399 us -> 374 us (0.937)
  waiting for transfers between devices: 107 us -> 92.4 us
    all_to_all x1, waiting for transfers between devices: 99.1 us -> 76.1 us  [shards(): lax.all_to_all(stacked, 'seq', split_axis=0, concat_axis=0, tiled=True)]
    ppermute x2, waiting for transfers between devices: 7.68 us -> 15.7 us  [padded(): after = lax.ppermute(first, axis, down)]
  transfers between devices with their start and end apart: 5 -> 5, of which waited for: 2 -> 4; matrix products, arithmetic and copies ran while one was open for 7% -> 7% of each run, Pallas kernels for 0% -> 0%
where the time goes in v8:
time: 374 us
  blocking collectives  98.8 us (26%)
  waiting for transfers between devices  92.4 us (25%)
  local copies, waits for them, and re-layouts  84.8 us (23%)
  Pallas kernels  65.4 us (17%)
  starting transfers between devices  26.7 us (7%)
  other arithmetic  4.72 us (1%)
    all_to_all x1, blocking collectives, shards(): back = lax.all_to_all(vox, 'seq', split_axis=0, concat_axis=0, tiled=True)  98.8 us
    all_to_all x1, waiting for transfers between devices, shards(): lax.all_to_all(stacked, 'seq', split_axis=0, concat_axis=0, tiled=True)  76.1 us
    pallas_call x1, Pallas kernels, window_attention(): pl.pallas_call(attention_kernel, out_shape=(jax.ShapeDtypeStruct((windows...  65.4 us
    gather x2, local copies, waits for them, and re-layouts, gather_rows(): return source.at[indices].get(mode='promise_in_bounds')  42.1 us
    scatter x1, local copies, waits for them, and re-layouts, shards(): slot_of = jnp.zeros((voxel_count,), jnp.int32).at[flat_slots].set(jnp.ara...  23 us
    all_to_all x1, starting transfers between devices, shards(): lax.all_to_all(stacked, 'seq', split_axis=0, concat_axis=0, tiled=True)  15.9 us
    ppermute x2, waiting for transfers between devices, padded(): after = lax.ppermute(first, axis, down)  15.7 us
  transfers between devices with their start and end apart: 5, of which 4 were waited for; matrix products, arithmetic and copies ran while one was open for 7% of the time, Pallas kernels for 0%

profile of v8, /device:TPU:57, one launch (start us, length us, event | category | flops | bytes accessed | tf_op | source)
XLA Modules:
  0.0 373.7 jit_solution(5565403520090654802)
XLA Ops:
  0.7 1.4 copy.17
  2.1 1.3 copy.19
  3.4 0.3 copy.20
  3.7 0.3 copy.18
  3.9 0.3 pad_maximum_fusion.1
  4.2 1.5 copy.21
  5.7 15.9 %all-to-all-start = ((bf16[32,128,256]{1,2,0:T(8,128)(2,1)}), bf16[32,128,256]{1,2,0:T(8,128)(2,1)}, u32[]{:S(2)}, u32[]{:S(2)}) async-start(bf16[32,128,256]{1,2,0:T(8,128)(2,1)} %bitcast.15), calls=%async_computation | async-start | bytes 4194304 | tf_op jit(solution)/shard_map/all_to_all | solution.py:187
  21.9 0.8 constant_dynamic-slice_fusion.2
  23.1 23.0 %scatter_custom_fusion = s32[4096]{0:T(1024)S(1)} fusion(s32[6144]{0:T(1024)S(1)} %bitcast.69, s32[6144]{0:T(1024)S(1)} %iota.12, s32[]{:T(128)} %constant.81.clone.1), kind=kCustom, calls=%fused_computation.20 | custom fusion | bytes 16388 | tf_op jit(solution)/shard_map/scatter | solution.py:194
  46.2 76.1 %all-to-all-done = bf16[32,128,256]{1,2,0:T(8,128)(2,1)} async-done(((bf16[32,128,256]{1,2,0:T(8,128)(2,1)}), bf16[32,128,256]{1,2,0:T(8,128)(2,1)}, u32[]{:S(2)}, u32[]{:S(2)}) %all-to-all-start) | async-done | bytes 2097184 | tf_op jit(solution)/shard_map/all_to_all | solution.py:187
  122.2 3.3 copy.22
  125.5 25.1 %gather_fusion = bf16[6144,256]{1,0:T(8,128)(2,1)} fusion(bf16[4096,256]{1,0:T(8,128)(2,1)S(1)} %bitcast.54, s32[6144]{0:T(1024)S(1)} %broadcast_clamp_fusion), kind=kCustom, calls=%fused_computation | custom fusion | bytes 6316032 | tf_op jit(solution)/shard_map/gather | solution.py:29
  150.6 1.1 fusion.9
  151.7 4.6 %collective-permute-start = (bf16[16,64,128]{2,1,0:T(8,128)(2,1)S(1)}, bf16[16,64,128]{2,1,0:T(8,128)(2,1)S(1)}, u32[]{:S(2)}, u32[]{:S(2)}) collective-permute-start(bf16[16,64,128]{2,1,0:T(8,128)(2,1)S(1)} %get-tuple-element.40), channel_id=1, source_target_pairs={{0,32},{32,64},{64,96},{96,128},{128,160},{160,192},{192,224},{224... | collective-permute-start | bytes 786440 | tf_op jit(solution)/shard_map/ppermute | solution.py:22
  156.2 1.9 collective-permute-start.1
  158.3 1.5 slice.120
  159.9 7.7 %collective-permute-done.1 = bf16[16,64,128]{2,1,0:T(8,128)(2,1)S(1)} collective-permute-done((bf16[16,64,128]{2,1,0:T(8,128)(2,1)S(1)}, bf16[16,64,128]{2,1,0:T(8,128)(2,1)S(1)}, u32[]{:S(2)}, u32[]{:S(2)}) %collective-permute-start.1) | collective-permute-done | bytes 262176 | tf_op jit(solution)/shard_map/ppermute | solution.py:23
  167.8 65.4 %shard_map.102 = (bf16[96,64,128]{2,1,0:T(8,128)(2,1)S(1)}, f32[128,64,128]{2,1,0:T(8,128)}) custom-call(s32[576]{0:T(1024)S(1)} %reshape.159.idx_ref, s32[128]{0:T(128)S(1)} %pad_add_fusion.1.len_ref, bf16[96,64,256]{2,1,0:T(8,128)(2,1)} %bitcast.58, bf16[128,64,128]{2,1,0:T(8,128)(2,1)S(1)} %pad_maximum_fusion.2.kv_ref), custom_call_target="tpu_custom_call" | custom-call | flops 3623878656 | bytes 8388608 | tf_op jit(solution)/shard_map/pallas_call | solution.py:139
  233.2 2.8 convert.6
  236.1 1.9 collective-permute-start.2
  238.0 2.4 collective-permute-start.3
  240.7 0.6 collective-permute-done.2
  241.3 8.0 %collective-permute-done.3 = bf16[16,64,128]{2,1,0:T(8,128)(2,1)S(1)} collective-permute-done((bf16[16,64,128]{2,1,0:T(8,128)(2,1)S(1)}, bf16[16,64,128]{2,1,0:T(8,128)(2,1)S(1)}, u32[]{:S(2)}, u32[]{:S(2)}) %collective-permute-start.3) | collective-permute-done | bytes 262176 | tf_op jit(solution)/shard_map/ppermute | solution.py:23
  249.5 0.3 convert_element_type.8
  249.9 0.6 pad_maximum_fusion
  250.5 17.0 %gather_fusion.1 = bf16[4096,256]{1,0:T(8,128)(2,1)} fusion(bf16[6144,256]{1,0:T(8,128)(2,1)S(1)} %bitcast.55, s32[4096]{0:T(1024)S(1)} %fusion.3), kind=kCustom, calls=%fused_computation.1 | custom fusion | bytes 4210688 | tf_op jit(solution)/shard_map/gather | solution.py:29
  267.5 3.2 copy.25
  270.7 98.8 %all_to_all.10 = bf16[32,128,256]{1,2,0:T(8,128)(2,1)S(1)} all-to-all(bf16[32,128,256]{1,2,0:T(8,128)(2,1)S(1)} %copy.25), channel_id=1, replica_groups=mesh['space'=16,'seq'=32] {'seq'}, dimensions={0} | all-to-all | bytes 4194304 | tf_op jit(solution)/shard_map/all_to_all | solution.py:221
  369.7 1.0 copy.29
  370.7 1.0 copy.28
  371.7 1.0 copy.27
  372.7 1.0 copy.26
  (32 shorter events, 1.7 us)
Async XLA Ops:
  0.6 2.7 copy-start.1
  0.6 3.0 copy-start.2
  5.7 15.9 %copy-start.4 = (s32[96,5]{0,1:T(8,128)S(1)}, s32[96,5]{0,1:T(8,128)}, u32[]{:S(2)}) copy-start(s32[96,5]{0,1:T(8,128)} %param.17) | copy-start | bytes 5764
  5.7 17.0 %copy-start.3 = (s32[96,64]{0,1:T(8,128)S(1)}, s32[96,64]{0,1:T(8,128)}, u32[]{:S(2)}) copy-start(s32[96,64]{0,1:T(8,128)} %param.16) | copy-start | bytes 73732
  5.7 116.5 %all-to-all-start = ((bf16[32,128,256]{1,2,0:T(8,128)(2,1)}), bf16[32,128,256]{1,2,0:T(8,128)(2,1)}, u32[]{:S(2)}, u32[]{:S(2)}) async-start(bf16[32,128,256]{1,2,0:T(8,128)(2,1)} %bitcast.15), calls=%async_computation | async-start | bytes 4194304 | tf_op jit(solution)/shard_map/all_to_all | solution.py:187
  151.7 8.2 %collective-permute-start = (bf16[16,64,128]{2,1,0:T(8,128)(2,1)S(1)}, bf16[16,64,128]{2,1,0:T(8,128)(2,1)S(1)}, u32[]{:S(2)}, u32[]{:S(2)}) collective-permute-start(bf16[16,64,128]{2,1,0:T(8,128)(2,1)S(1)} %get-tuple-element.40), channel_id=1, source_target_pairs={{0,32},{32,64},{64,96},{96,128},{128,160},{160,192},{192,224},{224... | collective-permute-start | bytes 786440 | tf_op jit(solution)/shard_map/ppermute | solution.py:22
  156.2 11.3 %collective-permute-start.1 = (bf16[16,64,128]{2,1,0:T(8,128)(2,1)S(1)}, bf16[16,64,128]{2,1,0:T(8,128)(2,1)S(1)}, u32[]{:S(2)}, u32[]{:S(2)}) collective-permute-start(bf16[16,64,128]{2,1,0:T(8,128)(2,1)S(1)} %get-tuple-element.41), channel_id=1, source_target_pairs={{32,0},{64,32},{96,64},{128,96},{160,128},{192,160},{224,192},{256... | collective-permute-start | bytes 786440 | tf_op jit(solution)/shard_map/ppermute | solution.py:23
  233.2 7.3 %copy-start = (f32[128,64,128]{2,1,0:T(8,128)S(1)}, f32[128,64,128]{2,1,0:T(8,128)}, u32[]{:S(2)}) copy-start(f32[128,64,128]{2,1,0:T(8,128)} %get-tuple-element.34) | copy-start | bytes 12582916
  236.1 5.2 %collective-permute-start.2 = (bf16[16,64,128]{2,1,0:T(8,128)(2,1)S(1)}, bf16[16,64,128]{2,1,0:T(8,128)(2,1)S(1)}, u32[]{:S(2)}, u32[]{:S(2)}) collective-permute-start(bf16[16,64,128]{2,1,0:T(8,128)(2,1)S(1)} %get-tuple-element.46), channel_id=1, source_target_pairs={{0,32},{32,64},{64,96},{96,128},{128,160},{160,192},{192,224},{224... | collective-permute-start | bytes 786440 | tf_op jit(solution)/shard_map/ppermute | solution.py:22
  238.0 11.3 %collective-permute-start.3 = (bf16[16,64,128]{2,1,0:T(8,128)(2,1)S(1)}, bf16[16,64,128]{2,1,0:T(8,128)(2,1)S(1)}, u32[]{:S(2)}, u32[]{:S(2)}) collective-permute-start(bf16[16,64,128]{2,1,0:T(8,128)(2,1)S(1)} %get-tuple-element.47), channel_id=1, source_target_pairs={{32,0},{64,32},{96,64},{128,96},{160,128},{192,160},{224,192},{256... | collective-permute-start | bytes 786440 | tf_op jit(solution)/shard_map/ppermute | solution.py:23

commit v9 on v8

--- a/solution.py
+++ b/solution.py
@@ -74,7 +74,7 @@
     return (attn_probs, query_heads, key_heads, value_heads, score_scale)
 
 
-def attention_kernel(idx_ref, len_ref, win_ref, kv_ref, out_ref, dkv_ref):
+def attention_kernel(idx_ref, len_ref, win_ref, kv_ref, out_ref, dkv_ref, rim_ref):
     windows_n = win_ref.shape[0]
     lanes = kv_ref.shape[-1]
     width = lanes // 2
@@ -126,6 +126,10 @@
         return carry
 
     lax.fori_loop(0, windows_n, body, 0, unroll=8)
+    ext_n = dkv_ref.shape[0]
+    border = rim_ref.shape[0] // 2
+    rim_ref[:border] = dkv_ref[:border].astype(rim_ref.dtype)
+    rim_ref[border:] = dkv_ref[ext_n - border :].astype(rim_ref.dtype)
 
 
 def window_attention(key_index, length_ext, win_all, kv_ext):
@@ -141,9 +145,10 @@
         out_shape=(
             jax.ShapeDtypeStruct((windows_n, WIN, lanes), jnp.bfloat16),
             jax.ShapeDtypeStruct((ext_n, WIN, lanes), jnp.float32),
+            jax.ShapeDtypeStruct((ext_n - windows_n, WIN, lanes), jnp.bfloat16),
         ),
         in_specs=[smem, smem, vmem, vmem],
-        out_specs=(vmem, vmem),
+        out_specs=(vmem, vmem, vmem),
         compiler_params=pltpu.CompilerParams(vmem_limit_bytes=48 * 1024 * 1024),
         cost_estimate=pl.CostEstimate(
             flops=flops, transcendentals=windows_n * WIN * keys, bytes_accessed=8 * 1024 * 1024
@@ -207,10 +212,8 @@
     key_index = jnp.concatenate(
         [border + jnp.arange(windows_n, dtype=jnp.int32)[:, None], neighbours], axis=1
     ).reshape(-1)
-    dq_out, grad_ext = window_attention(key_index, length_ext, win_all, kv_ext)
-    received_grads = padded(
-        border_rows(grad_ext, border).astype(jnp.bfloat16), (("space", 0),), border
-    ).astype(jnp.float32)
+    dq_out, grad_ext, rim_grads = window_attention(key_index, length_ext, win_all, kv_ext)
+    received_grads = padded(rim_grads, (("space", 0),), border).astype(jnp.float32)
     own_grads = grad_ext[border : border + windows_n]
     own_grads = own_grads.at[:border].add(received_grads[:border])
     own_grads = own_grads.at[windows_n - border :].add(received_grads[3 * border :])

time: 374 us -> 372 us (level)
  transfers between devices with their start and end apart: 5 -> 5, of which waited for: 4 -> 3; matrix products, arithmetic and copies ran while one was open for 7% -> 8% of each run, Pallas kernels for 0% -> 0%
where the time goes in v9:
time: 372 us
  blocking collectives  98.7 us (27%)
  waiting for transfers between devices  90.5 us (24%)
  local copies, waits for them, and re-layouts  86.4 us (23%)
  Pallas kernels  65.4 us (18%)
  starting transfers between devices  26.7 us (7%)
    all_to_all x1, blocking collectives, shards(): back = lax.all_to_all(vox, 'seq', split_axis=0, concat_axis=0, tiled=True)  98.7 us
    all_to_all x1, waiting for transfers between devices, shards(): lax.all_to_all(stacked, 'seq', split_axis=0, concat_axis=0, tiled=True)  76.1 us
    pallas_call x1, Pallas kernels, window_attention(): pl.pallas_call(attention_kernel, out_shape=(jax.ShapeDtypeStruct((windows...  65.4 us
    gather x2, local copies, waits for them, and re-layouts, gather_rows(): return source.at[indices].get(mode='promise_in_bounds')  41.8 us
    scatter x1, local copies, waits for them, and re-layouts, shards(): slot_of = jnp.zeros((voxel_count,), jnp.int32).at[flat_slots].set(jnp.ara...  23 us
    all_to_all x1, starting transfers between devices, shards(): lax.all_to_all(stacked, 'seq', split_axis=0, concat_axis=0, tiled=True)  15.9 us
    ppermute x2, waiting for transfers between devices, padded(): after = lax.ppermute(first, axis, down)  14.4 us
  transfers between devices with their start and end apart: 5, of which 3 were waited for; matrix products, arithmetic and copies ran while one was open for 8% of the time, Pallas kernels for 0%

profile of v9, /device:TPU:57, one launch (start us, length us, event | category | flops | bytes accessed | tf_op | source)
XLA Modules:
  0.0 371.6 jit_solution(8327593850200955142)
XLA Ops:
  0.7 1.4 copy.17
  2.1 1.3 copy.19
  3.4 0.3 copy.20
  3.7 0.3 copy.18
  3.9 0.3 pad_maximum_fusion.1
  4.2 1.5 copy.21
  5.7 15.9 %all-to-all-start = ((bf16[32,128,256]{1,2,0:T(8,128)(2,1)}), bf16[32,128,256]{1,2,0:T(8,128)(2,1)}, u32[]{:S(2)}, u32[]{:S(2)}) async-start(bf16[32,128,256]{1,2,0:T(8,128)(2,1)} %bitcast.15), calls=%async_computation | async-start | bytes 4194304 | tf_op jit(solution)/shard_map/all_to_all | solution.py:192
  21.9 0.8 constant_dynamic-slice_fusion.2
  23.1 23.0 %scatter_custom_fusion = s32[4096]{0:T(1024)S(1)} fusion(s32[6144]{0:T(1024)S(1)} %bitcast.69, s32[6144]{0:T(1024)S(1)} %iota.12, s32[]{:T(128)} %constant.81.clone.1), kind=kCustom, calls=%fused_computation.19 | custom fusion | bytes 16388 | tf_op jit(solution)/shard_map/scatter | solution.py:199
  46.1 76.1 %all-to-all-done = bf16[32,128,256]{1,2,0:T(8,128)(2,1)} async-done(((bf16[32,128,256]{1,2,0:T(8,128)(2,1)}), bf16[32,128,256]{1,2,0:T(8,128)(2,1)}, u32[]{:S(2)}, u32[]{:S(2)}) %all-to-all-start) | async-done | bytes 2097184 | tf_op jit(solution)/shard_map/all_to_all | solution.py:192
  122.2 3.3 copy.22
  125.5 24.9 %gather_fusion = bf16[6144,256]{1,0:T(8,128)(2,1)} fusion(bf16[4096,256]{1,0:T(8,128)(2,1)S(1)} %bitcast.54, s32[6144]{0:T(1024)S(1)} %broadcast_clamp_fusion), kind=kCustom, calls=%fused_computation | custom fusion | bytes 6316032 | tf_op jit(solution)/shard_map/gather | solution.py:29
  150.4 1.1 fusion.9
  151.5 4.6 %collective-permute-start = (bf16[16,64,128]{2,1,0:T(8,128)(2,1)S(1)}, bf16[16,64,128]{2,1,0:T(8,128)(2,1)S(1)}, u32[]{:S(2)}, u32[]{:S(2)}) collective-permute-start(bf16[16,64,128]{2,1,0:T(8,128)(2,1)S(1)} %get-tuple-element.42), channel_id=1, source_target_pairs={{0,32},{32,64},{64,96},{96,128},{128,160},{160,192},{192,224},{224... | collective-permute-start | bytes 786440 | tf_op jit(solution)/shard_map/ppermute | solution.py:22
  156.0 1.9 collective-permute-start.1
  158.1 1.5 slice.116
  159.6 7.7 %collective-permute-done.1 = bf16[16,64,128]{2,1,0:T(8,128)(2,1)S(1)} collective-permute-done((bf16[16,64,128]{2,1,0:T(8,128)(2,1)S(1)}, bf16[16,64,128]{2,1,0:T(8,128)(2,1)S(1)}, u32[]{:S(2)}, u32[]{:S(2)}) %collective-permute-start.1) | collective-permute-done | bytes 262176 | tf_op jit(solution)/shard_map/ppermute | solution.py:23
  167.6 65.4 %shard_map.102 = (bf16[96,64,128]{2,1,0:T(8,128)(2,1)S(1)}, f32[128,64,128]{2,1,0:T(8,128)}, bf16[32,64,128]{2,1,0:T(8,128)(2,1)S(1)}) custom-call(s32[576]{0:T(1024)S(1)} %reshape.159.idx_ref, s32[128]{0:T(128)S(1)} %pad_add_fusion.1.len_ref, bf16[96,64,256]{2,1,0:T(8,128)(2,1)} %bitcast.58, bf16[128,64,128]{2,1,0:T(8,128)(2,1)S(1)} %pad_maximum_fusion.2.kv_ref), custom_call_target="tpu_custom_call" | custom-call | flops 3623878656 | bytes 8388608 | tf_op jit(solution)/shard_map/pallas_call | solution.py:143
  233.0 1.9 collective-permute-start.2
  234.9 2.4 collective-permute-start.3
  237.4 2.1 slice.100
  239.5 6.7 %collective-permute-done.3 = bf16[16,64,128]{2,1,0:T(8,128)(2,1)S(1)} collective-permute-done((bf16[16,64,128]{2,1,0:T(8,128)(2,1)S(1)}, bf16[16,64,128]{2,1,0:T(8,128)(2,1)S(1)}, u32[]{:S(2)}, u32[]{:S(2)}) %collective-permute-start.3) | collective-permute-done | bytes 262176 | tf_op jit(solution)/shard_map/ppermute | solution.py:23
  246.2 1.1 fusion.1
  247.5 0.3 convert_element_type.7
  247.8 0.6 pad_maximum_fusion
  248.4 16.9 %gather_fusion.1 = bf16[4096,256]{1,0:T(8,128)(2,1)} fusion(bf16[6144,256]{1,0:T(8,128)(2,1)S(1)} %bitcast.55, s32[4096]{0:T(1024)S(1)} %fusion.3), kind=kCustom, calls=%fused_computation.1 | custom fusion | bytes 4210688 | tf_op jit(solution)/shard_map/gather | solution.py:29
  265.4 3.2 copy.25
  268.6 98.7 %all_to_all.10 = bf16[32,128,256]{1,2,0:T(8,128)(2,1)S(1)} all-to-all(bf16[32,128,256]{1,2,0:T(8,128)(2,1)S(1)} %copy.25), channel_id=1, replica_groups=mesh['space'=16,'seq'=32] {'seq'}, dimensions={0} | all-to-all | bytes 4194304 | tf_op jit(solution)/shard_map/all_to_all | solution.py:224
  367.5 1.0 copy.29
  368.6 1.0 copy.28
  369.6 1.0 copy.27
  370.6 1.0 copy.26
  (29 shorter events, 1.4 us)
Async XLA Ops:
  0.6 2.7 copy-start
  0.6 3.0 copy-start.1
  5.7 15.9 %copy-start.3 = (s32[96,5]{0,1:T(8,128)S(1)}, s32[96,5]{0,1:T(8,128)}, u32[]{:S(2)}) copy-start(s32[96,5]{0,1:T(8,128)} %param.17) | copy-start | bytes 5764
  5.7 17.0 %copy-start.2 = (s32[96,64]{0,1:T(8,128)S(1)}, s32[96,64]{0,1:T(8,128)}, u32[]{:S(2)}) copy-start(s32[96,64]{0,1:T(8,128)} %param.16) | copy-start | bytes 73732
  5.7 116.5 %all-to-all-start = ((bf16[32,128,256]{1,2,0:T(8,128)(2,1)}), bf16[32,128,256]{1,2,0:T(8,128)(2,1)}, u32[]{:S(2)}, u32[]{:S(2)}) async-start(bf16[32,128,256]{1,2,0:T(8,128)(2,1)} %bitcast.15), calls=%async_computation | async-start | bytes 4194304 | tf_op jit(solution)/shard_map/all_to_all | solution.py:192
  151.5 8.2 %collective-permute-start = (bf16[16,64,128]{2,1,0:T(8,128)(2,1)S(1)}, bf16[16,64,128]{2,1,0:T(8,128)(2,1)S(1)}, u32[]{:S(2)}, u32[]{:S(2)}) collective-permute-start(bf16[16,64,128]{2,1,0:T(8,128)(2,1)S(1)} %get-tuple-element.42), channel_id=1, source_target_pairs={{0,32},{32,64},{64,96},{96,128},{128,160},{160,192},{192,224},{224... | collective-permute-start | bytes 786440 | tf_op jit(solution)/shard_map/ppermute | solution.py:22
  156.0 11.3 %collective-permute-start.1 = (bf16[16,64,128]{2,1,0:T(8,128)(2,1)S(1)}, bf16[16,64,128]{2,1,0:T(8,128)(2,1)S(1)}, u32[]{:S(2)}, u32[]{:S(2)}) collective-permute-start(bf16[16,64,128]{2,1,0:T(8,128)(2,1)S(1)} %get-tuple-element.43), channel_id=1, source_target_pairs={{32,0},{64,32},{96,64},{128,96},{160,128},{192,160},{224,192},{256... | collective-permute-start | bytes 786440 | tf_op jit(solution)/shard_map/ppermute | solution.py:23
  233.0 6.5 %collective-permute-start.2 = (bf16[16,64,128]{2,1,0:T(8,128)(2,1)S(1)}, bf16[16,64,128]{2,1,0:T(8,128)(2,1)S(1)}, u32[]{:S(2)}, u32[]{:S(2)}) collective-permute-start(bf16[16,64,128]{2,1,0:T(8,128)(2,1)S(1)} %get-tuple-element.48), channel_id=1, source_target_pairs={{0,32},{32,64},{64,96},{96,128},{128,160},{160,192},{192,224},{224... | collective-permute-start | bytes 786440 | tf_op jit(solution)/shard_map/ppermute | solution.py:22
  234.9 11.3 %collective-permute-start.3 = (bf16[16,64,128]{2,1,0:T(8,128)(2,1)S(1)}, bf16[16,64,128]{2,1,0:T(8,128)(2,1)S(1)}, u32[]{:S(2)}, u32[]{:S(2)}) collective-permute-start(bf16[16,64,128]{2,1,0:T(8,128)(2,1)S(1)} %get-tuple-element.49), channel_id=1, source_target_pairs={{32,0},{64,32},{96,64},{128,96},{160,128},{192,160},{224,192},{256... | collective-permute-start | bytes 786440 | tf_op jit(solution)/shard_map/ppermute | solution.py:23

commit v10 on v9

--- a/solution.py
+++ b/solution.py
@@ -125,7 +125,7 @@
             dkv_ref[ids[j]] += grad_kv[j * WIN : (j + 1) * WIN]
         return carry
 
-    lax.fori_loop(0, windows_n, body, 0, unroll=8)
+    lax.fori_loop(0, windows_n, body, 0, unroll=16)
     ext_n = dkv_ref.shape[0]
     border = rim_ref.shape[0] // 2
     rim_ref[:border] = dkv_ref[:border].astype(rim_ref.dtype)

time: 372 us -> 371 us (level)
  no operation moved by 1% of the time
where the time goes in v10:
time: 371 us; the launch traced here: 370 us
  blocking collectives  98.8 us (27%)
  waiting for transfers between devices  90.5 us (24%)
  local copies, waits for them, and re-layouts  86.4 us (23%)
  Pallas kernels  64.2 us (17%)
  starting transfers between devices  26.7 us (7%)
    all_to_all x1, blocking collectives, shards(): back = lax.all_to_all(vox, 'seq', split_axis=0, concat_axis=0, tiled=True)  98.8 us
    all_to_all x1, waiting for transfers between devices, shards(): lax.all_to_all(stacked, 'seq', split_axis=0, concat_axis=0, tiled=True)  76.1 us
    pallas_call x1, Pallas kernels, window_attention(): pl.pallas_call(attention_kernel, out_shape=(jax.ShapeDtypeStruct((windows...  64.2 us
    gather x2, local copies, waits for them, and re-layouts, gather_rows(): return source.at[indices].get(mode='promise_in_bounds')  41.8 us
    scatter x1, local copies, waits for them, and re-layouts, shards(): slot_of = jnp.zeros((voxel_count,), jnp.int32).at[flat_slots].set(jnp.ara...  23 us
    all_to_all x1, starting transfers between devices, shards(): lax.all_to_all(stacked, 'seq', split_axis=0, concat_axis=0, tiled=True)  15.9 us
    ppermute x2, waiting for transfers between devices, padded(): after = lax.ppermute(first, axis, down)  14.4 us
  transfers between devices with their start and end apart: 5, of which 3 were waited for; matrix products, arithmetic and copies ran while one was open for 8% of the time, Pallas kernels for 0%

profile of v10, /device:TPU:57, one launch (start us, length us, event | category | flops | bytes accessed | tf_op | source)
XLA Modules:
  0.0 370.3 jit_solution(2846397051410818901)
XLA Ops:
  0.7 1.4 copy.17
  2.1 1.3 copy.19
  3.4 0.3 copy.20
  3.7 0.3 copy.18
  3.9 0.3 pad_maximum_fusion.1
  4.2 1.5 copy.21
  5.7 15.9 %all-to-all-start = ((bf16[32,128,256]{1,2,0:T(8,128)(2,1)}), bf16[32,128,256]{1,2,0:T(8,128)(2,1)}, u32[]{:S(2)}, u32[]{:S(2)}) async-start(bf16[32,128,256]{1,2,0:T(8,128)(2,1)} %bitcast.15), calls=%async_computation | async-start | bytes 4194304 | tf_op jit(solution)/shard_map/all_to_all | solution.py:192
  21.9 0.8 constant_dynamic-slice_fusion.2
  23.1 23.0 %scatter_custom_fusion = s32[4096]{0:T(1024)S(1)} fusion(s32[6144]{0:T(1024)S(1)} %bitcast.69, s32[6144]{0:T(1024)S(1)} %iota.12, s32[]{:T(128)} %constant.81.clone.1), kind=kCustom, calls=%fused_computation.19 | custom fusion | bytes 16388 | tf_op jit(solution)/shard_map/scatter | solution.py:199
  46.1 76.1 %all-to-all-done = bf16[32,128,256]{1,2,0:T(8,128)(2,1)} async-done(((bf16[32,128,256]{1,2,0:T(8,128)(2,1)}), bf16[32,128,256]{1,2,0:T(8,128)(2,1)}, u32[]{:S(2)}, u32[]{:S(2)}) %all-to-all-start) | async-done | bytes 2097184 | tf_op jit(solution)/shard_map/all_to_all | solution.py:192
  122.2 3.3 copy.22
  125.5 24.9 %gather_fusion = bf16[6144,256]{1,0:T(8,128)(2,1)} fusion(bf16[4096,256]{1,0:T(8,128)(2,1)S(1)} %bitcast.54, s32[6144]{0:T(1024)S(1)} %broadcast_clamp_fusion), kind=kCustom, calls=%fused_computation | custom fusion | bytes 6316032 | tf_op jit(solution)/shard_map/gather | solution.py:29
  150.4 1.1 fusion.9
  151.5 4.6 %collective-permute-start = (bf16[16,64,128]{2,1,0:T(8,128)(2,1)S(1)}, bf16[16,64,128]{2,1,0:T(8,128)(2,1)S(1)}, u32[]{:S(2)}, u32[]{:S(2)}) collective-permute-start(bf16[16,64,128]{2,1,0:T(8,128)(2,1)S(1)} %get-tuple-element.42), channel_id=1, source_target_pairs={{0,32},{32,64},{64,96},{96,128},{128,160},{160,192},{192,224},{224... | collective-permute-start | bytes 786440 | tf_op jit(solution)/shard_map/ppermute | solution.py:22
  156.0 1.9 collective-permute-start.1
  158.1 1.5 slice.116
  159.6 7.7 %collective-permute-done.1 = bf16[16,64,128]{2,1,0:T(8,128)(2,1)S(1)} collective-permute-done((bf16[16,64,128]{2,1,0:T(8,128)(2,1)S(1)}, bf16[16,64,128]{2,1,0:T(8,128)(2,1)S(1)}, u32[]{:S(2)}, u32[]{:S(2)}) %collective-permute-start.1) | collective-permute-done | bytes 262176 | tf_op jit(solution)/shard_map/ppermute | solution.py:23
  167.6 64.2 %shard_map.102 = (bf16[96,64,128]{2,1,0:T(8,128)(2,1)S(1)}, f32[128,64,128]{2,1,0:T(8,128)}, bf16[32,64,128]{2,1,0:T(8,128)(2,1)S(1)}) custom-call(s32[576]{0:T(1024)S(1)} %reshape.159.idx_ref, s32[128]{0:T(128)S(1)} %pad_add_fusion.1.len_ref, bf16[96,64,256]{2,1,0:T(8,128)(2,1)} %bitcast.58, bf16[128,64,128]{2,1,0:T(8,128)(2,1)S(1)} %pad_maximum_fusion.2.kv_ref), custom_call_target="tpu_custom_call" | custom-call | flops 3623878656 | bytes 8388608 | tf_op jit(solution)/shard_map/pallas_call | solution.py:143
  231.8 1.9 collective-permute-start.2
  233.7 2.4 collective-permute-start.3
  236.1 2.1 slice.100
  238.3 6.7 %collective-permute-done.3 = bf16[16,64,128]{2,1,0:T(8,128)(2,1)S(1)} collective-permute-done((bf16[16,64,128]{2,1,0:T(8,128)(2,1)S(1)}, bf16[16,64,128]{2,1,0:T(8,128)(2,1)S(1)}, u32[]{:S(2)}, u32[]{:S(2)}) %collective-permute-start.3) | collective-permute-done | bytes 262176 | tf_op jit(solution)/shard_map/ppermute | solution.py:23
  245.0 1.1 fusion.1
  246.3 0.3 convert_element_type.7
  246.6 0.6 pad_maximum_fusion
  247.2 16.9 %gather_fusion.1 = bf16[4096,256]{1,0:T(8,128)(2,1)} fusion(bf16[6144,256]{1,0:T(8,128)(2,1)S(1)} %bitcast.55, s32[4096]{0:T(1024)S(1)} %fusion.3), kind=kCustom, calls=%fused_computation.1 | custom fusion | bytes 4210688 | tf_op jit(solution)/shard_map/gather | solution.py:29
  264.1 3.2 copy.25
  267.4 98.8 %all_to_all.10 = bf16[32,128,256]{1,2,0:T(8,128)(2,1)S(1)} all-to-all(bf16[32,128,256]{1,2,0:T(8,128)(2,1)S(1)} %copy.25), channel_id=1, replica_groups=mesh['space'=16,'seq'=32] {'seq'}, dimensions={0} | all-to-all | bytes 4194304 | tf_op jit(solution)/shard_map/all_to_all | solution.py:224
  366.3 1.0 copy.29
  367.3 1.0 copy.28
  368.3 1.0 copy.27
  369.3 1.0 copy.26
  (29 shorter events, 1.4 us)
Async XLA Ops:
  0.6 2.7 copy-start
  0.6 3.0 copy-start.1
  5.7 15.9 %copy-start.3 = (s32[96,5]{0,1:T(8,128)S(1)}, s32[96,5]{0,1:T(8,128)}, u32[]{:S(2)}) copy-start(s32[96,5]{0,1:T(8,128)} %param.17) | copy-start | bytes 5764
  5.7 17.0 %copy-start.2 = (s32[96,64]{0,1:T(8,128)S(1)}, s32[96,64]{0,1:T(8,128)}, u32[]{:S(2)}) copy-start(s32[96,64]{0,1:T(8,128)} %param.16) | copy-start | bytes 73732
  5.7 116.5 %all-to-all-start = ((bf16[32,128,256]{1,2,0:T(8,128)(2,1)}), bf16[32,128,256]{1,2,0:T(8,128)(2,1)}, u32[]{:S(2)}, u32[]{:S(2)}) async-start(bf16[32,128,256]{1,2,0:T(8,128)(2,1)} %bitcast.15), calls=%async_computation | async-start | bytes 4194304 | tf_op jit(solution)/shard_map/all_to_all | solution.py:192
  151.5 8.2 %collective-permute-start = (bf16[16,64,128]{2,1,0:T(8,128)(2,1)S(1)}, bf16[16,64,128]{2,1,0:T(8,128)(2,1)S(1)}, u32[]{:S(2)}, u32[]{:S(2)}) collective-permute-start(bf16[16,64,128]{2,1,0:T(8,128)(2,1)S(1)} %get-tuple-element.42), channel_id=1, source_target_pairs={{0,32},{32,64},{64,96},{96,128},{128,160},{160,192},{192,224},{224... | collective-permute-start | bytes 786440 | tf_op jit(solution)/shard_map/ppermute | solution.py:22
  156.0 11.3 %collective-permute-start.1 = (bf16[16,64,128]{2,1,0:T(8,128)(2,1)S(1)}, bf16[16,64,128]{2,1,0:T(8,128)(2,1)S(1)}, u32[]{:S(2)}, u32[]{:S(2)}) collective-permute-start(bf16[16,64,128]{2,1,0:T(8,128)(2,1)S(1)} %get-tuple-element.43), channel_id=1, source_target_pairs={{32,0},{64,32},{96,64},{128,96},{160,128},{192,160},{224,192},{256... | collective-permute-start | bytes 786440 | tf_op jit(solution)/shard_map/ppermute | solution.py:23
  231.8 6.5 %collective-permute-start.2 = (bf16[16,64,128]{2,1,0:T(8,128)(2,1)S(1)}, bf16[16,64,128]{2,1,0:T(8,128)(2,1)S(1)}, u32[]{:S(2)}, u32[]{:S(2)}) collective-permute-start(bf16[16,64,128]{2,1,0:T(8,128)(2,1)S(1)} %get-tuple-element.48), channel_id=1, source_target_pairs={{0,32},{32,64},{64,96},{96,128},{128,160},{160,192},{192,224},{224... | collective-permute-start | bytes 786440 | tf_op jit(solution)/shard_map/ppermute | solution.py:22
  233.7 11.3 %collective-permute-start.3 = (bf16[16,64,128]{2,1,0:T(8,128)(2,1)S(1)}, bf16[16,64,128]{2,1,0:T(8,128)(2,1)S(1)}, u32[]{:S(2)}, u32[]{:S(2)}) collective-permute-start(bf16[16,64,128]{2,1,0:T(8,128)(2,1)S(1)} %get-tuple-element.49), channel_id=1, source_target_pairs={{32,0},{64,32},{96,64},{128,96},{160,128},{192,160},{224,192},{256... | collective-permute-start | bytes 786440 | tf_op jit(solution)/shard_map/ppermute | solution.py:23

commit v11 on v10

--- a/solution.py
+++ b/solution.py
@@ -74,7 +74,7 @@
     return (attn_probs, query_heads, key_heads, value_heads, score_scale)
 
 
-def attention_kernel(idx_ref, len_ref, win_ref, kv_ref, out_ref, dkv_ref, rim_ref):
+def attention_kernel(idx_ref, len_ref, win_ref, kv_ref, out_ref, own_rim_ref, rim_ref, dkv_ref):
     windows_n = win_ref.shape[0]
     lanes = kv_ref.shape[-1]
     width = lanes // 2
@@ -118,7 +118,7 @@
         )
         grad_scores = (probs * (grad_probs - delta) * scale).astype(jnp.bfloat16)
         dq_full = jnp.dot(grad_scores, kv_all, preferred_element_type=jnp.float32).astype(jnp.bfloat16)
-        out_ref[w] = jnp.where(first_half, dq_full, out_full)
+        out_ref[w, :, :lanes] = jnp.where(first_half, dq_full, out_full)
         score_blocks = jnp.concatenate([grad_scores, weights], axis=0)
         grad_kv = lax.dot_general(score_blocks, qg_blocks, tn, preferred_element_type=jnp.float32)
         for j in range(nb):
@@ -130,6 +130,9 @@
     border = rim_ref.shape[0] // 2
     rim_ref[:border] = dkv_ref[:border].astype(rim_ref.dtype)
     rim_ref[border:] = dkv_ref[ext_n - border :].astype(rim_ref.dtype)
+    own_rim_ref[:border] = dkv_ref[border : 2 * border]
+    own_rim_ref[border:] = dkv_ref[ext_n - 2 * border : ext_n - border]
+    out_ref[:, :, lanes:] = dkv_ref[border : border + windows_n].astype(out_ref.dtype)
 
 
 def window_attention(key_index, length_ext, win_all, kv_ext):
@@ -143,12 +146,13 @@
     return pl.pallas_call(
         attention_kernel,
         out_shape=(
-            jax.ShapeDtypeStruct((windows_n, WIN, lanes), jnp.bfloat16),
-            jax.ShapeDtypeStruct((ext_n, WIN, lanes), jnp.float32),
+            jax.ShapeDtypeStruct((windows_n, WIN, 2 * lanes), jnp.bfloat16),
+            jax.ShapeDtypeStruct((ext_n - windows_n, WIN, lanes), jnp.float32),
             jax.ShapeDtypeStruct((ext_n - windows_n, WIN, lanes), jnp.bfloat16),
         ),
         in_specs=[smem, smem, vmem, vmem],
         out_specs=(vmem, vmem, vmem),
+        scratch_shapes=[pltpu.VMEM((ext_n, WIN, lanes), jnp.float32)],
         compiler_params=pltpu.CompilerParams(vmem_limit_bytes=48 * 1024 * 1024),
         cost_estimate=pl.CostEstimate(
             flops=flops, transcendentals=windows_n * WIN * keys, bytes_accessed=8 * 1024 * 1024
@@ -212,14 +216,12 @@
     key_index = jnp.concatenate(
         [border + jnp.arange(windows_n, dtype=jnp.int32)[:, None], neighbours], axis=1
     ).reshape(-1)
-    dq_out, grad_ext, rim_grads = window_attention(key_index, length_ext, win_all, kv_ext)
+    slot_vals, own_rim, rim_grads = window_attention(key_index, length_ext, win_all, kv_ext)
     received_grads = padded(rim_grads, (("space", 0),), border).astype(jnp.float32)
-    own_grads = grad_ext[border : border + windows_n]
-    own_grads = own_grads.at[:border].add(received_grads[:border])
-    own_grads = own_grads.at[windows_n - border :].add(received_grads[3 * border :])
-    slot_vals = jnp.concatenate(
-        [dq_out, own_grads.astype(jnp.bfloat16)], axis=-1
-    )
+    low = (own_rim[:border] + received_grads[:border]).astype(jnp.bfloat16)
+    high = (own_rim[border:] + received_grads[3 * border :]).astype(jnp.bfloat16)
+    slot_vals = slot_vals.at[:border, :, 2 * col_width :].set(low)
+    slot_vals = slot_vals.at[windows_n - border :, :, 2 * col_width :].set(high)
     vox = to_voxels(slot_vals).reshape(seq_n, rows, 4 * col_width)
     back = lax.all_to_all(vox, "seq", split_axis=0, concat_axis=0, tiled=True)
     back = back.reshape(seq_n, rows, 4, col_width)

time: 371 us -> 378 us (1.019)
  local copies, waits for them, and re-layouts: 86.4 us -> 90.6 us
    another operation x0 -> x3, other arithmetic: none -> 5.06 us
    scatter x0 -> x1, local copies, waits for them, and re-layouts: none -> 4.24 us  [shards(): slot_vals = slot_vals.at[:border, :, 2 * col_width:].set(low)]
where the time goes in v11:
time: 378 us
  blocking collectives  98.8 us (26%)
  local copies, waits for them, and re-layouts  90.6 us (24%)
  waiting for transfers between devices  90.1 us (24%)
  Pallas kernels  64.1 us (17%)
  starting transfers between devices  26.7 us (7%)
  other arithmetic  6.59 us (2%)
    all_to_all x1, blocking collectives, shards(): back = lax.all_to_all(vox, 'seq', split_axis=0, concat_axis=0, tiled=True)  98.8 us
    all_to_all x1, waiting for transfers between devices, shards(): lax.all_to_all(stacked, 'seq', split_axis=0, concat_axis=0, tiled=True)  76.3 us
    pallas_call x1, Pallas kernels, window_attention(): pl.pallas_call(attention_kernel, out_shape=(jax.ShapeDtypeStruct((windows...  64.1 us
    gather x2, local copies, waits for them, and re-layouts, gather_rows(): return source.at[indices].get(mode='promise_in_bounds')  43.3 us
    scatter x1, local copies, waits for them, and re-layouts, shards(): slot_of = jnp.zeros((voxel_count,), jnp.int32).at[flat_slots].set(jnp.ara...  23 us
    all_to_all x1, starting transfers between devices, shards(): lax.all_to_all(stacked, 'seq', split_axis=0, concat_axis=0, tiled=True)  15.9 us
    ppermute x2, waiting for transfers between devices, padded(): after = lax.ppermute(first, axis, down)  13.8 us
  transfers between devices with their start and end apart: 5, of which 3 were waited for; matrix products, arithmetic and copies ran while one was open for 8% of the time, Pallas kernels for 0%

profile of v11, /device:TPU:57, one launch (start us, length us, event | category | flops | bytes accessed | tf_op | source)
XLA Modules:
  0.0 377.7 jit_solution(9786369942932162648)
XLA Ops:
  0.7 1.4 copy.19
  2.1 1.3 copy.20
  3.4 0.3 copy.17
  3.7 0.3 copy.18
  4.2 1.5 copy.21
  5.7 15.9 %all-to-all-start = ((bf16[32,128,256]{1,2,0:T(8,128)(2,1)}), bf16[32,128,256]{1,2,0:T(8,128)(2,1)}, u32[]{:S(2)}, u32[]{:S(2)}) async-start(bf16[32,128,256]{1,2,0:T(8,128)(2,1)} %bitcast.15), calls=%async_computation | async-start | bytes 4194304 | tf_op jit(solution)/shard_map/all_to_all | solution.py:196
  21.6 0.8 constant_dynamic-slice_fusion.2
  22.8 23.0 %scatter_custom_fusion = s32[4096]{0:T(1024)S(1)} fusion(s32[6144]{0:T(1024)S(1)} %bitcast.70, s32[6144]{0:T(1024)S(1)} %iota.19, s32[]{:T(128)} %constant.82.clone.1), kind=kCustom, calls=%fused_computation.19 | custom fusion | bytes 16388 | tf_op jit(solution)/shard_map/scatter | solution.py:203
  46.0 76.3 %all-to-all-done = bf16[32,128,256]{1,2,0:T(8,128)(2,1)} async-done(((bf16[32,128,256]{1,2,0:T(8,128)(2,1)}), bf16[32,128,256]{1,2,0:T(8,128)(2,1)}, u32[]{:S(2)}, u32[]{:S(2)}) %all-to-all-start) | async-done | bytes 2097184 | tf_op jit(solution)/shard_map/all_to_all | solution.py:196
  122.2 3.3 copy.22
  125.5 25.1 %gather_fusion = bf16[6144,256]{1,0:T(8,128)(2,1)} fusion(bf16[4096,256]{1,0:T(8,128)(2,1)S(1)} %bitcast.55, s32[6144]{0:T(1024)S(1)} %broadcast_clamp_fusion), kind=kCustom, calls=%fused_computation | custom fusion | bytes 6316032 | tf_op jit(solution)/shard_map/gather | solution.py:29
  150.6 1.1 fusion.10
  151.7 4.6 %collective-permute-start = (bf16[16,64,128]{2,1,0:T(8,128)(2,1)S(1)}, bf16[16,64,128]{2,1,0:T(8,128)(2,1)S(1)}, u32[]{:S(2)}, u32[]{:S(2)}) collective-permute-start(bf16[16,64,128]{2,1,0:T(8,128)(2,1)S(1)} %get-tuple-element.42), channel_id=1, source_target_pairs={{0,32},{32,64},{64,96},{96,128},{128,160},{160,192},{192,224},{224... | collective-permute-start | bytes 786440 | tf_op jit(solution)/shard_map/ppermute | solution.py:22
  156.2 1.9 collective-permute-start.1
  158.5 0.6 fusion.13
  159.1 1.5 slice.132
  160.6 6.9 %collective-permute-done.1 = bf16[16,64,128]{2,1,0:T(8,128)(2,1)S(1)} collective-permute-done((bf16[16,64,128]{2,1,0:T(8,128)(2,1)S(1)}, bf16[16,64,128]{2,1,0:T(8,128)(2,1)S(1)}, u32[]{:S(2)}, u32[]{:S(2)}) %collective-permute-start.1) | collective-permute-done | bytes 262176 | tf_op jit(solution)/shard_map/ppermute | solution.py:23
  167.8 64.1 %shard_map.102 = (bf16[96,64,256]{2,1,0:T(8,128)(2,1)}, f32[32,64,128]{2,1,0:T(8,128)S(1)}, bf16[32,64,128]{2,1,0:T(8,128)(2,1)S(1)}) custom-call(s32[576]{0:T(1024)S(1)} %reshape.176.idx_ref, s32[128]{0:T(128)S(1)} %pad_add_fusion.1.len_ref, bf16[96,64,256]{2,1,0:T(8,128)(2,1)} %bitcast.59, bf16[128,64,128]{2,1,0:T(8,128)(2,1)S(1)} %pad_maximum_fusion.1.kv_ref), custom_call_target="tpu_custom_call" | custom-call | flops 3623878656 | bytes 8388608 | tf_op jit(solution)/shard_map/pallas_call | solution.py:146
  231.9 1.9 collective-permute-start.2
  233.8 2.4 collective-permute-start.3
  236.2 2.0 and_reduce_fusion
  238.3 6.9 %collective-permute-done.3 = bf16[16,64,128]{2,1,0:T(8,128)(2,1)S(1)} collective-permute-done((bf16[16,64,128]{2,1,0:T(8,128)(2,1)S(1)}, bf16[16,64,128]{2,1,0:T(8,128)(2,1)S(1)}, u32[]{:S(2)}, u32[]{:S(2)}) %collective-permute-start.3) | collective-permute-done | bytes 262176 | tf_op jit(solution)/shard_map/ppermute | solution.py:23
  245.1 3.1 fusion.2
  248.2 4.2 %scatter.18 = bf16[96,64,256]{2,1,0:T(8,128)(2,1)} dynamic-update-slice(bf16[96,64,256]{2,1,0:T(8,128)(2,1)} %get-tuple-element.34, bf16[16,64,128]{2,1,0:T(8,128)(2,1)S(1)} %fusion.2, s32[]{:T(128)} %bitcast.19, s32[]{:T(128)} %constant.82.clone.1, s32[]{:T(128)} %bitcast.20) | dynamic-update-slice | bytes 524292 | tf_op jit(solution)/shard_map/scatter | solution.py:223
  252.4 0.8 fusion.1
  253.2 18.2 %gather_fusion.1 = bf16[4096,256]{1,0:T(8,128)(2,1)} fusion(bf16[6144,256]{1,0:T(8,128)(2,1)} %bitcast.56, s32[4096]{0:T(1024)S(1)} %fusion.4), kind=kCustom, calls=%fused_computation.1 | custom fusion | bytes 4210688 | tf_op jit(solution)/shard_map/gather | solution.py:29
  271.4 3.2 copy.25
  274.7 98.8 %all_to_all.10 = bf16[32,128,256]{1,2,0:T(8,128)(2,1)S(1)} all-to-all(bf16[32,128,256]{1,2,0:T(8,128)(2,1)S(1)} %copy.25), channel_id=1, replica_groups=mesh['space'=16,'seq'=32] {'seq'}, dimensions={0} | all-to-all | bytes 4194304 | tf_op jit(solution)/shard_map/all_to_all | solution.py:226
  373.6 1.0 copy.26
  374.6 1.0 copy.27
  375.6 1.0 copy.28
  376.6 1.0 copy.29
  (32 shorter events, 1.6 us)
Async XLA Ops:
  0.6 2.7 copy-start
  0.6 3.0 copy-start.1
  5.7 16.7 %copy-start.2 = (s32[96,64]{0,1:T(8,128)S(1)}, s32[96,64]{0,1:T(8,128)}, u32[]{:S(2)}) copy-start(s32[96,64]{0,1:T(8,128)} %param.16) | copy-start | bytes 73732
  5.7 40.1 %copy-start.3 = (s32[96,5]{0,1:T(8,128)S(1)}, s32[96,5]{0,1:T(8,128)}, u32[]{:S(2)}) copy-start(s32[96,5]{0,1:T(8,128)} %param.17) | copy-start | bytes 5764
  5.7 116.5 %all-to-all-start = ((bf16[32,128,256]{1,2,0:T(8,128)(2,1)}), bf16[32,128,256]{1,2,0:T(8,128)(2,1)}, u32[]{:S(2)}, u32[]{:S(2)}) async-start(bf16[32,128,256]{1,2,0:T(8,128)(2,1)} %bitcast.15), calls=%async_computation | async-start | bytes 4194304 | tf_op jit(solution)/shard_map/all_to_all | solution.py:196
  151.7 8.9 %collective-permute-start = (bf16[16,64,128]{2,1,0:T(8,128)(2,1)S(1)}, bf16[16,64,128]{2,1,0:T(8,128)(2,1)S(1)}, u32[]{:S(2)}, u32[]{:S(2)}) collective-permute-start(bf16[16,64,128]{2,1,0:T(8,128)(2,1)S(1)} %get-tuple-element.42), channel_id=1, source_target_pairs={{0,32},{32,64},{64,96},{96,128},{128,160},{160,192},{192,224},{224... | collective-permute-start | bytes 786440 | tf_op jit(solution)/shard_map/ppermute | solution.py:22
  156.2 11.3 %collective-permute-start.1 = (bf16[16,64,128]{2,1,0:T(8,128)(2,1)S(1)}, bf16[16,64,128]{2,1,0:T(8,128)(2,1)S(1)}, u32[]{:S(2)}, u32[]{:S(2)}) collective-permute-start(bf16[16,64,128]{2,1,0:T(8,128)(2,1)S(1)} %get-tuple-element.43), channel_id=1, source_target_pairs={{32,0},{64,32},{96,64},{128,96},{160,128},{192,160},{224,192},{256... | collective-permute-start | bytes 786440 | tf_op jit(solution)/shard_map/ppermute | solution.py:23
  167.8 68.5 %copy-start.4 = (s32[3]{0:T(128)S(1)}, s32[3]{0:T(128)}, u32[]{:S(2)}) copy-start(s32[3]{0:T(128)} %constant.89.clone.1) | copy-start | bytes 40
  231.9 6.4 %collective-permute-start.2 = (bf16[16,64,128]{2,1,0:T(8,128)(2,1)S(1)}, bf16[16,64,128]{2,1,0:T(8,128)(2,1)S(1)}, u32[]{:S(2)}, u32[]{:S(2)}) collective-permute-start(bf16[16,64,128]{2,1,0:T(8,128)(2,1)S(1)} %get-tuple-element.48), channel_id=1, source_target_pairs={{0,32},{32,64},{64,96},{96,128},{128,160},{160,192},{192,224},{224... | collective-permute-start | bytes 786440 | tf_op jit(solution)/shard_map/ppermute | solution.py:22
  233.8 11.3 %collective-permute-start.3 = (bf16[16,64,128]{2,1,0:T(8,128)(2,1)S(1)}, bf16[16,64,128]{2,1,0:T(8,128)(2,1)S(1)}, u32[]{:S(2)}, u32[]{:S(2)}) collective-permute-start(bf16[16,64,128]{2,1,0:T(8,128)(2,1)S(1)} %get-tuple-element.49), channel_id=1, source_target_pairs={{32,0},{64,32},{96,64},{128,96},{160,128},{192,160},{224,192},{256... | collective-permute-start | bytes 786440 | tf_op jit(solution)/shard_map/ppermute | solution.py:23

commit v12 on v10

--- a/solution.py
+++ b/solution.py
@@ -125,7 +125,7 @@
             dkv_ref[ids[j]] += grad_kv[j * WIN : (j + 1) * WIN]
         return carry
 
-    lax.fori_loop(0, windows_n, body, 0, unroll=16)
+    lax.fori_loop(0, windows_n, body, 0, unroll=32)
     ext_n = dkv_ref.shape[0]
     border = rim_ref.shape[0] // 2
     rim_ref[:border] = dkv_ref[:border].astype(rim_ref.dtype)

time: 371 us -> 370 us (level)
  no operation moved by 1% of the time
where the time goes in v12:
time: 370 us
  blocking collectives  98.7 us (27%)
  waiting for transfers between devices  90.3 us (24%)
  local copies, waits for them, and re-layouts  86.4 us (23%)
  Pallas kernels  63.5 us (17%)
  starting transfers between devices  26.9 us (7%)
    all_to_all x1, blocking collectives, shards(): back = lax.all_to_all(vox, 'seq', split_axis=0, concat_axis=0, tiled=True)  98.7 us
    all_to_all x1, waiting for transfers between devices, shards(): lax.all_to_all(stacked, 'seq', split_axis=0, concat_axis=0, tiled=True)  76.1 us
    pallas_call x1, Pallas kernels, window_attention(): pl.pallas_call(attention_kernel, out_shape=(jax.ShapeDtypeStruct((windows...  63.5 us
    gather x2, local copies, waits for them, and re-layouts, gather_rows(): return source.at[indices].get(mode='promise_in_bounds')  41.8 us
    scatter x1, local copies, waits for them, and re-layouts, shards(): slot_of = jnp.zeros((voxel_count,), jnp.int32).at[flat_slots].set(jnp.ara...  23 us
    all_to_all x1, starting transfers between devices, shards(): lax.all_to_all(stacked, 'seq', split_axis=0, concat_axis=0, tiled=True)  15.9 us
    ppermute x2, waiting for transfers between devices, padded(): after = lax.ppermute(first, axis, down)  14.2 us
  transfers between devices with their start and end apart: 5, of which 3 were waited for; matrix products, arithmetic and copies ran while one was open for 8% of the time, Pallas kernels for 0%

profile of v12, /device:TPU:57, one launch (start us, length us, event | category | flops | bytes accessed | tf_op | source)
XLA Modules:
  0.0 369.7 jit_solution(16196719862088166289)
XLA Ops:
  0.7 1.4 copy.17
  2.1 1.3 copy.19
  3.4 0.3 copy.20
  3.7 0.3 copy.18
  3.9 0.3 pad_maximum_fusion.1
  4.2 1.5 copy.21
  5.7 15.9 %all-to-all-start = ((bf16[32,128,256]{1,2,0:T(8,128)(2,1)}), bf16[32,128,256]{1,2,0:T(8,128)(2,1)}, u32[]{:S(2)}, u32[]{:S(2)}) async-start(bf16[32,128,256]{1,2,0:T(8,128)(2,1)} %bitcast.15), calls=%async_computation | async-start | bytes 4194304 | tf_op jit(solution)/shard_map/all_to_all | solution.py:192
  21.9 0.8 constant_dynamic-slice_fusion.2
  23.1 23.0 %scatter_custom_fusion = s32[4096]{0:T(1024)S(1)} fusion(s32[6144]{0:T(1024)S(1)} %bitcast.69, s32[6144]{0:T(1024)S(1)} %iota.12, s32[]{:T(128)} %constant.81.clone.1), kind=kCustom, calls=%fused_computation.19 | custom fusion | bytes 16388 | tf_op jit(solution)/shard_map/scatter | solution.py:199
  46.1 76.1 %all-to-all-done = bf16[32,128,256]{1,2,0:T(8,128)(2,1)} async-done(((bf16[32,128,256]{1,2,0:T(8,128)(2,1)}), bf16[32,128,256]{1,2,0:T(8,128)(2,1)}, u32[]{:S(2)}, u32[]{:S(2)}) %all-to-all-start) | async-done | bytes 2097184 | tf_op jit(solution)/shard_map/all_to_all | solution.py:192
  122.2 3.3 copy.22
  125.5 24.9 %gather_fusion = bf16[6144,256]{1,0:T(8,128)(2,1)} fusion(bf16[4096,256]{1,0:T(8,128)(2,1)S(1)} %bitcast.54, s32[6144]{0:T(1024)S(1)} %broadcast_clamp_fusion), kind=kCustom, calls=%fused_computation | custom fusion | bytes 6316032 | tf_op jit(solution)/shard_map/gather | solution.py:29
  150.4 1.1 fusion.9
  151.5 4.6 %collective-permute-start = (bf16[16,64,128]{2,1,0:T(8,128)(2,1)S(1)}, bf16[16,64,128]{2,1,0:T(8,128)(2,1)S(1)}, u32[]{:S(2)}, u32[]{:S(2)}) collective-permute-start(bf16[16,64,128]{2,1,0:T(8,128)(2,1)S(1)} %get-tuple-element.42), channel_id=1, source_target_pairs={{0,32},{32,64},{64,96},{96,128},{128,160},{160,192},{192,224},{224... | collective-permute-start | bytes 786440 | tf_op jit(solution)/shard_map/ppermute | solution.py:22
  156.0 2.1 collective-permute-start.1
  158.3 1.5 slice.116
  159.8 7.5 %collective-permute-done.1 = bf16[16,64,128]{2,1,0:T(8,128)(2,1)S(1)} collective-permute-done((bf16[16,64,128]{2,1,0:T(8,128)(2,1)S(1)}, bf16[16,64,128]{2,1,0:T(8,128)(2,1)S(1)}, u32[]{:S(2)}, u32[]{:S(2)}) %collective-permute-start.1) | collective-permute-done | bytes 262176 | tf_op jit(solution)/shard_map/ppermute | solution.py:23
  167.6 63.5 %shard_map.102 = (bf16[96,64,128]{2,1,0:T(8,128)(2,1)S(1)}, f32[128,64,128]{2,1,0:T(8,128)}, bf16[32,64,128]{2,1,0:T(8,128)(2,1)S(1)}) custom-call(s32[576]{0:T(1024)S(1)} %reshape.159.idx_ref, s32[128]{0:T(128)S(1)} %pad_add_fusion.1.len_ref, bf16[96,64,256]{2,1,0:T(8,128)(2,1)} %bitcast.58, bf16[128,64,128]{2,1,0:T(8,128)(2,1)S(1)} %pad_maximum_fusion.2.kv_ref), custom_call_target="tpu_custom_call" | custom-call | flops 3623878656 | bytes 8388608 | tf_op jit(solution)/shard_map/pallas_call | solution.py:143
  231.2 1.9 collective-permute-start.2
  233.1 2.4 collective-permute-start.3
  235.5 2.1 slice.100
  237.6 6.7 %collective-permute-done.3 = bf16[16,64,128]{2,1,0:T(8,128)(2,1)S(1)} collective-permute-done((bf16[16,64,128]{2,1,0:T(8,128)(2,1)S(1)}, bf16[16,64,128]{2,1,0:T(8,128)(2,1)S(1)}, u32[]{:S(2)}, u32[]{:S(2)}) %collective-permute-start.3) | collective-permute-done | bytes 262176 | tf_op jit(solution)/shard_map/ppermute | solution.py:23
  244.4 1.1 fusion.1
  245.6 0.3 convert_element_type.7
  246.0 0.6 pad_maximum_fusion
  246.6 16.9 %gather_fusion.1 = bf16[4096,256]{1,0:T(8,128)(2,1)} fusion(bf16[6144,256]{1,0:T(8,128)(2,1)S(1)} %bitcast.55, s32[4096]{0:T(1024)S(1)} %fusion.3), kind=kCustom, calls=%fused_computation.1 | custom fusion | bytes 4210688 | tf_op jit(solution)/shard_map/gather | solution.py:29
  263.5 3.2 copy.25
  266.7 98.7 %all_to_all.10 = bf16[32,128,256]{1,2,0:T(8,128)(2,1)S(1)} all-to-all(bf16[32,128,256]{1,2,0:T(8,128)(2,1)S(1)} %copy.25), channel_id=1, replica_groups=mesh['space'=16,'seq'=32] {'seq'}, dimensions={0} | all-to-all | bytes 4194304 | tf_op jit(solution)/shard_map/all_to_all | solution.py:224
  365.7 1.0 copy.29
  366.7 1.0 copy.28
  367.7 1.0 copy.27
  368.7 1.0 copy.26
  (29 shorter events, 1.4 us)
Async XLA Ops:
  0.6 2.7 copy-start
  0.6 3.0 copy-start.1
  5.7 15.9 %copy-start.3 = (s32[96,5]{0,1:T(8,128)S(1)}, s32[96,5]{0,1:T(8,128)}, u32[]{:S(2)}) copy-start(s32[96,5]{0,1:T(8,128)} %param.17) | copy-start | bytes 5764
  5.7 17.0 %copy-start.2 = (s32[96,64]{0,1:T(8,128)S(1)}, s32[96,64]{0,1:T(8,128)}, u32[]{:S(2)}) copy-start(s32[96,64]{0,1:T(8,128)} %param.16) | copy-start | bytes 73732
  5.7 116.5 %all-to-all-start = ((bf16[32,128,256]{1,2,0:T(8,128)(2,1)}), bf16[32,128,256]{1,2,0:T(8,128)(2,1)}, u32[]{:S(2)}, u32[]{:S(2)}) async-start(bf16[32,128,256]{1,2,0:T(8,128)(2,1)} %bitcast.15), calls=%async_computation | async-start | bytes 4194304 | tf_op jit(solution)/shard_map/all_to_all | solution.py:192
  151.5 8.4 %collective-permute-start = (bf16[16,64,128]{2,1,0:T(8,128)(2,1)S(1)}, bf16[16,64,128]{2,1,0:T(8,128)(2,1)S(1)}, u32[]{:S(2)}, u32[]{:S(2)}) collective-permute-start(bf16[16,64,128]{2,1,0:T(8,128)(2,1)S(1)} %get-tuple-element.42), channel_id=1, source_target_pairs={{0,32},{32,64},{64,96},{96,128},{128,160},{160,192},{192,224},{224... | collective-permute-start | bytes 786440 | tf_op jit(solution)/shard_map/ppermute | solution.py:22
  156.0 11.3 %collective-permute-start.1 = (bf16[16,64,128]{2,1,0:T(8,128)(2,1)S(1)}, bf16[16,64,128]{2,1,0:T(8,128)(2,1)S(1)}, u32[]{:S(2)}, u32[]{:S(2)}) collective-permute-start(bf16[16,64,128]{2,1,0:T(8,128)(2,1)S(1)} %get-tuple-element.43), channel_id=1, source_target_pairs={{32,0},{64,32},{96,64},{128,96},{160,128},{192,160},{224,192},{256... | collective-permute-start | bytes 786440 | tf_op jit(solution)/shard_map/ppermute | solution.py:23
  231.2 6.5 %collective-permute-start.2 = (bf16[16,64,128]{2,1,0:T(8,128)(2,1)S(1)}, bf16[16,64,128]{2,1,0:T(8,128)(2,1)S(1)}, u32[]{:S(2)}, u32[]{:S(2)}) collective-permute-start(bf16[16,64,128]{2,1,0:T(8,128)(2,1)S(1)} %get-tuple-element.48), channel_id=1, source_target_pairs={{0,32},{32,64},{64,96},{96,128},{128,160},{160,192},{192,224},{224... | collective-permute-start | bytes 786440 | tf_op jit(solution)/shard_map/ppermute | solution.py:22
  233.1 11.3 %collective-permute-start.3 = (bf16[16,64,128]{2,1,0:T(8,128)(2,1)S(1)}, bf16[16,64,128]{2,1,0:T(8,128)(2,1)S(1)}, u32[]{:S(2)}, u32[]{:S(2)}) collective-permute-start(bf16[16,64,128]{2,1,0:T(8,128)(2,1)S(1)} %get-tuple-element.49), channel_id=1, source_target_pairs={{32,0},{64,32},{96,64},{128,96},{160,128},{192,160},{224,192},{256... | collective-permute-start | bytes 786440 | tf_op jit(solution)/shard_map/ppermute | solution.py:23
